TPU v7x, 256 devices: a whole 4x4x8 slice. The times are simulated.
256 devices in a mesh: dp: 8 (over y, x_lo), expert: 32 (over x_hi, z, core).
Axes of the slice: x: 4 (x_hi: 2, x_lo: 2; x = x_hi * 2 + x_lo), y: 4, z: 8, core: 2. Of those that a mesh axis runs over, the one named last changes fastest.
Arguments:
- tokens: bfloat16 [32768, 2048], P(('dp', 'expert')), may hold values from -24 to 24
- out_grad: bfloat16 [32768, 2048], P(('dp', 'expert')), may hold values from -6 to 6
- expert_ids: int32 [32768, 8], P(('dp', 'expert')), may hold values from 0 to 63, all different within a row; in each aligned block of 128 rows (0 to 127, 128 to 255, ...) at most 18 rows name the same one
- route_probs: float32 [32768, 8], P(('dp', 'expert')), may hold values from 0.05 to 0.5
- gate_weight: bfloat16 [64, 2048, 384], P('expert'), may hold values from -0.125 to 0.125
- up_weight: bfloat16 [64, 2048, 384], P('expert'), may hold values from -0.125 to 0.125
- down_weight: bfloat16 [64, 384, 2048], P('expert'), may hold values from -0.3125 to 0.3125
Outputs:
- in_grad: bfloat16 [32768, 2048], P(('dp', 'expert'))
- grad_gate: bfloat16 [64, 2048, 384], P('expert', 'dp')
- grad_up: bfloat16 [64, 2048, 384], P('expert', 'dp')
- grad_down: bfloat16 [64, 384, 2048], P('expert', None, 'dp')
Inputs may be any that keep to these rules, and one draw needn't show every extreme that they name: `expert_ids`: within the 128 tokens of one device no expert is named more than 18 times, a bound that some block reaches; a token names 8 different experts.
All inputs are finite; a program needn't handle non-finite values.
Results may differ from a plain program's by a relative error of at most 0.014.
Values may be sent and summed in bfloat16 or wider, within the bound.
No kernel may reach another device: no remote copies, remote signals or barrier semaphores. Data moves between devices by JAX's collectives and lax.ppermute only.
A program may use at most 128 MiB of HBM per device.

v0:
```python
import jax
import jax.numpy as jnp
from jax import lax
from jax.sharding import PartitionSpec as P


def contract(left, right, left_dim, right_dim):
    return lax.dot_general(
        left, right, (((left_dim,), (right_dim,)), ((), ())), preferred_element_type=jnp.float32
    )


def expert_work(xr, scaled, w_gate, w_up, w_down):
    gate = jnp.dot(xr, w_gate, preferred_element_type=jnp.float32)
    up = jnp.dot(xr, w_up, preferred_element_type=jnp.float32)
    sig = jax.nn.sigmoid(gate)
    act = (gate * sig * up).astype(jnp.bfloat16)
    dh = contract(scaled, w_down, 1, 1)
    dgate = (dh * up * sig * (1.0 + gate * (1.0 - sig))).astype(jnp.bfloat16)
    dup = (dh * gate * sig).astype(jnp.bfloat16)
    contrib = (contract(dgate, w_gate, 1, 1) + contract(dup, w_up, 1, 1)).astype(jnp.bfloat16)
    grad_g = contract(xr, dgate, 0, 0).astype(jnp.bfloat16)
    grad_u = contract(xr, dup, 0, 0).astype(jnp.bfloat16)
    grad_d = contract(act, scaled, 0, 0).astype(jnp.bfloat16)
    return (contrib, grad_g, grad_u, grad_d)


def per_device(tokens, out_grad, expert_ids, route_probs, gate_weight, up_weight, down_weight):
    tok_dev, width = tokens.shape
    top_k = expert_ids.shape[1]
    exp_dev = gate_weight.shape[0]
    n_owner = lax.axis_size("expert")
    experts = exp_dev * n_owner
    slots = tok_dev * top_k * 9 // (experts * 8)
    pairs = tok_dev * top_k
    flat = expert_ids.reshape(-1)
    columns = jnp.arange(experts, dtype=jnp.int32)
    onehot = (flat[:, None] == columns[None, :]).astype(jnp.int32)
    rank = jnp.sum(jnp.cumsum(onehot, axis=0) * onehot, axis=1) - 1
    dest = flat * slots + rank
    table = jnp.full((experts * slots,), pairs, dtype=jnp.int32)
    table = table.at[dest].set(jnp.arange(pairs, dtype=jnp.int32))
    tok_index = table // top_k
    zero_row = jnp.zeros((1, width), dtype=jnp.bfloat16)
    x_pad = jnp.concatenate([tokens, zero_row], axis=0)
    dy_pad = jnp.concatenate([out_grad, zero_row], axis=0)
    p_pad = jnp.concatenate([route_probs.reshape(-1), jnp.zeros((1,), dtype=jnp.float32)], axis=0)
    send_x = x_pad[tok_index]
    send_dy = (p_pad[table][:, None] * dy_pad[tok_index].astype(jnp.float32)).astype(jnp.bfloat16)
    send_x = send_x.reshape(n_owner, exp_dev * slots, width)
    send_dy = send_dy.reshape(n_owner, exp_dev * slots, width)
    recv_x, recv_dy = (
        lax.all_to_all(send_x, "expert", split_axis=0, concat_axis=0, tiled=True),
        lax.all_to_all(send_dy, "expert", split_axis=0, concat_axis=0, tiled=True),
    )
    recv_x = recv_x.reshape(n_owner, exp_dev, slots, width)
    recv_dy = recv_dy.reshape(n_owner, exp_dev, slots, width)
    contribs = []
    gates = []
    ups = []
    downs = []
    for local in range(exp_dev):
        xr = recv_x[:, local].reshape(n_owner * slots, width)
        scaled = recv_dy[:, local].reshape(n_owner * slots, width)
        contrib, grad_g, grad_u, grad_d = expert_work(
            xr, scaled, gate_weight[local], up_weight[local], down_weight[local]
        )
        contribs.append(contrib.reshape(n_owner, slots, width))
        gates.append(grad_g)
        ups.append(grad_u)
        downs.append(grad_d)
    back = jnp.stack(contribs, axis=1).reshape(n_owner, exp_dev * slots, width)
    returned = lax.all_to_all(back, "expert", split_axis=0, concat_axis=0, tiled=True)
    returned = returned.reshape(experts * slots, width)
    rows = returned[dest].reshape(tok_dev, top_k, width)
    in_grad = jnp.sum(rows.astype(jnp.float32), axis=1).astype(jnp.bfloat16)
    stack_g = jnp.stack(gates, axis=0)
    stack_u = jnp.stack(ups, axis=0)
    stack_d = jnp.stack(downs, axis=0)
    stack_g, stack_u, stack_d = (
        lax.psum_scatter(stack_g, "dp", scatter_dimension=1, tiled=True).astype(jnp.float32),
        lax.psum_scatter(stack_u, "dp", scatter_dimension=1, tiled=True).astype(jnp.float32),
        lax.psum_scatter(stack_d, "dp", scatter_dimension=2, tiled=True).astype(jnp.float32),
    )
    stack_g = stack_g.astype(jnp.bfloat16)
    stack_u = stack_u.astype(jnp.bfloat16)
    stack_d = stack_d.astype(jnp.bfloat16)
    return (in_grad, stack_g, stack_u, stack_d)


def solution(mesh):
    in_specs = (
        P(("dp", "expert"), None),
        P(("dp", "expert"), None),
        P(("dp", "expert"), None),
        P(("dp", "expert"), None),
        P("expert", None, None),
        P("expert", None, None),
        P("expert", None, None),
    )
    out_specs = (
        P(("dp", "expert"), None),
        P("expert", "dp", None),
        P("expert", "dp", None),
        P("expert", None, "dp"),
    )
    return jax.shard_map(
        per_device, mesh=mesh, in_specs=in_specs, out_specs=out_specs, check_vma=False
    )
```

profile of v0, /device:TPU:1, one launch (start us, length us, event | category | flops | bytes accessed | tf_op | source)
XLA Modules:
  0.0 610.5 jit_solution(16220200354138669468)
XLA Ops:
  8.9 18.0 %reduce-window.6 = s32[64,8,128]{2,1,0:T(8,128)S(1)} reduce-window(s32[64,8,128]{2,1,0:T(8,128)S(1)} %fusion.38, s32[]{:T(128)} %constant.17.clone.1), window={size=1x1x128 pad=0_0x0_0x127_0}, to_apply=%region_0.0 | reduce-window | flops 8323072 | bytes 524292 | tf_op jit(solution)/shard_map/reduce-window
  27.8 4.3 scatter_custom_fusion
  32.2 6.0 gather_fusion.2
  38.2 7.2 %reshape.93 = bf16[32,36,2048]{2,1,0:T(8,128)(2,1)} reshape(bf16[1152,2048]{1,0:T(8,128)(2,1)} %gather_fusion.2) | data formatting | bytes 9437184 | tf_op jit(solution)/shard_map/reshape | solution.py:50
  45.4 12.8 %all-to-all-start.1 = ((bf16[32,36,2048]{2,1,0:T(8,128)(2,1)}), bf16[32,36,2048]{2,1,0:T(8,128)(2,1)}, u32[]{:S(2)}, u32[]{:S(2)}) async-start(bf16[32,36,2048]{2,1,0:T(8,128)(2,1)} %reshape.93), calls=%async_computation.1 | async-start | bytes 10485760 | tf_op jit(solution)/shard_map/all_to_all | solution.py:53
  58.2 6.0 gather_fusion.1
  64.2 7.9 %reshape.98 = f32[32,36,2048]{2,1,0:T(8,128)} reshape(bf16[1152,2048]{1,0:T(8,128)(2,1)} %gather_fusion.1) | data formatting | bytes 14155776 | tf_op jit(solution)/shard_map/convert_element_type | solution.py:49
  72.3 6.5 %gather_fusion = f32[1152]{0:T(1024)S(1)} fusion(f32[1025]{0:T(1024)S(1)} %pad_maximum_fusion.4, s32[2048]{0:T(1024)S(1)} %get-tuple-element.15), kind=kCustom, calls=%fused_computation | custom fusion | bytes 13824 | tf_op jit(solution)/shard_map/gather | solution.py:49
  78.9 6.9 %multiply_convert_fusion = bf16[32,36,2048]{2,1,0:T(8,128)(2,1)} fusion(f32[32,36,2048]{2,1,0:T(8,128)} %reshape.98, f32[32,36]{1,0:T(8,128)S(1)} %mul.82), kind=kLoop, calls=%fused_computation.5 | loop fusion | flops 4718592 | bytes 14160384 | tf_op jit(solution)/shard_map/convert_element_type | solution.py:49
  85.8 90.8 %all-to-all-done.1 = bf16[32,36,2048]{2,1,0:T(8,128)(2,1)} async-done(((bf16[32,36,2048]{2,1,0:T(8,128)(2,1)}), bf16[32,36,2048]{2,1,0:T(8,128)(2,1)}, u32[]{:S(2)}, u32[]{:S(2)}) %all-to-all-start.1) | async-done | bytes 4718624 | tf_op jit(solution)/shard_map/all_to_all | solution.py:53
  176.7 8.0 %all-to-all-start = ((bf16[32,36,2048]{2,1,0:T(8,128)(2,1)}), bf16[32,36,2048]{2,1,0:T(8,128)(2,1)}, u32[]{:S(2)}, u32[]{:S(2)}) async-start(bf16[32,36,2048]{2,1,0:T(8,128)(2,1)} %multiply_convert_fusion), calls=%async_computation | async-start | bytes 10485760 | tf_op jit(solution)/shard_map/all_to_all | solution.py:54
  184.7 5.1 copy.33
  195.5 3.0 copy.36
  200.8 4.6 fusion.17
  212.4 90.8 %all-to-all-done = bf16[32,36,2048]{2,1,0:T(8,128)(2,1)} async-done(((bf16[32,36,2048]{2,1,0:T(8,128)(2,1)}), bf16[32,36,2048]{2,1,0:T(8,128)(2,1)}, u32[]{:S(2)}, u32[]{:S(2)}) %all-to-all-start) | async-done | bytes 4718624 | tf_op jit(solution)/shard_map/all_to_all | solution.py:54
  303.2 5.1 copy.31
  313.9 3.0 copy.35
  319.4 3.8 fusion.4
  326.9 5.1 multiply_convert_fusion.5
  346.3 2.9 add_convert_fusion.1
  349.2 3.1 stack_reshape.6
  352.3 3.1 fusion.6
  355.5 2.9 add_convert_fusion
  358.3 4.3 stack_reshape.7
  365.2 2.6 copy.37
  367.8 5.0 copy.38
  372.8 8.3 %all-to-all-start.2 = ((bf16[32,36,2048]{2,1,0:T(8,128)(2,1)}), bf16[32,36,2048]{2,1,0:T(8,128)(2,1)}, u32[]{:S(2)}, u32[]{:S(2)}) async-start(bf16[32,36,2048]{2,1,0:T(8,128)(2,1)} %copy.38), calls=%async_computation.2 | async-start | bytes 10485760 | tf_op jit(solution)/shard_map/all_to_all | solution.py:73
  386.9 112.7 %all-to-all-done.2 = bf16[32,36,2048]{2,1,0:T(8,128)(2,1)} async-done(((bf16[32,36,2048]{2,1,0:T(8,128)(2,1)}), bf16[32,36,2048]{2,1,0:T(8,128)(2,1)}, u32[]{:S(2)}, u32[]{:S(2)}) %all-to-all-start.2) | async-done | bytes 4718624 | tf_op jit(solution)/shard_map/all_to_all | solution.py:73
  499.6 7.3 %reshape.96 = bf16[1152,2048]{1,0:T(8,128)(2,1)} reshape(bf16[32,36,2048]{2,1,0:T(8,128)(2,1)} %all-to-all-done.2) | data formatting | bytes 9437184 | tf_op jit(solution)/shard_map/reshape | solution.py:74
  506.9 11.8 %gather_fusion.3 = bf16[1024,2048]{1,0:T(8,128)(2,1)} fusion(bf16[1152,2048]{1,0:T(8,128)(2,1)} %reshape.96, s32[1024]{0:T(1024)S(1)} %broadcast_clamp_fusion), kind=kCustom, calls=%fused_computation.3 | custom fusion | bytes 8392704 | tf_op jit(solution)/shard_map/gather | solution.py:75
  518.7 5.9 bitcast_reduce_fusion
  526.5 77.3 %reduce-scatter.4.cloned.1.call-done = bf16[2,256,384]{2,1,0:T(8,128)(2,1)} async-done(((bf16[2,2048,384]{2,1,0:T(8,128)(2,1)}), bf16[2,256,384]{2,1,0:T(8,128)(2,1)}) %reduce-scatter.4.cloned.1.call-update) | async-done | bytes 393232 | tf_op jit(solution)/shard_map/reduce_scatter | solution.py:81
  (108 shorter events, 54.0 us)
Async XLA Ops:
  7.2 25.0 %copy-start.15 = (bf16[128,2048]{1,0:T(8,128)(2,1)S(1)}, bf16[128,2048]{1,0:T(8,128)(2,1)}, u32[]{:S(2)}) copy-start(bf16[128,2048]{1,0:T(8,128)(2,1)} %param.7) | copy-start | bytes 1572868
  45.4 12.8 %copy-start.16 = (bf16[128,2048]{1,0:T(8,128)(2,1)S(1)}, bf16[128,2048]{1,0:T(8,128)(2,1)}, u32[]{:S(2)}) copy-start(bf16[128,2048]{1,0:T(8,128)(2,1)} %param.8) | copy-start | bytes 1572868
  45.4 131.3 %all-to-all-start.1 = ((bf16[32,36,2048]{2,1,0:T(8,128)(2,1)}), bf16[32,36,2048]{2,1,0:T(8,128)(2,1)}, u32[]{:S(2)}, u32[]{:S(2)}) async-start(bf16[32,36,2048]{2,1,0:T(8,128)(2,1)} %reshape.93), calls=%async_computation.1 | async-start | bytes 10485760 | tf_op jit(solution)/shard_map/all_to_all | solution.py:53
  64.2 7.9 %copy-start.21 = (f32[128,8]{0,1:T(8,128)S(1)}, f32[128,8]{0,1:T(8,128)}, u32[]{:S(2)}) copy-start(f32[128,8]{0,1:T(8,128)} %param.10) | copy-start | bytes 12292
  176.7 126.6 %all-to-all-start = ((bf16[32,36,2048]{2,1,0:T(8,128)(2,1)}), bf16[32,36,2048]{2,1,0:T(8,128)(2,1)}, u32[]{:S(2)}, u32[]{:S(2)}) async-start(bf16[32,36,2048]{2,1,0:T(8,128)(2,1)} %multiply_convert_fusion), calls=%async_computation | async-start | bytes 10485760 | tf_op jit(solution)/shard_map/all_to_all | solution.py:54
  184.7 339.9 %reduce-scatter.8.cloned.1.call-start = ((), (), s32[]{:S(2)}) async-start(), calls=%async_computation.8 | async-start | bytes 3538944 | tf_op jit(solution)/shard_map/reduce_scatter | solution.py:83
  200.8 4.6 copy-start.2
  200.8 4.6 copy-start.5
  205.4 2.3 copy-start.8
  207.7 2.4 copy-start
  319.3 3.9 copy-start.11
  319.4 3.9 copy-start.23
  319.4 3.9 copy-start.24
  326.8 5.2 copy-start.6
  326.8 199.6 %reduce-scatter.6.cloned.1.call-start = ((), (), s32[]{:S(2)}) async-start(), calls=%async_computation.7 | async-start | bytes 3538944 | tf_op jit(solution)/shard_map/reduce_scatter | solution.py:82
  332.0 1.8 copy-start.17
  332.0 1.8 copy-start.12
  332.0 2.8 copy-start.22
  332.0 2.9 copy-start.25
  335.0 3.1 copy-start.9
  337.3 0.8 copy-start.19
  341.8 1.9 copy-start.1
  343.7 2.6 copy-start.3
  343.7 2.6 copy-start.18
  352.3 3.1 copy-start.4
  352.3 3.1 copy-start.20
  372.8 8.6 %copy-start.7 = (bf16[576,2048]{1,0:T(8,128)(2,1)S(1)}, bf16[576,2048]{1,0:T(8,128)(2,1)}, u32[]{:S(2)}) copy-start(bf16[576,2048]{1,0:T(8,128)(2,1)} %reshape_squeeze.13) | copy-start | bytes 7077892
  372.8 8.6 %copy-start.13 = (bf16[576,384]{1,0:T(8,128)(2,1)S(1)}, bf16[576,384]{1,0:T(8,128)(2,1)}, u32[]{:S(2)}) copy-start(bf16[576,384]{1,0:T(8,128)(2,1)} %get-tuple-element.9) | copy-start | bytes 1327108
  372.8 126.9 %all-to-all-start.2 = ((bf16[32,36,2048]{2,1,0:T(8,128)(2,1)}), bf16[32,36,2048]{2,1,0:T(8,128)(2,1)}, u32[]{:S(2)}, u32[]{:S(2)}) async-start(bf16[32,36,2048]{2,1,0:T(8,128)(2,1)} %copy.38), calls=%async_computation.2 | async-start | bytes 10485760 | tf_op jit(solution)/shard_map/all_to_all | solution.py:73
  381.1 2.0 copy-start.14
  381.1 222.7 %reduce-scatter.4.cloned.1.call-start = ((), (), s32[]{:S(2)}) async-start(), calls=%async_computation.6 | async-start | bytes 3538944 | tf_op jit(solution)/shard_map/reduce_scatter | solution.py:81
  381.3 1.7 copy-start.10
Sparse Core Ops, SparseCore 0:
  326.9 94.8 reduce-scatter.7
  425.0 101.3 reduce-scatter.5
  529.6 74.1 reduce-scatter.3
where the time goes:
time: 619 us; the launch traced here: 610 us
  waiting for transfers between devices  374 us (60%)
  local copies, waits for them, and re-layouts  110 us (18%)
  matrix products  42.6 us (7%)
  other arithmetic  40.5 us (7%)
  starting transfers between devices  29.4 us (5%)
  between operations  14.4 us (2%)
    all_to_all x1, waiting for transfers between devices, per_device(): lax.all_to_all(back, 'expert', split_axis=0, concat_axis=0, tiled=True)  113 us
    all_to_all x1, waiting for transfers between devices, per_device(): lax.all_to_all(send_x, 'expert', split_axis=0, concat_axis=0, tiled=True)  90.8 us
    all_to_all x1, waiting for transfers between devices, per_device(): lax.all_to_all(send_dy, 'expert', split_axis=0, concat_axis=0, tiled=True)  90.8 us
    reduce_scatter x1, waiting for transfers between devices, per_device(): lax.psum_scatter(stack_g, 'dp', scatter_dimension=1, tiled=True)  77.3 us
    dot_general x12, matrix products, contract(): lax.dot_general(left, right, (((left_dim,), (right_dim,)), ((), ())), pre...  31.1 us
    another operation x3, other arithmetic  18.2 us
    all_to_all x1, starting transfers between devices, per_device(): lax.all_to_all(send_x, 'expert', split_axis=0, concat_axis=0, tiled=True)  12.8 us
  transfers between devices with their start and end apart: 6, of which 5 were waited for; matrix products, arithmetic and copies ran while one was open for 21% of the time, Pallas kernels for 0%

commit v1 on v0

v1 whole, which is shorter than its diff:
```python
import jax
import jax.numpy as jnp
from jax import lax
from jax.sharding import PartitionSpec as P


def contract(left, right, left_dims, right_dims):
    return lax.dot_general(
        left, right, ((left_dims, right_dims), ((), ())), preferred_element_type=jnp.float32
    )


def dp_ring(n_dp):
    half = n_dp // 2
    return [2 * i for i in range(half)] + [2 * (half - 1 - i) + 1 for i in range(half)]


def ring_reduce_scatter(packed, n_dp):
    ring = dp_ring(n_dp)
    pos_of = [ring.index(d) for d in range(n_dp)]
    ring_arr = jnp.array(ring, dtype=jnp.int32)
    pos = jnp.array(pos_of, dtype=jnp.int32)[lax.axis_index("dp")]
    k = packed.shape[1] // 2
    halves = (packed[:, :k], packed[:, k:])
    steps = (1, -1)
    perms = [
        [(ring[i], ring[(i + st) % n_dp]) for i in range(n_dp)] for st in steps
    ]

    def own(h, c):
        return lax.dynamic_index_in_dim(halves[h], ring_arr[c % n_dp], axis=0, keepdims=False)

    send = [own(h, pos - steps[h]) for h in range(2)]
    acc = [None, None]
    for s in range(n_dp - 1):
        for h in range(2):
            recv = lax.ppermute(send[h], "dp", perms[h])
            chunk = pos - steps[h] * (s + 2)
            acc[h] = recv.astype(jnp.float32) + own(h, chunk).astype(jnp.float32)
            send[h] = acc[h].astype(jnp.bfloat16)
    return jnp.concatenate([send[0], send[1]], axis=0)


def expert_work(xr, scaled, w_gate, w_up, w_down):
    gate = contract(xr, w_gate, (1,), (0,))
    up = contract(xr, w_up, (1,), (0,))
    sig = jax.nn.sigmoid(gate)
    act = (gate * sig * up).astype(jnp.bfloat16)
    dh = contract(scaled, w_down, (1,), (1,))
    dgate = (dh * up * sig * (1.0 + gate * (1.0 - sig))).astype(jnp.bfloat16)
    dup = (dh * gate * sig).astype(jnp.bfloat16)
    contrib = (contract(dgate, w_gate, (1,), (1,)) + contract(dup, w_up, (1,), (1,))).astype(
        jnp.bfloat16
    )
    grad_g = contract(xr, dgate, (0,), (0,)).astype(jnp.bfloat16)
    grad_u = contract(xr, dup, (0,), (0,)).astype(jnp.bfloat16)
    grad_d = contract(act, scaled, (0,), (0,)).astype(jnp.bfloat16)
    return contrib, grad_g, grad_u, grad_d


def per_device(tokens, out_grad, expert_ids, route_probs, gate_weight, up_weight, down_weight):
    tok_dev, width = tokens.shape
    top_k = expert_ids.shape[1]
    exp_dev, _, hid = gate_weight.shape
    n_owner = lax.axis_size("expert")
    n_dp = lax.axis_size("dp")
    experts = exp_dev * n_owner
    slots = tok_dev * top_k * 9 // (experts * 8)
    n_slot = experts * slots
    rows = n_owner * slots

    columns = jnp.arange(experts, dtype=jnp.int32)
    onehot = expert_ids[:, :, None] == columns[None, None, :]
    per_tok = jnp.sum(onehot.astype(jnp.float32), axis=1).astype(jnp.bfloat16)
    t_ids = jnp.arange(tok_dev, dtype=jnp.int32)
    lower = (t_ids[None, :] < t_ids[:, None]).astype(jnp.bfloat16)
    before = contract(lower, per_tok, (1,), (0,))
    rank_prev = jnp.sum(jnp.where(onehot, before[:, None, :], 0.0), axis=2).astype(jnp.int32)
    k_ids = jnp.arange(top_k, dtype=jnp.int32)
    same = (expert_ids[:, :, None] == expert_ids[:, None, :]) & (k_ids[None, None, :] < k_ids[None, :, None])
    rank = rank_prev + jnp.sum(same.astype(jnp.int32), axis=2)
    dest = expert_ids * slots + rank

    s_ids = jnp.arange(n_slot, dtype=jnp.int32)
    hit = s_ids[:, None, None] == dest[None, :, :]
    sel = jnp.any(hit, axis=2).astype(jnp.bfloat16)
    p_slot = jnp.sum(jnp.where(hit, route_probs[None, :, :], 0.0), axis=(1, 2))
    sel = sel.reshape(n_owner, exp_dev, slots, tok_dev)
    p_slot = p_slot.reshape(n_owner, exp_dev, slots)

    contrib_back = []
    grads = []
    for local in range(exp_dev):
        sel_l = sel[:, local]
        send_x = contract(sel_l, tokens, (2,), (0,)).astype(jnp.bfloat16)
        dy_rows = contract(sel_l, out_grad, (2,), (0,))
        send_dy = (p_slot[:, local][:, :, None] * dy_rows).astype(jnp.bfloat16)
        send = jnp.concatenate([send_x, send_dy], axis=1)
        recv = lax.all_to_all(send, "expert", split_axis=0, concat_axis=0, tiled=True)
        xr = recv[:, :slots].reshape(rows, width)
        scaled = recv[:, slots:].reshape(rows, width)
        contrib, grad_g, grad_u, grad_d = expert_work(
            xr, scaled, gate_weight[local], up_weight[local], down_weight[local]
        )
        back = lax.all_to_all(
            contrib.reshape(n_owner, slots, width), "expert", split_axis=0, concat_axis=0, tiled=True
        )
        contrib_back.append(back)
        grads.append((grad_g, grad_u, grad_d))

    in_grad = None
    for local in range(exp_dev):
        part = contract(sel[:, local], contrib_back[local], (0, 1), (0, 1))
        in_grad = part if in_grad is None else in_grad + part
    in_grad = in_grad.astype(jnp.bfloat16)

    dsl = width // n_dp
    reduced = []
    for grad_g, grad_u, grad_d in grads:
        packed = jnp.concatenate(
            [
                grad_g.reshape(n_dp, dsl * hid),
                grad_u.reshape(n_dp, dsl * hid),
                grad_d.reshape(hid, n_dp, dsl).transpose(1, 0, 2).reshape(n_dp, hid * dsl),
            ],
            axis=1,
        )
        reduced.append(ring_reduce_scatter(packed, n_dp))
    stack_g = jnp.stack([r[: dsl * hid].reshape(dsl, hid) for r in reduced], axis=0)
    stack_u = jnp.stack([r[dsl * hid : 2 * dsl * hid].reshape(dsl, hid) for r in reduced], axis=0)
    stack_d = jnp.stack([r[2 * dsl * hid :].reshape(hid, dsl) for r in reduced], axis=0)
    return (in_grad, stack_g, stack_u, stack_d)


def solution(mesh):
    in_specs = (
        P(("dp", "expert"), None),
        P(("dp", "expert"), None),
        P(("dp", "expert"), None),
        P(("dp", "expert"), None),
        P("expert", None, None),
        P("expert", None, None),
        P("expert", None, None),
    )
    out_specs = (
        P(("dp", "expert"), None),
        P("expert", "dp", None),
        P("expert", "dp", None),
        P("expert", None, "dp"),
    )
    return jax.shard_map(
        per_device, mesh=mesh, in_specs=in_specs, out_specs=out_specs, check_vma=False
    )
```

time: 619 us -> 712 us (1.15)
  other arithmetic: 40.5 us -> 142 us
  waiting for transfers between devices: 374 us -> 309 us
  starting transfers between devices: 29.4 us -> 73.3 us
  local copies, waits for them, and re-layouts: 110 us -> 73.6 us
  between operations: 14.4 us -> 42.5 us
  matrix products: 42.6 us -> 64.8 us
    reduce_scatter x3 -> x0, waiting for transfers between devices: 79.2 us -> none  [the longest x1 77.3 us: per_device(): lax.psum_scatter(stack_g, 'dp', scatter_dimension=1, tiled=True)]
    ppermute x0 -> x28, waiting for transfers between devices: none -> 70.6 us  [ring_reduce_scatter(): recv = lax.ppermute(send[h], 'dp', perms[h])]
    convert_element_type x2 -> x32, other arithmetic: 6.95 us -> 67.7 us  [the longest x4 61.6 us: ring_reduce_scatter(): acc[h] = recv.astype(jnp.float32) + own(h, chunk).astype(jnp.float32)]
    all_to_all x3 -> x4, waiting for transfers between devices: 294 us -> 239 us  [the longest x2 171 us: per_device(): lax.all_to_all(send, 'expert', split_axis=0, concat_axis=0, tiled=True)]
    dynamic_slice x0 -> x2, other arithmetic: none -> 55.4 us  [own(): lax.dynamic_index_in_dim(halves[h], ring_arr[c % n_dp], axis=0, keepdims=...]
    ppermute x0 -> x28, starting transfers between devices: none -> 32.3 us  [ring_reduce_scatter(): recv = lax.ppermute(send[h], 'dp', perms[h])]
    gather x4 -> x0, local copies, waits for them, and re-layouts: 30.2 us -> none  [the longest x1 11.8 us: per_device(): rows = returned[dest].reshape(tok_dev, top_k, width)]
    another operation x7 -> x2, other arithmetic: 26.8 us -> 1.75 us  [the longest x1 0.96 us: per_device(): jnp.stack([r[:dsl * hid].reshape(dsl, hid) for r in reduced], axis=0)]
  transfers between devices with their start and end apart: 6 -> 32, of which waited for: 5 -> 27; matrix products, arithmetic and copies ran while one was open for 21% -> 7% of each run, Pallas kernels for 0% -> 0%
where the time goes in v1:
time: 712 us; the launch traced here: 706 us
  waiting for transfers between devices  309 us (43%)
  other arithmetic  142 us (20%)
  local copies, waits for them, and re-layouts  73.6 us (10%)
  starting transfers between devices  73.3 us (10%)
  matrix products  64.8 us (9%)
  between operations  42.5 us (6%)
    all_to_all x2, waiting for transfers between devices, per_device(): lax.all_to_all(send, 'expert', split_axis=0, concat_axis=0, tiled=True)  171 us
    ppermute x28, waiting for transfers between devices, ring_reduce_scatter(): recv = lax.ppermute(send[h], 'dp', perms[h])  70.6 us
    all_to_all x2, waiting for transfers between devices, per_device(): lax.all_to_all(contrib.reshape(n_owner, slots, width), 'expert', split_ax...  67.8 us
    dot_general x23, matrix products, contract(): lax.dot_general(left, right, ((left_dims, right_dims), ((), ())), preferr...  64.8 us
    convert_element_type x4, other arithmetic, ring_reduce_scatter(): acc[h] = recv.astype(jnp.float32) + own(h, chunk).astype(jnp.float32)  61.6 us
    dynamic_slice x2, other arithmetic, own(): lax.dynamic_index_in_dim(halves[h], ring_arr[c % n_dp], axis=0, keepdims=...  55.4 us
    ppermute x28, starting transfers between devices, ring_reduce_scatter(): recv = lax.ppermute(send[h], 'dp', perms[h])  32.3 us
    all_to_all x2, starting transfers between devices, per_device(): lax.all_to_all(send, 'expert', split_axis=0, concat_axis=0, tiled=True)  21 us
  transfers between devices with their start and end apart: 32, of which 27 were waited for; matrix products, arithmetic and copies ran while one was open for 7% of the time, Pallas kernels for 0%

profile of v1, /device:TPU:1, one launch (start us, length us, event | category | flops | bytes accessed | tf_op | source)
XLA Modules:
  0.0 706.0 jit_solution(14575385695354478881)
XLA Ops:
  8.3 9.4 %select_reduce_fusion = f32[1152]{0:T(1024)S(1)} fusion(f32[128,8]{0,1:T(8,128)} %param.14, s32[128,8]{0,1:T(8,128)S(1)} %add_add_fusion), kind=kLoop, calls=%fused_computation.6 | loop fusion | flops 3537792 | bytes 12800 | tf_op jit(solution)/shard_map/reduce_sum | solution.py:87
  19.9 5.0 copy.55
  24.9 13.1 %all-to-all-start = ((bf16[32,36,2048]{2,1,0:T(8,128)(2,1)}), bf16[32,36,2048]{2,1,0:T(8,128)(2,1)}, u32[]{:S(2)}, u32[]{:S(2)}) async-start(bf16[32,36,2048]{2,1,0:T(8,128)(2,1)} %copy.55), calls=%async_computation | async-start | bytes 10485760 | tf_op jit(solution)/shard_map/all_to_all | solution.py:99
  40.0 5.0 copy.59
  45.0 111.3 %all-to-all-done = bf16[32,36,2048]{2,1,0:T(8,128)(2,1)} async-done(((bf16[32,36,2048]{2,1,0:T(8,128)(2,1)}), bf16[32,36,2048]{2,1,0:T(8,128)(2,1)}, u32[]{:S(2)}, u32[]{:S(2)}) %all-to-all-start) | async-done | bytes 4718624 | tf_op jit(solution)/shard_map/all_to_all | solution.py:99
  156.3 8.0 %all-to-all-start.2 = ((bf16[32,36,2048]{2,1,0:T(8,128)(2,1)}), bf16[32,36,2048]{2,1,0:T(8,128)(2,1)}, u32[]{:S(2)}, u32[]{:S(2)}) async-start(bf16[32,36,2048]{2,1,0:T(8,128)(2,1)} %copy.59), calls=%async_computation.2 | async-start | bytes 10485760 | tf_op jit(solution)/shard_map/all_to_all | solution.py:99
  206.7 7.4 %fusion.107 = (bf16[32,18,2048]{2,1,0:T(8,128)(2,1)}, bf16[32,18,2048]{2,1,0:T(8,128)(2,1)}) fusion(bf16[32,36,2048]{2,1,0:T(8,128)(2,1)} %all-to-all-done), kind=kLoop, calls=%fused_computation.239 | loop fusion | bytes 9437184 | tf_op jit(solution)/shard_map/slice | solution.py:101
  223.3 59.6 %all-to-all-done.2 = bf16[32,36,2048]{2,1,0:T(8,128)(2,1)} async-done(((bf16[32,36,2048]{2,1,0:T(8,128)(2,1)}), bf16[32,36,2048]{2,1,0:T(8,128)(2,1)}, u32[]{:S(2)}, u32[]{:S(2)}) %all-to-all-start.2) | async-done | bytes 4718624 | tf_op jit(solution)/shard_map/all_to_all | solution.py:99
  282.9 7.5 %fusion.108 = (bf16[32,18,2048]{2,1,0:T(8,128)(2,1)}, bf16[32,18,2048]{2,1,0:T(8,128)(2,1)}) fusion(bf16[32,36,2048]{2,1,0:T(8,128)(2,1)} %all-to-all-done.2), kind=kLoop, calls=%fused_computation.240 | loop fusion | bytes 9437184 | tf_op jit(solution)/shard_map/slice | solution.py:101
  290.4 4.4 reshape.220
  294.8 4.6 fusion.10
  301.6 4.3 reshape.216
  305.9 5.0 convolution_convert_fusion.3
  314.7 12.8 %reshape.219 = bf16[576,2048]{1,0:T(8,128)(2,1)} reshape(bf16[32,18,2048]{2,1,0:T(8,128)(2,1)} %get-tuple-element.10) | data formatting | bytes 4718592 | tf_op jit(solution)/shard_map/reshape | solution.py:101
  327.5 5.1 multiply_convert_fusion.4
  355.3 4.8 convolution_convert_fusion.5
  365.8 19.5 %fusion.90 = (f32[1,147456]{1,0:T(1,128)}, f32[1,147456]{1,0:T(1,128)}, f32[1,147456]{1,0:T(1,128)}, f32[1,147456]{1,0:T(1,128)}, f32[1,147456]{1,0:T(1,128)}, /*index=5*/f32[1,147456]{1,0:T(1,128)}) fusion(s32[]{:T(128)S(6)} %select_n.347, bf16[8,98304]{1,0:T(8,128)(2,1)S(1)} %copy-done.2, bf16[8,98304]{1,0:T(8,128)(2,1)S(1)} %copy-done.5, ...), kind=kLoop, calls=%fused_computation.208 | loop fusion | flops 3538944 | bytes 6684696 | tf_op jit(solution)/shard_map/convert_element_type | solution.py:39
  385.3 19.8 %fusion.83 = (f32[1,147456]{1,0:T(1,128)}, f32[1,147456]{1,0:T(1,128)}, f32[1,147456]{1,0:T(1,128)}, f32[1,147456]{1,0:T(1,128)}, f32[1,147456]{1,0:T(1,128)}, /*index=5*/f32[1,147456]{1,0:T(1,128)}) fusion(s32[]{:T(128)S(6)} %select_n.347, bf16[8,98304]{1,0:T(8,128)(2,1)S(1)} %reshape.225, bf16[8,98304]{1,0:T(8,128)(2,1)S(1)} %copy-done.4, ...), kind=kLoop, calls=%fused_computation.201 | loop fusion | flops 3538944 | bytes 6684696 | tf_op jit(solution)/shard_map/convert_element_type | solution.py:39
  405.0 27.8 %fusion.94 = (bf16[147456]{0:T(1024)(128)(2,1)}, bf16[147456]{0:T(1024)(128)(2,1)}, f32[1,147456]{1,0:T(1,128)}, f32[1,147456]{1,0:T(1,128)}, f32[1,147456]{1,0:T(1,128)}, /*index=5*/f32[1,147456]{1,0:T(1,128)}) fusion(s32[]{:T(128)S(6)} %select_n.389, bf16[8,98304]{1,0:T(8,128)(2,1)S(1)} %bitcast.155, bf16[8,98304]{1,0:T(8,128)(2,1)S(1)} %copy-done.2, ...), kind=kLoop, calls=%fused_computation.212 | loop fusion | flops 3538944 | bytes 7667736 | tf_op jit(solution)/shard_map/jit(dynamic_index_in_dim)/dynamic_slice | solution.py:31
  432.9 27.6 %fusion.93 = (bf16[147456]{0:T(1024)(128)(2,1)}, bf16[147456]{0:T(1024)(128)(2,1)}, f32[1,147456]{1,0:T(1,128)}, f32[1,147456]{1,0:T(1,128)}, f32[1,147456]{1,0:T(1,128)}, /*index=5*/f32[1,147456]{1,0:T(1,128)}) fusion(s32[]{:T(128)S(6)} %select_n.389, bf16[8,98304]{1,0:T(8,128)(2,1)S(1)} %bitcast.153, bf16[8,98304]{1,0:T(8,128)(2,1)S(1)} %reshape.225, ...), kind=kLoop, calls=%fused_computation.211 | loop fusion | flops 3538944 | bytes 7667736 | tf_op jit(solution)/shard_map/jit(dynamic_index_in_dim)/dynamic_slice | solution.py:31
  460.4 11.2 %fusion.74 = (f32[1,147456]{1,0:T(1,128)}, f32[1,147456]{1,0:T(1,128)}, f32[1,147456]{1,0:T(1,128)}, f32[1,147456]{1,0:T(1,128)}) fusion(s32[]{:T(128)S(6)} %select_n.401, bf16[8,98304]{1,0:T(8,128)(2,1)S(1)} %bitcast.156, bf16[8,98304]{1,0:T(8,128)(2,1)S(1)} %copy-done.2, s32[]{:T(128)S(6)} %select_n.404, s32[]{:T(128)S(6)} %select_n.407, s32[]{:T(128)S(6)} %select_n.410), kind=kLoop, calls=%fused_computation.192 | loop fusion | flops 2359296 | bytes 5505040 | tf_op jit(solution)/shard_map/convert_element_type | solution.py:39
  471.6 11.2 %fusion.67 = (f32[1,147456]{1,0:T(1,128)}, f32[1,147456]{1,0:T(1,128)}, f32[1,147456]{1,0:T(1,128)}, f32[1,147456]{1,0:T(1,128)S(1)}) fusion(s32[]{:T(128)S(6)} %select_n.401, bf16[8,98304]{1,0:T(8,128)(2,1)S(1)} %bitcast.154, bf16[8,98304]{1,0:T(8,128)(2,1)S(1)} %reshape.225, s32[]{:T(128)S(6)} %select_n.404, s32[]{:T(128)S(6)} %select_n.407, s32[]{:T(128)S(6)} %select_n.410), kind=kLoop, calls=%fused_computation.185 | loop fusion | flops 2359296 | bytes 5505040 | tf_op jit(solution)/shard_map/convert_element_type | solution.py:39
  494.7 9.3 %all-to-all-start.3 = ((bf16[32,18,2048]{2,1,0:T(8,128)(2,1)}), bf16[32,18,2048]{2,1,0:T(8,128)(2,1)}, u32[]{:S(2)}, u32[]{:S(2)}) async-start(bf16[32,18,2048]{2,1,0:T(8,128)(2,1)} %reshape.221), calls=%async_computation.3 | async-start | bytes 6291456 | tf_op jit(solution)/shard_map/all_to_all | solution.py:105
  518.8 6.1 collective-permute-done.1
  529.5 4.3 collective-permute-done.8
  540.5 5.8 collective-permute-done.2
  552.6 6.1 collective-permute-done.9
  564.0 5.1 collective-permute-done.3
  573.1 5.3 collective-permute-done.10
  610.8 5.6 collective-permute-done.13
  617.1 10.7 %all-to-all-start.1 = ((bf16[32,18,2048]{2,1,0:T(8,128)(2,1)}), bf16[32,18,2048]{2,1,0:T(8,128)(2,1)}, u32[]{:S(2)}, u32[]{:S(2)}) async-start(bf16[32,18,2048]{2,1,0:T(8,128)(2,1)} %reshape.218), calls=%async_computation.1 | async-start | bytes 6291456 | tf_op jit(solution)/shard_map/all_to_all | solution.py:105
  633.8 67.7 %all-to-all-done.1 = bf16[32,18,2048]{2,1,0:T(8,128)(2,1)} async-done(((bf16[32,18,2048]{2,1,0:T(8,128)(2,1)}), bf16[32,18,2048]{2,1,0:T(8,128)(2,1)}, u32[]{:S(2)}, u32[]{:S(2)}) %all-to-all-start.1) | async-done | bytes 2359328 | tf_op jit(solution)/shard_map/all_to_all | solution.py:105
  (244 shorter events, 153.2 us)
Async XLA Ops:
  24.9 131.4 %all-to-all-start = ((bf16[32,36,2048]{2,1,0:T(8,128)(2,1)}), bf16[32,36,2048]{2,1,0:T(8,128)(2,1)}, u32[]{:S(2)}, u32[]{:S(2)}) async-start(bf16[32,36,2048]{2,1,0:T(8,128)(2,1)} %copy.55), calls=%async_computation | async-start | bytes 10485760 | tf_op jit(solution)/shard_map/all_to_all | solution.py:99
  156.3 126.5 %all-to-all-start.2 = ((bf16[32,36,2048]{2,1,0:T(8,128)(2,1)}), bf16[32,36,2048]{2,1,0:T(8,128)(2,1)}, u32[]{:S(2)}, u32[]{:S(2)}) async-start(bf16[32,36,2048]{2,1,0:T(8,128)(2,1)} %copy.59), calls=%async_computation.2 | async-start | bytes 10485760 | tf_op jit(solution)/shard_map/all_to_all | solution.py:99
  487.9 22.8 %collective-permute-start = (bf16[147456]{0:T(1024)(128)(2,1)}, bf16[147456]{0:T(1024)(128)(2,1)}, u32[]{:S(2)}, u32[]{:S(2)}) collective-permute-start(bf16[147456]{0:T(1024)(128)(2,1)} %get-tuple-element.5), channel_id=1, source_target_pairs={{0,64},{64,128},{128,192},{192,224},{224,160},{160,96},{96,32},{32... | collective-permute-start | bytes 884744 | tf_op jit(solution)/shard_map/ppermute | solution.py:37
  489.2 24.2 %collective-permute-start.14 = (bf16[147456]{0:T(1024)(128)(2,1)}, bf16[147456]{0:T(1024)(128)(2,1)}, u32[]{:S(2)}, u32[]{:S(2)}) collective-permute-start(bf16[147456]{0:T(1024)(128)(2,1)} %get-tuple-element.4), channel_id=1, source_target_pairs={{0,32},{64,0},{128,64},{192,128},{224,192},{160,224},{96,160},{32,... | collective-permute-start | bytes 884744 | tf_op jit(solution)/shard_map/ppermute | solution.py:37
  489.3 25.6 %collective-permute-start.7 = (bf16[147456]{0:T(1024)(128)(2,1)}, bf16[147456]{0:T(1024)(128)(2,1)}, u32[]{:S(2)}, u32[]{:S(2)}) collective-permute-start(bf16[147456]{0:T(1024)(128)(2,1)} %get-tuple-element.7), channel_id=1, source_target_pairs={{0,64},{64,128},{128,192},{192,224},{224,160},{160,96},{96,32},{32... | collective-permute-start | bytes 884744 | tf_op jit(solution)/shard_map/ppermute | solution.py:37
  490.6 26.8 %collective-permute-start.21 = (bf16[147456]{0:T(1024)(128)(2,1)}, bf16[147456]{0:T(1024)(128)(2,1)}, u32[]{:S(2)}, u32[]{:S(2)}) collective-permute-start(bf16[147456]{0:T(1024)(128)(2,1)} %get-tuple-element.6), channel_id=1, source_target_pairs={{0,32},{64,0},{128,64},{192,128},{224,192},{160,224},{96,160},{32,... | collective-permute-start | bytes 884744 | tf_op jit(solution)/shard_map/ppermute | solution.py:37
  494.7 122.4 %all-to-all-start.3 = ((bf16[32,18,2048]{2,1,0:T(8,128)(2,1)}), bf16[32,18,2048]{2,1,0:T(8,128)(2,1)}, u32[]{:S(2)}, u32[]{:S(2)}) async-start(bf16[32,18,2048]{2,1,0:T(8,128)(2,1)} %reshape.221), calls=%async_computation.3 | async-start | bytes 6291456 | tf_op jit(solution)/shard_map/all_to_all | solution.py:105
  512.0 12.8 %collective-permute-start.1 = (bf16[147456]{0:T(1024)(128)(2,1)S(1)}, bf16[147456]{0:T(1024)(128)(2,1)S(1)}, u32[]{:S(2)}, u32[]{:S(2)}) collective-permute-start(bf16[147456]{0:T(1024)(128)(2,1)S(1)} %add_convert_fusion.29), channel_id=1, source_target_pairs={{0,64},{64,128},{128,192},{192,224},{224,160},{160,96},{96,32},{32... | collective-permute-start | bytes 884744 | tf_op jit(solution)/shard_map/ppermute | solution.py:37
  514.7 12.2 %collective-permute-start.15 = (bf16[147456]{0:T(1024)(128)(2,1)S(1)}, bf16[147456]{0:T(1024)(128)(2,1)S(1)}, u32[]{:S(2)}, u32[]{:S(2)}) collective-permute-start(bf16[147456]{0:T(1024)(128)(2,1)S(1)} %add_convert_fusion.15), channel_id=1, source_target_pairs={{0,32},{64,0},{128,64},{192,128},{224,192},{160,224},{96,160},{32,... | collective-permute-start | bytes 884744 | tf_op jit(solution)/shard_map/ppermute | solution.py:37
  516.0 17.9 %collective-permute-start.8 = (bf16[147456]{0:T(1024)(128)(2,1)S(1)}, bf16[147456]{0:T(1024)(128)(2,1)S(1)}, u32[]{:S(2)}, u32[]{:S(2)}) collective-permute-start(bf16[147456]{0:T(1024)(128)(2,1)S(1)} %add_convert_fusion.22), channel_id=1, source_target_pairs={{0,64},{64,128},{128,192},{192,224},{224,160},{160,96},{96,32},{32... | collective-permute-start | bytes 884744 | tf_op jit(solution)/shard_map/ppermute | solution.py:37
  518.5 19.1 %collective-permute-start.22 = (bf16[147456]{0:T(1024)(128)(2,1)S(1)}, bf16[147456]{0:T(1024)(128)(2,1)S(1)}, u32[]{:S(2)}, u32[]{:S(2)}) collective-permute-start(bf16[147456]{0:T(1024)(128)(2,1)S(1)} %add_convert_fusion.8), channel_id=1, source_target_pairs={{0,32},{64,0},{128,64},{192,128},{224,192},{160,224},{96,160},{32,... | collective-permute-start | bytes 884744 | tf_op jit(solution)/shard_map/ppermute | solution.py:37
  524.9 21.3 %collective-permute-start.2 = (bf16[147456]{0:T(1024)(128)(2,1)S(1)}, bf16[147456]{0:T(1024)(128)(2,1)S(1)}, u32[]{:S(2)}, u32[]{:S(2)}) collective-permute-start(bf16[147456]{0:T(1024)(128)(2,1)S(1)} %add_convert_fusion.28), channel_id=1, source_target_pairs={{0,64},{64,128},{128,192},{192,224},{224,160},{160,96},{96,32},{32... | collective-permute-start | bytes 884744 | tf_op jit(solution)/shard_map/ppermute | solution.py:37
  526.9 22.8 %collective-permute-start.16 = (bf16[147456]{0:T(1024)(128)(2,1)S(1)}, bf16[147456]{0:T(1024)(128)(2,1)S(1)}, u32[]{:S(2)}, u32[]{:S(2)}) collective-permute-start(bf16[147456]{0:T(1024)(128)(2,1)S(1)} %add_convert_fusion.14), channel_id=1, source_target_pairs={{0,32},{64,0},{128,64},{192,128},{224,192},{160,224},{96,160},{32,... | collective-permute-start | bytes 884744 | tf_op jit(solution)/shard_map/ppermute | solution.py:37
  534.0 24.8 %collective-permute-start.9 = (bf16[147456]{0:T(1024)(128)(2,1)S(1)}, bf16[147456]{0:T(1024)(128)(2,1)S(1)}, u32[]{:S(2)}, u32[]{:S(2)}) collective-permute-start(bf16[147456]{0:T(1024)(128)(2,1)S(1)} %add_convert_fusion.21), channel_id=1, source_target_pairs={{0,64},{64,128},{128,192},{192,224},{224,160},{160,96},{96,32},{32... | collective-permute-start | bytes 884744 | tf_op jit(solution)/shard_map/ppermute | solution.py:37
  537.7 23.6 %collective-permute-start.23 = (bf16[147456]{0:T(1024)(128)(2,1)S(1)}, bf16[147456]{0:T(1024)(128)(2,1)S(1)}, u32[]{:S(2)}, u32[]{:S(2)}) collective-permute-start(bf16[147456]{0:T(1024)(128)(2,1)S(1)} %add_convert_fusion.7), channel_id=1, source_target_pairs={{0,32},{64,0},{128,64},{192,128},{224,192},{160,224},{96,160},{32,... | collective-permute-start | bytes 884744 | tf_op jit(solution)/shard_map/ppermute | solution.py:37
  546.3 22.8 %collective-permute-start.3 = (bf16[147456]{0:T(1024)(128)(2,1)S(1)}, bf16[147456]{0:T(1024)(128)(2,1)S(1)}, u32[]{:S(2)}, u32[]{:S(2)}) collective-permute-start(bf16[147456]{0:T(1024)(128)(2,1)S(1)} %add_convert_fusion.27), channel_id=1, source_target_pairs={{0,64},{64,128},{128,192},{192,224},{224,160},{160,96},{96,32},{32... | collective-permute-start | bytes 884744 | tf_op jit(solution)/shard_map/ppermute | solution.py:37
  549.8 20.6 %collective-permute-start.17 = (bf16[147456]{0:T(1024)(128)(2,1)S(1)}, bf16[147456]{0:T(1024)(128)(2,1)S(1)}, u32[]{:S(2)}, u32[]{:S(2)}) collective-permute-start(bf16[147456]{0:T(1024)(128)(2,1)S(1)} %add_convert_fusion.13), channel_id=1, source_target_pairs={{0,32},{64,0},{128,64},{192,128},{224,192},{160,224},{96,160},{32,... | collective-permute-start | bytes 884744 | tf_op jit(solution)/shard_map/ppermute | solution.py:37
  558.8 19.6 %collective-permute-start.10 = (bf16[147456]{0:T(1024)(128)(2,1)S(1)}, bf16[147456]{0:T(1024)(128)(2,1)S(1)}, u32[]{:S(2)}, u32[]{:S(2)}) collective-permute-start(bf16[147456]{0:T(1024)(128)(2,1)S(1)} %add_convert_fusion.20), channel_id=1, source_target_pairs={{0,64},{64,128},{128,192},{192,224},{224,160},{160,96},{96,32},{32... | collective-permute-start | bytes 884744 | tf_op jit(solution)/shard_map/ppermute | solution.py:37
  561.3 17.8 %collective-permute-start.24 = (bf16[147456]{0:T(1024)(128)(2,1)S(1)}, bf16[147456]{0:T(1024)(128)(2,1)S(1)}, u32[]{:S(2)}, u32[]{:S(2)}) collective-permute-start(bf16[147456]{0:T(1024)(128)(2,1)S(1)} %add_convert_fusion.6), channel_id=1, source_target_pairs={{0,32},{64,0},{128,64},{192,128},{224,192},{160,224},{96,160},{32,... | collective-permute-start | bytes 884744 | tf_op jit(solution)/shard_map/ppermute | solution.py:37
  569.2 15.6 %collective-permute-start.4 = (bf16[147456]{0:T(1024)(128)(2,1)S(1)}, bf16[147456]{0:T(1024)(128)(2,1)S(1)}, u32[]{:S(2)}, u32[]{:S(2)}) collective-permute-start(bf16[147456]{0:T(1024)(128)(2,1)S(1)} %add_convert_fusion.26), channel_id=1, source_target_pairs={{0,64},{64,128},{128,192},{192,224},{224,160},{160,96},{96,32},{32... | collective-permute-start | bytes 884744 | tf_op jit(solution)/shard_map/ppermute | solution.py:37
  570.5 14.9 %collective-permute-start.18 = (bf16[147456]{0:T(1024)(128)(2,1)S(1)}, bf16[147456]{0:T(1024)(128)(2,1)S(1)}, u32[]{:S(2)}, u32[]{:S(2)}) collective-permute-start(bf16[147456]{0:T(1024)(128)(2,1)S(1)} %add_convert_fusion.12), channel_id=1, source_target_pairs={{0,32},{64,0},{128,64},{192,128},{224,192},{160,224},{96,160},{32,... | collective-permute-start | bytes 884744 | tf_op jit(solution)/shard_map/ppermute | solution.py:37
  578.5 12.6 %collective-permute-start.11 = (bf16[147456]{0:T(1024)(128)(2,1)S(1)}, bf16[147456]{0:T(1024)(128)(2,1)S(1)}, u32[]{:S(2)}, u32[]{:S(2)}) collective-permute-start(bf16[147456]{0:T(1024)(128)(2,1)S(1)} %add_convert_fusion.19), channel_id=1, source_target_pairs={{0,64},{64,128},{128,192},{192,224},{224,160},{160,96},{96,32},{32... | collective-permute-start | bytes 884744 | tf_op jit(solution)/shard_map/ppermute | solution.py:37
  579.2 12.6 %collective-permute-start.25 = (bf16[147456]{0:T(1024)(128)(2,1)S(1)}, bf16[147456]{0:T(1024)(128)(2,1)S(1)}, u32[]{:S(2)}, u32[]{:S(2)}) collective-permute-start(bf16[147456]{0:T(1024)(128)(2,1)S(1)} %add_convert_fusion.5), channel_id=1, source_target_pairs={{0,32},{64,0},{128,64},{192,128},{224,192},{160,224},{96,160},{32,... | collective-permute-start | bytes 884744 | tf_op jit(solution)/shard_map/ppermute | solution.py:37
  584.8 12.6 %collective-permute-start.5 = (bf16[147456]{0:T(1024)(128)(2,1)S(1)}, bf16[147456]{0:T(1024)(128)(2,1)S(1)}, u32[]{:S(2)}, u32[]{:S(2)}) collective-permute-start(bf16[147456]{0:T(1024)(128)(2,1)S(1)} %add_convert_fusion.25), channel_id=1, source_target_pairs={{0,64},{64,128},{128,192},{192,224},{224,160},{160,96},{96,32},{32... | collective-permute-start | bytes 884744 | tf_op jit(solution)/shard_map/ppermute | solution.py:37
  585.5 12.6 %collective-permute-start.19 = (bf16[147456]{0:T(1024)(128)(2,1)S(1)}, bf16[147456]{0:T(1024)(128)(2,1)S(1)}, u32[]{:S(2)}, u32[]{:S(2)}) collective-permute-start(bf16[147456]{0:T(1024)(128)(2,1)S(1)} %add_convert_fusion.11), channel_id=1, source_target_pairs={{0,32},{64,0},{128,64},{192,128},{224,192},{160,224},{96,160},{32,... | collective-permute-start | bytes 884744 | tf_op jit(solution)/shard_map/ppermute | solution.py:37
  591.2 12.6 %collective-permute-start.12 = (bf16[147456]{0:T(1024)(128)(2,1)S(1)}, bf16[147456]{0:T(1024)(128)(2,1)S(1)}, u32[]{:S(2)}, u32[]{:S(2)}) collective-permute-start(bf16[147456]{0:T(1024)(128)(2,1)S(1)} %add_convert_fusion.18), channel_id=1, source_target_pairs={{0,64},{64,128},{128,192},{192,224},{224,160},{160,96},{96,32},{32... | collective-permute-start | bytes 884744 | tf_op jit(solution)/shard_map/ppermute | solution.py:37
  591.9 12.6 %collective-permute-start.26 = (bf16[147456]{0:T(1024)(128)(2,1)S(1)}, bf16[147456]{0:T(1024)(128)(2,1)S(1)}, u32[]{:S(2)}, u32[]{:S(2)}) collective-permute-start(bf16[147456]{0:T(1024)(128)(2,1)S(1)} %add_convert_fusion.4), channel_id=1, source_target_pairs={{0,32},{64,0},{128,64},{192,128},{224,192},{160,224},{96,160},{32,... | collective-permute-start | bytes 884744 | tf_op jit(solution)/shard_map/ppermute | solution.py:37
  597.5 12.6 %collective-permute-start.6 = (bf16[147456]{0:T(1024)(128)(2,1)S(1)}, bf16[147456]{0:T(1024)(128)(2,1)S(1)}, u32[]{:S(2)}, u32[]{:S(2)}) collective-permute-start(bf16[147456]{0:T(1024)(128)(2,1)S(1)} %add_convert_fusion.24), channel_id=1, source_target_pairs={{0,64},{64,128},{128,192},{192,224},{224,160},{160,96},{96,32},{32... | collective-permute-start | bytes 884744 | tf_op jit(solution)/shard_map/ppermute | solution.py:37
  598.1 12.6 %collective-permute-start.20 = (bf16[147456]{0:T(1024)(128)(2,1)S(1)}, bf16[147456]{0:T(1024)(128)(2,1)S(1)}, u32[]{:S(2)}, u32[]{:S(2)}) collective-permute-start(bf16[147456]{0:T(1024)(128)(2,1)S(1)} %add_convert_fusion.10), channel_id=1, source_target_pairs={{0,32},{64,0},{128,64},{192,128},{224,192},{160,224},{96,160},{32,... | collective-permute-start | bytes 884744 | tf_op jit(solution)/shard_map/ppermute | solution.py:37
  603.8 12.6 %collective-permute-start.13 = (bf16[147456]{0:T(1024)(128)(2,1)S(1)}, bf16[147456]{0:T(1024)(128)(2,1)S(1)}, u32[]{:S(2)}, u32[]{:S(2)}) collective-permute-start(bf16[147456]{0:T(1024)(128)(2,1)S(1)} %add_convert_fusion.17), channel_id=1, source_target_pairs={{0,64},{64,128},{128,192},{192,224},{224,160},{160,96},{96,32},{32... | collective-permute-start | bytes 884744 | tf_op jit(solution)/shard_map/ppermute | solution.py:37
  604.5 12.6 %collective-permute-start.27 = (bf16[147456]{0:T(1024)(128)(2,1)S(1)}, bf16[147456]{0:T(1024)(128)(2,1)S(1)}, u32[]{:S(2)}, u32[]{:S(2)}) collective-permute-start(bf16[147456]{0:T(1024)(128)(2,1)S(1)} %add_convert_fusion.3), channel_id=1, source_target_pairs={{0,32},{64,0},{128,64},{192,128},{224,192},{160,224},{96,160},{32,... | collective-permute-start | bytes 884744 | tf_op jit(solution)/shard_map/ppermute | solution.py:37
  617.1 84.4 %all-to-all-start.1 = ((bf16[32,18,2048]{2,1,0:T(8,128)(2,1)}), bf16[32,18,2048]{2,1,0:T(8,128)(2,1)}, u32[]{:S(2)}, u32[]{:S(2)}) async-start(bf16[32,18,2048]{2,1,0:T(8,128)(2,1)} %reshape.218), calls=%async_computation.1 | async-start | bytes 6291456 | tf_op jit(solution)/shard_map/all_to_all | solution.py:105
  (56 other events, 1033.0 us)

commit v2 on v1

--- a/solution.py
+++ b/solution.py
@@ -42,19 +42,19 @@
 
 
 def expert_work(xr, scaled, w_gate, w_up, w_down):
-    gate = contract(xr, w_gate, (1,), (0,))
-    up = contract(xr, w_up, (1,), (0,))
+    gate = contract(xr, w_gate, (2,), (0,))
+    up = contract(xr, w_up, (2,), (0,))
     sig = jax.nn.sigmoid(gate)
     act = (gate * sig * up).astype(jnp.bfloat16)
-    dh = contract(scaled, w_down, (1,), (1,))
+    dh = contract(scaled, w_down, (2,), (1,))
     dgate = (dh * up * sig * (1.0 + gate * (1.0 - sig))).astype(jnp.bfloat16)
     dup = (dh * gate * sig).astype(jnp.bfloat16)
-    contrib = (contract(dgate, w_gate, (1,), (1,)) + contract(dup, w_up, (1,), (1,))).astype(
+    contrib = (contract(dgate, w_gate, (2,), (1,)) + contract(dup, w_up, (2,), (1,))).astype(
         jnp.bfloat16
     )
-    grad_g = contract(xr, dgate, (0,), (0,)).astype(jnp.bfloat16)
-    grad_u = contract(xr, dup, (0,), (0,)).astype(jnp.bfloat16)
-    grad_d = contract(act, scaled, (0,), (0,)).astype(jnp.bfloat16)
+    grad_g = contract(xr, dgate, (0, 1), (0, 1)).astype(jnp.bfloat16)
+    grad_u = contract(xr, dup, (0, 1), (0, 1)).astype(jnp.bfloat16)
+    grad_d = contract(act, scaled, (0, 1), (0, 1)).astype(jnp.bfloat16)
     return contrib, grad_g, grad_u, grad_d
 
 
@@ -67,7 +67,6 @@
     experts = exp_dev * n_owner
     slots = tok_dev * top_k * 9 // (experts * 8)
     n_slot = experts * slots
-    rows = n_owner * slots
 
     columns = jnp.arange(experts, dtype=jnp.int32)
     onehot = expert_ids[:, :, None] == columns[None, None, :]
@@ -97,14 +96,12 @@
         send_dy = (p_slot[:, local][:, :, None] * dy_rows).astype(jnp.bfloat16)
         send = jnp.concatenate([send_x, send_dy], axis=1)
         recv = lax.all_to_all(send, "expert", split_axis=0, concat_axis=0, tiled=True)
-        xr = recv[:, :slots].reshape(rows, width)
-        scaled = recv[:, slots:].reshape(rows, width)
+        xr = recv[:, :slots]
+        scaled = recv[:, slots:]
         contrib, grad_g, grad_u, grad_d = expert_work(
             xr, scaled, gate_weight[local], up_weight[local], down_weight[local]
         )
-        back = lax.all_to_all(
-            contrib.reshape(n_owner, slots, width), "expert", split_axis=0, concat_axis=0, tiled=True
-        )
+        back = lax.all_to_all(contrib, "expert", split_axis=0, concat_axis=0, tiled=True)
         contrib_back.append(back)
         grads.append((grad_g, grad_u, grad_d))
 
@@ -117,18 +114,19 @@
     dsl = width // n_dp
     reduced = []
     for grad_g, grad_u, grad_d in grads:
+        lanes = 1024
         packed = jnp.concatenate(
             [
-                grad_g.reshape(n_dp, dsl * hid),
-                grad_u.reshape(n_dp, dsl * hid),
-                grad_d.reshape(hid, n_dp, dsl).transpose(1, 0, 2).reshape(n_dp, hid * dsl),
+                grad_g.reshape(n_dp, dsl * hid // lanes, lanes),
+                grad_u.reshape(n_dp, dsl * hid // lanes, lanes),
+                grad_d.reshape(hid, n_dp, dsl).transpose(1, 0, 2).reshape(n_dp, hid * dsl // lanes, lanes),
             ],
             axis=1,
         )
-        reduced.append(ring_reduce_scatter(packed, n_dp))
-    stack_g = jnp.stack([r[: dsl * hid].reshape(dsl, hid) for r in reduced], axis=0)
-    stack_u = jnp.stack([r[dsl * hid : 2 * dsl * hid].reshape(dsl, hid) for r in reduced], axis=0)
-    stack_d = jnp.stack([r[2 * dsl * hid :].reshape(hid, dsl) for r in reduced], axis=0)
+        reduced.append(ring_reduce_scatter(packed, n_dp).reshape(3, dsl * hid))
+    stack_g = jnp.stack([r[0].reshape(dsl, hid) for r in reduced], axis=0)
+    stack_u = jnp.stack([r[1].reshape(dsl, hid) for r in reduced], axis=0)
+    stack_d = jnp.stack([r[2].reshape(hid, dsl) for r in reduced], axis=0)
     return (in_grad, stack_g, stack_u, stack_d)
 
 

time: 712 us -> 613 us (0.86)
  other arithmetic: 142 us -> 64.8 us
  local copies, waits for them, and re-layouts: 73.6 us -> 53.8 us
    all_to_all x2, waiting for transfers between devices: 67.8 us -> 0.01 us  [per_device(): lax.all_to_all(contrib, 'expert', split_axis=0, concat_axis=0, tiled=True)]
    convert_element_type x4 -> x0, other arithmetic: 61.6 us -> none  [ring_reduce_scatter(): acc[h] = recv.astype(jnp.float32) + own(h, chunk).astype(jnp.float32)]
    dynamic_slice x2 -> x0, other arithmetic: 55.4 us -> none  [own(): lax.dynamic_index_in_dim(halves[h], ring_arr[c % n_dp], axis=0, keepdims=...]
    ppermute x28, waiting for transfers between devices: 70.6 us -> 111 us  [ring_reduce_scatter(): recv = lax.ppermute(send[h], 'dp', perms[h])]
    convert_element_type x28 -> x25, other arithmetic: 6.12 us -> 41 us  [ring_reduce_scatter(): send[h] = acc[h].astype(jnp.bfloat16)]
    all_to_all x2, waiting for transfers between devices: 171 us -> 202 us  [per_device(): lax.all_to_all(send, 'expert', split_axis=0, concat_axis=0, tiled=True)]
    reshape x10 -> x6, local copies, waits for them, and re-layouts: 41.5 us -> 17.5 us  [the longest x2 7.83 us: per_device(): grad_g.reshape(n_dp, dsl * hid // lanes, lanes)]
    ppermute x28, starting transfers between devices: 32.3 us -> 24 us  [ring_reduce_scatter(): recv = lax.ppermute(send[h], 'dp', perms[h])]
  transfers between devices with their start and end apart: 32 -> 32, of which waited for: 27 -> 23; matrix products, arithmetic and copies ran while one was open for 7% -> 17% of each run, Pallas kernels for 0% -> 0%
where the time goes in v2:
time: 613 us; the launch traced here: 603 us
  waiting for transfers between devices  313 us (51%)
  starting transfers between devices  67.9 us (11%)
  other arithmetic  64.8 us (11%)
  matrix products  61.4 us (10%)
  local copies, waits for them, and re-layouts  53.8 us (9%)
  between operations  42.3 us (7%)
    all_to_all x2, waiting for transfers between devices, per_device(): lax.all_to_all(send, 'expert', split_axis=0, concat_axis=0, tiled=True)  202 us
    ppermute x28, waiting for transfers between devices, ring_reduce_scatter(): recv = lax.ppermute(send[h], 'dp', perms[h])  111 us
    dot_general x23, matrix products, contract(): lax.dot_general(left, right, ((left_dims, right_dims), ((), ())), preferr...  61.4 us
    convert_element_type x25, other arithmetic, ring_reduce_scatter(): send[h] = acc[h].astype(jnp.bfloat16)  41 us
    ppermute x28, starting transfers between devices, ring_reduce_scatter(): recv = lax.ppermute(send[h], 'dp', perms[h])  24 us
    all_to_all x2, starting transfers between devices, per_device(): lax.all_to_all(contrib, 'expert', split_axis=0, concat_axis=0, tiled=True)  22.8 us
    all_to_all x2, starting transfers between devices, per_device(): lax.all_to_all(send, 'expert', split_axis=0, concat_axis=0, tiled=True)  21 us
  transfers between devices with their start and end apart: 32, of which 23 were waited for; matrix products, arithmetic and copies ran while one was open for 17% of the time, Pallas kernels for 0%

profile of v2, /device:TPU:1, one launch (start us, length us, event | category | flops | bytes accessed | tf_op | source)
XLA Modules:
  0.0 602.8 jit_solution(11594493043088756394)
XLA Ops:
  3.9 4.2 fusion
  8.1 9.3 %select_reduce_fusion = f32[1152]{0:T(1024)S(1)} fusion(f32[128,8]{0,1:T(8,128)} %param.14, s32[128,8]{0,1:T(8,128)S(1)} %add_add_fusion), kind=kLoop, calls=%fused_computation.6 | loop fusion | flops 3537792 | bytes 12800 | tf_op jit(solution)/shard_map/reduce_sum | solution.py:86
  19.9 5.0 copy.59
  24.9 13.1 %all-to-all-start = ((bf16[32,36,2048]{2,1,0:T(8,128)(2,1)}), bf16[32,36,2048]{2,1,0:T(8,128)(2,1)}, u32[]{:S(2)}, u32[]{:S(2)}) async-start(bf16[32,36,2048]{2,1,0:T(8,128)(2,1)} %copy.59), calls=%async_computation | async-start | bytes 10485760 | tf_op jit(solution)/shard_map/all_to_all | solution.py:98
  40.0 5.0 copy.66
  45.0 111.4 %all-to-all-done = bf16[32,36,2048]{2,1,0:T(8,128)(2,1)} async-done(((bf16[32,36,2048]{2,1,0:T(8,128)(2,1)}), bf16[32,36,2048]{2,1,0:T(8,128)(2,1)}, u32[]{:S(2)}, u32[]{:S(2)}) %all-to-all-start) | async-done | bytes 4718624 | tf_op jit(solution)/shard_map/all_to_all | solution.py:98
  156.3 8.0 %all-to-all-start.2 = ((bf16[32,36,2048]{2,1,0:T(8,128)(2,1)}), bf16[32,36,2048]{2,1,0:T(8,128)(2,1)}, u32[]{:S(2)}, u32[]{:S(2)}) async-start(bf16[32,36,2048]{2,1,0:T(8,128)(2,1)} %copy.66), calls=%async_computation.2 | async-start | bytes 10485760 | tf_op jit(solution)/shard_map/all_to_all | solution.py:98
  180.3 6.3 %fusion.119 = (bf16[32,18,2048]{2,1,0:T(8,128)(2,1)}, bf16[32,18,2048]{2,1,0:T(8,128)(2,1)S(1)}) fusion(bf16[32,36,2048]{2,1,0:T(8,128)(2,1)} %all-to-all-done), kind=kLoop, calls=%fused_computation.251 | loop fusion | bytes 9437184 | tf_op jit(solution)/shard_map/slice | solution.py:100
  192.4 90.4 %all-to-all-done.2 = bf16[32,36,2048]{2,1,0:T(8,128)(2,1)} async-done(((bf16[32,36,2048]{2,1,0:T(8,128)(2,1)}), bf16[32,36,2048]{2,1,0:T(8,128)(2,1)}, u32[]{:S(2)}, u32[]{:S(2)}) %all-to-all-start.2) | async-done | bytes 4718624 | tf_op jit(solution)/shard_map/all_to_all | solution.py:98
  282.9 4.3 fusion.120
  295.0 11.5 %multiply_convert_fusion.6 = (bf16[32,18,384]{2,0,1:T(8,128)(2,1)}, bf16[32,18,384]{2,0,1:T(8,128)(2,1)}) fusion(f32[32,18,384]{2,0,1:T(8,128)S(1)} %copy-done.44, f32[32,18,384]{2,0,1:T(8,128)S(1)} %copy-done.45, bf16[2,384,2048]{2,1,0:T(8,128)(2,1)S(1)} %copy-done.42, bf16[32,18,2048]{2,1,0:T(8,128)(2,1)S(1)} %copy-done.22), kind=kOutput, calls=%fused_computation.124 | convolution fusion | flops 908845056 | bytes 7372800 | tf_op jit(solution)/shard_map/dot_general | solution.py:8
  315.9 4.4 bitcast_convert_fusion.4
  341.8 9.3 %all-to-all-start.3 = ((bf16[32,18,2048]{2,1,0:T(8,128)(2,1)}), bf16[32,18,2048]{2,1,0:T(8,128)(2,1)}, u32[]{:S(2)}, u32[]{:S(2)}) async-start(bf16[32,18,2048]{2,1,0:T(8,128)(2,1)} %copy.69), calls=%async_computation.3 | async-start | bytes 6291456 | tf_op jit(solution)/shard_map/all_to_all | solution.py:104
  351.2 5.4 bitcast_convert_fusion.3
  363.0 4.3 reshape.198
  375.0 4.1 collective-permute-done.21
  385.1 6.0 collective-permute-done.15
  395.3 8.2 %collective-permute-done.22 = bf16[144,1024]{1,0:T(8,128)(2,1)} collective-permute-done((bf16[144,1024]{1,0:T(8,128)(2,1)}, bf16[144,1024]{1,0:T(8,128)(2,1)}, u32[]{:S(2)}, u32[]{:S(2)}) %collective-permute-start.22) | collective-permute-done | bytes 294944 | tf_op jit(solution)/shard_map/ppermute | solution.py:37
  409.8 4.4 collective-permute-done.16
  418.5 5.5 collective-permute-done.23
  456.8 5.8 collective-permute-done.26
  470.4 13.5 %all-to-all-start.1 = ((bf16[32,18,2048]{2,1,0:T(8,128)(2,1)}), bf16[32,18,2048]{2,1,0:T(8,128)(2,1)}, u32[]{:S(2)}, u32[]{:S(2)}) async-start(bf16[32,18,2048]{2,1,0:T(8,128)(2,1)} %copy.62), calls=%async_computation.1 | async-start | bytes 6291456 | tf_op jit(solution)/shard_map/all_to_all | solution.py:104
  491.3 11.8 %collective-permute-done.8 = bf16[144,1024]{1,0:T(8,128)(2,1)} collective-permute-done((bf16[144,1024]{1,0:T(8,128)(2,1)}, bf16[144,1024]{1,0:T(8,128)(2,1)}, u32[]{:S(2)}, u32[]{:S(2)}) %collective-permute-start.8) | collective-permute-done | bytes 294944 | tf_op jit(solution)/shard_map/ppermute | solution.py:37
  506.7 5.2 collective-permute-done.2
  513.7 10.2 %collective-permute-done.9 = bf16[144,1024]{1,0:T(8,128)(2,1)} collective-permute-done((bf16[144,1024]{1,0:T(8,128)(2,1)}, bf16[144,1024]{1,0:T(8,128)(2,1)}, u32[]{:S(2)}, u32[]{:S(2)}) %collective-permute-start.9) | collective-permute-done | bytes 294944 | tf_op jit(solution)/shard_map/ppermute | solution.py:37
  527.8 8.2 %collective-permute-done.3 = bf16[144,1024]{1,0:T(8,128)(2,1)} collective-permute-done((bf16[144,1024]{1,0:T(8,128)(2,1)}, bf16[144,1024]{1,0:T(8,128)(2,1)}, u32[]{:S(2)}, u32[]{:S(2)}) %collective-permute-start.3) | collective-permute-done | bytes 294944 | tf_op jit(solution)/shard_map/ppermute | solution.py:37
  537.8 8.4 %collective-permute-done.10 = bf16[144,1024]{1,0:T(8,128)(2,1)} collective-permute-done((bf16[144,1024]{1,0:T(8,128)(2,1)}, bf16[144,1024]{1,0:T(8,128)(2,1)}, u32[]{:S(2)}, u32[]{:S(2)}) %collective-permute-start.10) | collective-permute-done | bytes 294944 | tf_op jit(solution)/shard_map/ppermute | solution.py:37
  549.8 7.0 %collective-permute-done.4 = bf16[144,1024]{1,0:T(8,128)(2,1)} collective-permute-done((bf16[144,1024]{1,0:T(8,128)(2,1)}, bf16[144,1024]{1,0:T(8,128)(2,1)}, u32[]{:S(2)}, u32[]{:S(2)}) %collective-permute-start.4) | collective-permute-done | bytes 294944 | tf_op jit(solution)/shard_map/ppermute | solution.py:37
  558.6 4.5 collective-permute-done.11
  571.3 4.5 collective-permute-done.12
  582.1 6.3 %collective-permute-done.13 = bf16[144,1024]{1,0:T(8,128)(2,1)} collective-permute-done((bf16[144,1024]{1,0:T(8,128)(2,1)}, bf16[144,1024]{1,0:T(8,128)(2,1)}, u32[]{:S(2)}, u32[]{:S(2)}) %collective-permute-start.13) | collective-permute-done | bytes 294944 | tf_op jit(solution)/shard_map/ppermute | solution.py:37
  598.1 4.2 fusion.2
  (218 shorter events, 150.5 us)
Async XLA Ops:
  24.9 131.4 %all-to-all-start = ((bf16[32,36,2048]{2,1,0:T(8,128)(2,1)}), bf16[32,36,2048]{2,1,0:T(8,128)(2,1)}, u32[]{:S(2)}, u32[]{:S(2)}) async-start(bf16[32,36,2048]{2,1,0:T(8,128)(2,1)} %copy.59), calls=%async_computation | async-start | bytes 10485760 | tf_op jit(solution)/shard_map/all_to_all | solution.py:98
  156.3 126.5 %all-to-all-start.2 = ((bf16[32,36,2048]{2,1,0:T(8,128)(2,1)}), bf16[32,36,2048]{2,1,0:T(8,128)(2,1)}, u32[]{:S(2)}, u32[]{:S(2)}) async-start(bf16[32,36,2048]{2,1,0:T(8,128)(2,1)} %copy.66), calls=%async_computation.2 | async-start | bytes 10485760 | tf_op jit(solution)/shard_map/all_to_all | solution.py:98
  331.2 40.5 %collective-permute-start.14 = (bf16[144,1024]{1,0:T(8,128)(2,1)}, bf16[144,1024]{1,0:T(8,128)(2,1)}, u32[]{:S(2)}, u32[]{:S(2)}) collective-permute-start(bf16[144,1024]{1,0:T(8,128)(2,1)} %get-tuple-element.14), channel_id=1, source_target_pairs={{0,32},{64,0},{128,64},{192,128},{224,192},{160,224},{96,160},{32,... | collective-permute-start | bytes 884744 | tf_op jit(solution)/shard_map/ppermute | solution.py:37
  341.8 128.6 %all-to-all-start.3 = ((bf16[32,18,2048]{2,1,0:T(8,128)(2,1)}), bf16[32,18,2048]{2,1,0:T(8,128)(2,1)}, u32[]{:S(2)}, u32[]{:S(2)}) async-start(bf16[32,18,2048]{2,1,0:T(8,128)(2,1)} %copy.69), calls=%async_computation.3 | async-start | bytes 6291456 | tf_op jit(solution)/shard_map/all_to_all | solution.py:104
  369.2 9.9 %collective-permute-start.21 = (bf16[144,1024]{1,0:T(8,128)(2,1)}, bf16[144,1024]{1,0:T(8,128)(2,1)}, u32[]{:S(2)}, u32[]{:S(2)}) collective-permute-start(bf16[144,1024]{1,0:T(8,128)(2,1)} %get-tuple-element.18), channel_id=1, source_target_pairs={{0,32},{64,0},{128,64},{192,128},{224,192},{160,224},{96,160},{32,... | collective-permute-start | bytes 884744 | tf_op jit(solution)/shard_map/ppermute | solution.py:37
  373.7 17.4 %collective-permute-start.15 = (bf16[144,1024]{1,0:T(8,128)(2,1)}, bf16[144,1024]{1,0:T(8,128)(2,1)}, u32[]{:S(2)}, u32[]{:S(2)}) collective-permute-start(bf16[144,1024]{1,0:T(8,128)(2,1)} %fusion.50), channel_id=1, source_target_pairs={{0,32},{64,0},{128,64},{192,128},{224,192},{160,224},{96,160},{32,... | collective-permute-start | bytes 884744 | tf_op jit(solution)/shard_map/ppermute | solution.py:37
  380.8 22.7 %collective-permute-start.22 = (bf16[144,1024]{1,0:T(8,128)(2,1)}, bf16[144,1024]{1,0:T(8,128)(2,1)}, u32[]{:S(2)}, u32[]{:S(2)}) collective-permute-start(bf16[144,1024]{1,0:T(8,128)(2,1)} %fusion.43), channel_id=1, source_target_pairs={{0,32},{64,0},{128,64},{192,128},{224,192},{160,224},{96,160},{32,... | collective-permute-start | bytes 884744 | tf_op jit(solution)/shard_map/ppermute | solution.py:37
  392.9 21.4 %collective-permute-start.16 = (bf16[144,1024]{1,0:T(8,128)(2,1)}, bf16[144,1024]{1,0:T(8,128)(2,1)}, u32[]{:S(2)}, u32[]{:S(2)}) collective-permute-start(bf16[144,1024]{1,0:T(8,128)(2,1)} %fusion.49), channel_id=1, source_target_pairs={{0,32},{64,0},{128,64},{192,128},{224,192},{160,224},{96,160},{32,... | collective-permute-start | bytes 884744 | tf_op jit(solution)/shard_map/ppermute | solution.py:37
  405.3 18.7 %collective-permute-start.23 = (bf16[144,1024]{1,0:T(8,128)(2,1)}, bf16[144,1024]{1,0:T(8,128)(2,1)}, u32[]{:S(2)}, u32[]{:S(2)}) collective-permute-start(bf16[144,1024]{1,0:T(8,128)(2,1)} %fusion.42), channel_id=1, source_target_pairs={{0,32},{64,0},{128,64},{192,128},{224,192},{160,224},{96,160},{32,... | collective-permute-start | bytes 884744 | tf_op jit(solution)/shard_map/ppermute | solution.py:37
  416.1 14.2 %collective-permute-start.17 = (bf16[144,1024]{1,0:T(8,128)(2,1)}, bf16[144,1024]{1,0:T(8,128)(2,1)}, u32[]{:S(2)}, u32[]{:S(2)}) collective-permute-start(bf16[144,1024]{1,0:T(8,128)(2,1)} %fusion.48), channel_id=1, source_target_pairs={{0,32},{64,0},{128,64},{192,128},{224,192},{160,224},{96,160},{32,... | collective-permute-start | bytes 884744 | tf_op jit(solution)/shard_map/ppermute | solution.py:37
  425.7 10.9 %collective-permute-start.24 = (bf16[144,1024]{1,0:T(8,128)(2,1)}, bf16[144,1024]{1,0:T(8,128)(2,1)}, u32[]{:S(2)}, u32[]{:S(2)}) collective-permute-start(bf16[144,1024]{1,0:T(8,128)(2,1)} %fusion.41), channel_id=1, source_target_pairs={{0,32},{64,0},{128,64},{192,128},{224,192},{160,224},{96,160},{32,... | collective-permute-start | bytes 884744 | tf_op jit(solution)/shard_map/ppermute | solution.py:37
  432.1 15.9 %collective-permute-start.18 = (bf16[144,1024]{1,0:T(8,128)(2,1)}, bf16[144,1024]{1,0:T(8,128)(2,1)}, u32[]{:S(2)}, u32[]{:S(2)}) collective-permute-start(bf16[144,1024]{1,0:T(8,128)(2,1)} %fusion.47), channel_id=1, source_target_pairs={{0,32},{64,0},{128,64},{192,128},{224,192},{160,224},{96,160},{32,... | collective-permute-start | bytes 884744 | tf_op jit(solution)/shard_map/ppermute | solution.py:37
  438.4 10.9 %collective-permute-start.25 = (bf16[144,1024]{1,0:T(8,128)(2,1)}, bf16[144,1024]{1,0:T(8,128)(2,1)}, u32[]{:S(2)}, u32[]{:S(2)}) collective-permute-start(bf16[144,1024]{1,0:T(8,128)(2,1)} %fusion.40), channel_id=1, source_target_pairs={{0,32},{64,0},{128,64},{192,128},{224,192},{160,224},{96,160},{32,... | collective-permute-start | bytes 884744 | tf_op jit(solution)/shard_map/ppermute | solution.py:37
  449.2 7.1 %collective-permute-start.19 = (bf16[144,1024]{1,0:T(8,128)(2,1)S(1)}, bf16[144,1024]{1,0:T(8,128)(2,1)S(1)}, u32[]{:S(2)}, u32[]{:S(2)}) collective-permute-start(bf16[144,1024]{1,0:T(8,128)(2,1)S(1)} %fusion.46), channel_id=1, source_target_pairs={{0,32},{64,0},{128,64},{192,128},{224,192},{160,224},{96,160},{32,... | collective-permute-start | bytes 884744 | tf_op jit(solution)/shard_map/ppermute | solution.py:37
  450.8 11.9 %collective-permute-start.26 = (bf16[144,1024]{1,0:T(8,128)(2,1)S(1)}, bf16[144,1024]{1,0:T(8,128)(2,1)S(1)}, u32[]{:S(2)}, u32[]{:S(2)}) collective-permute-start(bf16[144,1024]{1,0:T(8,128)(2,1)S(1)} %fusion.39), channel_id=1, source_target_pairs={{0,32},{64,0},{128,64},{192,128},{224,192},{160,224},{96,160},{32,... | collective-permute-start | bytes 884744 | tf_op jit(solution)/shard_map/ppermute | solution.py:37
  454.0 14.3 %collective-permute-start = (bf16[144,1024]{1,0:T(8,128)(2,1)S(1)}, bf16[144,1024]{1,0:T(8,128)(2,1)S(1)}, u32[]{:S(2)}, u32[]{:S(2)}) collective-permute-start(bf16[144,1024]{1,0:T(8,128)(2,1)S(1)} %get-tuple-element.15), channel_id=1, source_target_pairs={{0,64},{64,128},{128,192},{192,224},{224,160},{160,96},{96,32},{32... | collective-permute-start | bytes 884744 | tf_op jit(solution)/shard_map/ppermute | solution.py:37
  454.1 29.9 %collective-permute-start.7 = (bf16[144,1024]{1,0:T(8,128)(2,1)}, bf16[144,1024]{1,0:T(8,128)(2,1)}, u32[]{:S(2)}, u32[]{:S(2)}) collective-permute-start(bf16[144,1024]{1,0:T(8,128)(2,1)} %get-tuple-element.19), channel_id=1, source_target_pairs={{0,64},{64,128},{128,192},{192,224},{224,160},{160,96},{96,32},{32... | collective-permute-start | bytes 884744 | tf_op jit(solution)/shard_map/ppermute | solution.py:37
  456.5 12.6 %collective-permute-start.20 = (bf16[144,1024]{1,0:T(8,128)(2,1)S(1)}, bf16[144,1024]{1,0:T(8,128)(2,1)S(1)}, u32[]{:S(2)}, u32[]{:S(2)}) collective-permute-start(bf16[144,1024]{1,0:T(8,128)(2,1)S(1)} %fusion.45), channel_id=1, source_target_pairs={{0,32},{64,0},{128,64},{192,128},{224,192},{160,224},{96,160},{32,... | collective-permute-start | bytes 884744 | tf_op jit(solution)/shard_map/ppermute | solution.py:37
  463.5 20.5 %collective-permute-start.27 = (bf16[144,1024]{1,0:T(8,128)(2,1)}, bf16[144,1024]{1,0:T(8,128)(2,1)}, u32[]{:S(2)}, u32[]{:S(2)}) collective-permute-start(bf16[144,1024]{1,0:T(8,128)(2,1)} %fusion.38), channel_id=1, source_target_pairs={{0,32},{64,0},{128,64},{192,128},{224,192},{160,224},{96,160},{32,... | collective-permute-start | bytes 884744 | tf_op jit(solution)/shard_map/ppermute | solution.py:37
  470.1 18.4 %collective-permute-start.1 = (bf16[144,1024]{1,0:T(8,128)(2,1)}, bf16[144,1024]{1,0:T(8,128)(2,1)}, u32[]{:S(2)}, u32[]{:S(2)}) collective-permute-start(bf16[144,1024]{1,0:T(8,128)(2,1)} %get-tuple-element.13), channel_id=1, source_target_pairs={{0,64},{64,128},{128,192},{192,224},{224,160},{160,96},{96,32},{32... | collective-permute-start | bytes 884744 | tf_op jit(solution)/shard_map/ppermute | solution.py:37
  470.4 127.7 %all-to-all-start.1 = ((bf16[32,18,2048]{2,1,0:T(8,128)(2,1)}), bf16[32,18,2048]{2,1,0:T(8,128)(2,1)}, u32[]{:S(2)}, u32[]{:S(2)}) async-start(bf16[32,18,2048]{2,1,0:T(8,128)(2,1)} %copy.62), calls=%async_computation.1 | async-start | bytes 6291456 | tf_op jit(solution)/shard_map/all_to_all | solution.py:104
  486.3 16.8 %collective-permute-start.8 = (bf16[144,1024]{1,0:T(8,128)(2,1)}, bf16[144,1024]{1,0:T(8,128)(2,1)}, u32[]{:S(2)}, u32[]{:S(2)}) collective-permute-start(bf16[144,1024]{1,0:T(8,128)(2,1)} %get-tuple-element.17), channel_id=1, source_target_pairs={{0,64},{64,128},{128,192},{192,224},{224,160},{160,96},{96,32},{32... | collective-permute-start | bytes 884744 | tf_op jit(solution)/shard_map/ppermute | solution.py:37
  490.4 21.5 %collective-permute-start.2 = (bf16[144,1024]{1,0:T(8,128)(2,1)}, bf16[144,1024]{1,0:T(8,128)(2,1)}, u32[]{:S(2)}, u32[]{:S(2)}) collective-permute-start(bf16[144,1024]{1,0:T(8,128)(2,1)} %fusion.63), channel_id=1, source_target_pairs={{0,64},{64,128},{128,192},{192,224},{224,160},{160,96},{96,32},{32... | collective-permute-start | bytes 884744 | tf_op jit(solution)/shard_map/ppermute | solution.py:37
  504.8 19.1 %collective-permute-start.9 = (bf16[144,1024]{1,0:T(8,128)(2,1)}, bf16[144,1024]{1,0:T(8,128)(2,1)}, u32[]{:S(2)}, u32[]{:S(2)}) collective-permute-start(bf16[144,1024]{1,0:T(8,128)(2,1)} %fusion.56), channel_id=1, source_target_pairs={{0,64},{64,128},{128,192},{192,224},{224,160},{160,96},{96,32},{32... | collective-permute-start | bytes 884744 | tf_op jit(solution)/shard_map/ppermute | solution.py:37
  513.7 22.2 %collective-permute-start.3 = (bf16[144,1024]{1,0:T(8,128)(2,1)}, bf16[144,1024]{1,0:T(8,128)(2,1)}, u32[]{:S(2)}, u32[]{:S(2)}) collective-permute-start(bf16[144,1024]{1,0:T(8,128)(2,1)} %fusion.62), channel_id=1, source_target_pairs={{0,64},{64,128},{128,192},{192,224},{224,160},{160,96},{96,32},{32... | collective-permute-start | bytes 884744 | tf_op jit(solution)/shard_map/ppermute | solution.py:37
  525.7 20.4 %collective-permute-start.10 = (bf16[144,1024]{1,0:T(8,128)(2,1)}, bf16[144,1024]{1,0:T(8,128)(2,1)}, u32[]{:S(2)}, u32[]{:S(2)}) collective-permute-start(bf16[144,1024]{1,0:T(8,128)(2,1)} %fusion.55), channel_id=1, source_target_pairs={{0,64},{64,128},{128,192},{192,224},{224,160},{160,96},{96,32},{32... | collective-permute-start | bytes 884744 | tf_op jit(solution)/shard_map/ppermute | solution.py:37
  537.8 19.0 %collective-permute-start.4 = (bf16[144,1024]{1,0:T(8,128)(2,1)}, bf16[144,1024]{1,0:T(8,128)(2,1)}, u32[]{:S(2)}, u32[]{:S(2)}) collective-permute-start(bf16[144,1024]{1,0:T(8,128)(2,1)} %fusion.61), channel_id=1, source_target_pairs={{0,64},{64,128},{128,192},{192,224},{224,160},{160,96},{96,32},{32... | collective-permute-start | bytes 884744 | tf_op jit(solution)/shard_map/ppermute | solution.py:37
  547.9 15.2 %collective-permute-start.11 = (bf16[144,1024]{1,0:T(8,128)(2,1)}, bf16[144,1024]{1,0:T(8,128)(2,1)}, u32[]{:S(2)}, u32[]{:S(2)}) collective-permute-start(bf16[144,1024]{1,0:T(8,128)(2,1)} %fusion.54), channel_id=1, source_target_pairs={{0,64},{64,128},{128,192},{192,224},{224,160},{160,96},{96,32},{32... | collective-permute-start | bytes 884744 | tf_op jit(solution)/shard_map/ppermute | solution.py:37
  558.6 10.8 %collective-permute-start.5 = (bf16[144,1024]{1,0:T(8,128)(2,1)}, bf16[144,1024]{1,0:T(8,128)(2,1)}, u32[]{:S(2)}, u32[]{:S(2)}) collective-permute-start(bf16[144,1024]{1,0:T(8,128)(2,1)} %fusion.60), channel_id=1, source_target_pairs={{0,64},{64,128},{128,192},{192,224},{224,160},{160,96},{96,32},{32... | collective-permute-start | bytes 884744 | tf_op jit(solution)/shard_map/ppermute | solution.py:37
  564.9 10.9 %collective-permute-start.12 = (bf16[144,1024]{1,0:T(8,128)(2,1)}, bf16[144,1024]{1,0:T(8,128)(2,1)}, u32[]{:S(2)}, u32[]{:S(2)}) collective-permute-start(bf16[144,1024]{1,0:T(8,128)(2,1)} %fusion.53), channel_id=1, source_target_pairs={{0,64},{64,128},{128,192},{192,224},{224,160},{160,96},{96,32},{32... | collective-permute-start | bytes 884744 | tf_op jit(solution)/shard_map/ppermute | solution.py:37
  571.3 10.8 %collective-permute-start.6 = (bf16[144,1024]{1,0:T(8,128)(2,1)}, bf16[144,1024]{1,0:T(8,128)(2,1)}, u32[]{:S(2)}, u32[]{:S(2)}) collective-permute-start(bf16[144,1024]{1,0:T(8,128)(2,1)} %fusion.59), channel_id=1, source_target_pairs={{0,64},{64,128},{128,192},{192,224},{224,160},{160,96},{96,32},{32... | collective-permute-start | bytes 884744 | tf_op jit(solution)/shard_map/ppermute | solution.py:37
  577.5 10.9 %collective-permute-start.13 = (bf16[144,1024]{1,0:T(8,128)(2,1)}, bf16[144,1024]{1,0:T(8,128)(2,1)}, u32[]{:S(2)}, u32[]{:S(2)}) collective-permute-start(bf16[144,1024]{1,0:T(8,128)(2,1)} %fusion.52), channel_id=1, source_target_pairs={{0,64},{64,128},{128,192},{192,224},{224,160},{160,96},{96,32},{32... | collective-permute-start | bytes 884744 | tf_op jit(solution)/shard_map/ppermute | solution.py:37
  (46 other events, 557.7 us)

commit v3 on v2

--- a/solution.py
+++ b/solution.py
@@ -87,7 +87,7 @@
     sel = sel.reshape(n_owner, exp_dev, slots, tok_dev)
     p_slot = p_slot.reshape(n_owner, exp_dev, slots)
 
-    contrib_back = []
+    contribs = []
     grads = []
     for local in range(exp_dev):
         sel_l = sel[:, local]
@@ -101,15 +101,14 @@
         contrib, grad_g, grad_u, grad_d = expert_work(
             xr, scaled, gate_weight[local], up_weight[local], down_weight[local]
         )
-        back = lax.all_to_all(contrib, "expert", split_axis=0, concat_axis=0, tiled=True)
-        contrib_back.append(back)
+        contribs.append(contrib)
         grads.append((grad_g, grad_u, grad_d))
 
-    in_grad = None
-    for local in range(exp_dev):
-        part = contract(sel[:, local], contrib_back[local], (0, 1), (0, 1))
-        in_grad = part if in_grad is None else in_grad + part
-    in_grad = in_grad.astype(jnp.bfloat16)
+    back = lax.all_to_all(
+        jnp.concatenate(contribs, axis=1), "expert", split_axis=0, concat_axis=0, tiled=True
+    )
+    sel_all = sel.reshape(n_owner, exp_dev * slots, tok_dev)
+    in_grad = contract(sel_all, back, (0, 1), (0, 1)).astype(jnp.bfloat16)
 
     dsl = width // n_dp
     reduced = []

time: 613 us -> 587 us (0.958)
  waiting for transfers between devices: 313 us -> 294 us
  other arithmetic: 64.8 us -> 73.8 us
  starting transfers between devices: 67.9 us -> 60.6 us
    ppermute x28, waiting for transfers between devices: 111 us -> 92.3 us  [ring_reduce_scatter(): recv = lax.ppermute(send[h], 'dp', perms[h])]
    all_to_all x2 -> x1, starting transfers between devices: 22.8 us -> 8.3 us  [per_device(): lax.all_to_all(jnp.concatenate(contribs, axis=1), 'expert', split_axis=0,...]
    ppermute x28, starting transfers between devices: 24 us -> 31.3 us  [ring_reduce_scatter(): recv = lax.ppermute(send[h], 'dp', perms[h])]
    convert_element_type x2 -> x0, local copies, waits for them, and re-layouts: 6.16 us -> none  [expert_work(): (contract(dgate, w_gate, (2,), (1,)) + contract(dup, w_up, (2,), (1,))).a...]
    dot_general x23 -> x22, matrix products: 61.4 us -> 57.8 us  [contract(): lax.dot_general(left, right, ((left_dims, right_dims), ((), ())), preferr...]
  transfers between devices with their start and end apart: 32 -> 31, of which waited for: 23 -> 26; matrix products, arithmetic and copies ran while one was open for 17% -> 18% of each run, Pallas kernels for 0% -> 0%
where the time goes in v3:
time: 587 us; the launch traced here: 576 us
  waiting for transfers between devices  294 us (50%)
  other arithmetic  73.8 us (13%)
  starting transfers between devices  60.6 us (10%)
  matrix products  57.8 us (10%)
  local copies, waits for them, and re-layouts  48.2 us (8%)
  between operations  41.8 us (7%)
    all_to_all x2, waiting for transfers between devices, per_device(): lax.all_to_all(send, 'expert', split_axis=0, concat_axis=0, tiled=True)  202 us
    ppermute x28, waiting for transfers between devices, ring_reduce_scatter(): recv = lax.ppermute(send[h], 'dp', perms[h])  92.3 us
    dot_general x22, matrix products, contract(): lax.dot_general(left, right, ((left_dims, right_dims), ((), ())), preferr...  57.8 us
    convert_element_type x25, other arithmetic, ring_reduce_scatter(): send[h] = acc[h].astype(jnp.bfloat16)  45.9 us
    ppermute x28, starting transfers between devices, ring_reduce_scatter(): recv = lax.ppermute(send[h], 'dp', perms[h])  31.3 us
    all_to_all x2, starting transfers between devices, per_device(): lax.all_to_all(send, 'expert', split_axis=0, concat_axis=0, tiled=True)  21 us
  transfers between devices with their start and end apart: 31, of which 26 were waited for; matrix products, arithmetic and copies ran while one was open for 18% of the time, Pallas kernels for 0%

profile of v3, /device:TPU:1, one launch (start us, length us, event | category | flops | bytes accessed | tf_op | source)
XLA Modules:
  0.0 576.4 jit_solution(2959227597251327280)
XLA Ops:
  3.9 4.2 fusion
  8.1 9.4 %select_reduce_fusion = f32[1152]{0:T(1024)S(1)} fusion(f32[128,8]{0,1:T(8,128)} %param.14, s32[128,8]{0,1:T(8,128)S(1)} %add_add_fusion), kind=kLoop, calls=%fused_computation.7 | loop fusion | flops 3537792 | bytes 12800 | tf_op jit(solution)/shard_map/reduce_sum | solution.py:86
  19.9 5.0 copy.59
  24.9 13.1 %all-to-all-start = ((bf16[32,36,2048]{2,1,0:T(8,128)(2,1)}), bf16[32,36,2048]{2,1,0:T(8,128)(2,1)}, u32[]{:S(2)}, u32[]{:S(2)}) async-start(bf16[32,36,2048]{2,1,0:T(8,128)(2,1)} %copy.59), calls=%async_computation | async-start | bytes 10485760 | tf_op jit(solution)/shard_map/all_to_all | solution.py:98
  40.0 5.0 copy.66
  45.0 111.4 %all-to-all-done = bf16[32,36,2048]{2,1,0:T(8,128)(2,1)} async-done(((bf16[32,36,2048]{2,1,0:T(8,128)(2,1)}), bf16[32,36,2048]{2,1,0:T(8,128)(2,1)}, u32[]{:S(2)}, u32[]{:S(2)}) %all-to-all-start) | async-done | bytes 4718624 | tf_op jit(solution)/shard_map/all_to_all | solution.py:98
  156.4 8.0 %all-to-all-start.1 = ((bf16[32,36,2048]{2,1,0:T(8,128)(2,1)}), bf16[32,36,2048]{2,1,0:T(8,128)(2,1)}, u32[]{:S(2)}, u32[]{:S(2)}) async-start(bf16[32,36,2048]{2,1,0:T(8,128)(2,1)} %copy.66), calls=%async_computation.1 | async-start | bytes 10485760 | tf_op jit(solution)/shard_map/all_to_all | solution.py:98
  180.3 6.3 %fusion.120 = (bf16[32,18,2048]{2,1,0:T(8,128)(2,1)}, bf16[32,18,2048]{2,1,0:T(8,128)(2,1)S(1)}) fusion(bf16[32,36,2048]{2,1,0:T(8,128)(2,1)} %all-to-all-done), kind=kLoop, calls=%fused_computation.252 | loop fusion | bytes 9437184 | tf_op jit(solution)/shard_map/slice | solution.py:100
  192.4 90.5 %all-to-all-done.1 = bf16[32,36,2048]{2,1,0:T(8,128)(2,1)} async-done(((bf16[32,36,2048]{2,1,0:T(8,128)(2,1)}), bf16[32,36,2048]{2,1,0:T(8,128)(2,1)}, u32[]{:S(2)}, u32[]{:S(2)}) %all-to-all-start.1) | async-done | bytes 4718624 | tf_op jit(solution)/shard_map/all_to_all | solution.py:98
  282.9 4.3 fusion.121
  296.2 10.7 %multiply_convert_fusion.6 = (bf16[32,18,384]{2,0,1:T(8,128)(2,1)S(1)}, bf16[32,18,384]{2,0,1:T(8,128)(2,1)S(1)}) fusion(f32[32,18,384]{2,0,1:T(8,128)S(1)} %copy-done.39, f32[32,18,384]{2,0,1:T(8,128)S(1)} %copy-done.40, bf16[2,384,2048]{2,1,0:T(8,128)(2,1)S(1)} %copy-done.37, bf16[32,18,2048]{2,1,0:T(8,128)(2,1)S(1)} %copy-done.22), kind=kOutput, calls=%fused_computation.121 | convolution fusion | flops 908845056 | bytes 7372800 | tf_op jit(solution)/shard_map/dot_general | solution.py:8
  308.8 3.5 bitcast_convert_fusion
  312.3 3.5 bitcast_convert_fusion.5
  327.2 4.0 pad_maximum_fusion
  331.2 8.3 %all-to-all-start.2 = ((bf16[32,36,2048]{2,1,0:T(8,128)(2,1)}), bf16[32,36,2048]{2,1,0:T(8,128)(2,1)}, u32[]{:S(2)}, u32[]{:S(2)}) async-start(bf16[32,36,2048]{2,1,0:T(8,128)(2,1)} %pad_maximum_fusion), calls=%async_computation.2 | async-start | bytes 10485760 | tf_op jit(solution)/shard_map/all_to_all | solution.py:107
  339.6 4.6 bitcast_convert_fusion.2
  365.0 4.3 reshape.198
  386.0 8.5 %collective-permute-done.15 = bf16[144,1024]{1,0:T(8,128)(2,1)} collective-permute-done((bf16[144,1024]{1,0:T(8,128)(2,1)}, bf16[144,1024]{1,0:T(8,128)(2,1)}, u32[]{:S(2)}, u32[]{:S(2)}) %collective-permute-start.15) | collective-permute-done | bytes 294944 | tf_op jit(solution)/shard_map/ppermute | solution.py:37
  398.7 5.5 collective-permute-done.22
  410.4 6.3 %collective-permute-done.16 = bf16[144,1024]{1,0:T(8,128)(2,1)} collective-permute-done((bf16[144,1024]{1,0:T(8,128)(2,1)}, bf16[144,1024]{1,0:T(8,128)(2,1)}, u32[]{:S(2)}, u32[]{:S(2)}) %collective-permute-start.16) | collective-permute-done | bytes 294944 | tf_op jit(solution)/shard_map/ppermute | solution.py:37
  421.4 4.6 collective-permute-done.23
  427.7 3.7 collective-permute-start.24
  433.2 6.8 %collective-permute-done.17 = bf16[144,1024]{1,0:T(8,128)(2,1)} collective-permute-done((bf16[144,1024]{1,0:T(8,128)(2,1)}, bf16[144,1024]{1,0:T(8,128)(2,1)}, u32[]{:S(2)}, u32[]{:S(2)}) %collective-permute-start.17) | collective-permute-done | bytes 294944 | tf_op jit(solution)/shard_map/ppermute | solution.py:37
  444.5 4.2 collective-permute-done.24
  454.7 3.8 collective-permute-done.18
  496.5 5.8 %collective-permute-done.8 = bf16[144,1024]{1,0:T(8,128)(2,1)} collective-permute-done((bf16[144,1024]{1,0:T(8,128)(2,1)}, bf16[144,1024]{1,0:T(8,128)(2,1)}, u32[]{:S(2)}, u32[]{:S(2)}) %collective-permute-start.8) | collective-permute-done | bytes 294944 | tf_op jit(solution)/shard_map/ppermute | solution.py:37
  510.4 4.5 collective-permute-done.9
  523.1 4.5 collective-permute-done.10
  535.7 4.5 collective-permute-done.11
  548.4 4.5 collective-permute-done.12
  559.2 6.3 %collective-permute-done.13 = bf16[144,1024]{1,0:T(8,128)(2,1)} collective-permute-done((bf16[144,1024]{1,0:T(8,128)(2,1)}, bf16[144,1024]{1,0:T(8,128)(2,1)}, u32[]{:S(2)}, u32[]{:S(2)}) %collective-permute-start.13) | collective-permute-done | bytes 294944 | tf_op jit(solution)/shard_map/ppermute | solution.py:37
  571.7 4.2 fusion.1
  (205 shorter events, 160.7 us)
Async XLA Ops:
  24.9 131.4 %all-to-all-start = ((bf16[32,36,2048]{2,1,0:T(8,128)(2,1)}), bf16[32,36,2048]{2,1,0:T(8,128)(2,1)}, u32[]{:S(2)}, u32[]{:S(2)}) async-start(bf16[32,36,2048]{2,1,0:T(8,128)(2,1)} %copy.59), calls=%async_computation | async-start | bytes 10485760 | tf_op jit(solution)/shard_map/all_to_all | solution.py:98
  45.0 130.6 %copy-start.36 = (s32[8]{0:T(128)S(1)}, s32[8]{0:T(128)}, u32[]{:S(2)}) copy-start(s32[8]{0:T(128)} %constant.317.clone) | copy-start | bytes 100
  156.4 126.5 %all-to-all-start.1 = ((bf16[32,36,2048]{2,1,0:T(8,128)(2,1)}), bf16[32,36,2048]{2,1,0:T(8,128)(2,1)}, u32[]{:S(2)}, u32[]{:S(2)}) async-start(bf16[32,36,2048]{2,1,0:T(8,128)(2,1)} %copy.66), calls=%async_computation.1 | async-start | bytes 10485760 | tf_op jit(solution)/shard_map/all_to_all | solution.py:98
  331.2 240.5 %all-to-all-start.2 = ((bf16[32,36,2048]{2,1,0:T(8,128)(2,1)}), bf16[32,36,2048]{2,1,0:T(8,128)(2,1)}, u32[]{:S(2)}, u32[]{:S(2)}) async-start(bf16[32,36,2048]{2,1,0:T(8,128)(2,1)} %pad_maximum_fusion), calls=%async_computation.2 | async-start | bytes 10485760 | tf_op jit(solution)/shard_map/all_to_all | solution.py:107
  354.5 19.8 %collective-permute-start.14 = (bf16[144,1024]{1,0:T(8,128)(2,1)}, bf16[144,1024]{1,0:T(8,128)(2,1)}, u32[]{:S(2)}, u32[]{:S(2)}) collective-permute-start(bf16[144,1024]{1,0:T(8,128)(2,1)} %get-tuple-element.14), channel_id=1, source_target_pairs={{0,32},{64,0},{128,64},{192,128},{224,192},{160,224},{96,160},{32,... | collective-permute-start | bytes 884744 | tf_op jit(solution)/shard_map/ppermute | solution.py:37
  371.2 8.6 %collective-permute-start.21 = (bf16[144,1024]{1,0:T(8,128)(2,1)}, bf16[144,1024]{1,0:T(8,128)(2,1)}, u32[]{:S(2)}, u32[]{:S(2)}) collective-permute-start(bf16[144,1024]{1,0:T(8,128)(2,1)} %get-tuple-element.18), channel_id=1, source_target_pairs={{0,32},{64,0},{128,64},{192,128},{224,192},{160,224},{96,160},{32,... | collective-permute-start | bytes 884744 | tf_op jit(solution)/shard_map/ppermute | solution.py:37
  376.2 18.2 %collective-permute-start.15 = (bf16[144,1024]{1,0:T(8,128)(2,1)}, bf16[144,1024]{1,0:T(8,128)(2,1)}, u32[]{:S(2)}, u32[]{:S(2)}) collective-permute-start(bf16[144,1024]{1,0:T(8,128)(2,1)} %fusion.47), channel_id=1, source_target_pairs={{0,32},{64,0},{128,64},{192,128},{224,192},{160,224},{96,160},{32,... | collective-permute-start | bytes 884744 | tf_op jit(solution)/shard_map/ppermute | solution.py:37
  381.6 22.6 %collective-permute-start.22 = (bf16[144,1024]{1,0:T(8,128)(2,1)}, bf16[144,1024]{1,0:T(8,128)(2,1)}, u32[]{:S(2)}, u32[]{:S(2)}) collective-permute-start(bf16[144,1024]{1,0:T(8,128)(2,1)} %fusion.40), channel_id=1, source_target_pairs={{0,32},{64,0},{128,64},{192,128},{224,192},{160,224},{96,160},{32,... | collective-permute-start | bytes 884744 | tf_op jit(solution)/shard_map/ppermute | solution.py:37
  396.2 20.5 %collective-permute-start.16 = (bf16[144,1024]{1,0:T(8,128)(2,1)}, bf16[144,1024]{1,0:T(8,128)(2,1)}, u32[]{:S(2)}, u32[]{:S(2)}) collective-permute-start(bf16[144,1024]{1,0:T(8,128)(2,1)} %fusion.46), channel_id=1, source_target_pairs={{0,32},{64,0},{128,64},{192,128},{224,192},{160,224},{96,160},{32,... | collective-permute-start | bytes 884744 | tf_op jit(solution)/shard_map/ppermute | solution.py:37
  406.0 20.0 %collective-permute-start.23 = (bf16[144,1024]{1,0:T(8,128)(2,1)}, bf16[144,1024]{1,0:T(8,128)(2,1)}, u32[]{:S(2)}, u32[]{:S(2)}) collective-permute-start(bf16[144,1024]{1,0:T(8,128)(2,1)} %fusion.39), channel_id=1, source_target_pairs={{0,32},{64,0},{128,64},{192,128},{224,192},{160,224},{96,160},{32,... | collective-permute-start | bytes 884744 | tf_op jit(solution)/shard_map/ppermute | solution.py:37
  418.6 21.4 %collective-permute-start.17 = (bf16[144,1024]{1,0:T(8,128)(2,1)}, bf16[144,1024]{1,0:T(8,128)(2,1)}, u32[]{:S(2)}, u32[]{:S(2)}) collective-permute-start(bf16[144,1024]{1,0:T(8,128)(2,1)} %fusion.45), channel_id=1, source_target_pairs={{0,32},{64,0},{128,64},{192,128},{224,192},{160,224},{96,160},{32,... | collective-permute-start | bytes 884744 | tf_op jit(solution)/shard_map/ppermute | solution.py:37
  427.7 20.9 %collective-permute-start.24 = (bf16[144,1024]{1,0:T(8,128)(2,1)}, bf16[144,1024]{1,0:T(8,128)(2,1)}, u32[]{:S(2)}, u32[]{:S(2)}) collective-permute-start(bf16[144,1024]{1,0:T(8,128)(2,1)} %fusion.38), channel_id=1, source_target_pairs={{0,32},{64,0},{128,64},{192,128},{224,192},{160,224},{96,160},{32,... | collective-permute-start | bytes 884744 | tf_op jit(solution)/shard_map/ppermute | solution.py:37
  441.8 16.7 %collective-permute-start.18 = (bf16[144,1024]{1,0:T(8,128)(2,1)}, bf16[144,1024]{1,0:T(8,128)(2,1)}, u32[]{:S(2)}, u32[]{:S(2)}) collective-permute-start(bf16[144,1024]{1,0:T(8,128)(2,1)} %fusion.44), channel_id=1, source_target_pairs={{0,32},{64,0},{128,64},{192,128},{224,192},{160,224},{96,160},{32,... | collective-permute-start | bytes 884744 | tf_op jit(solution)/shard_map/ppermute | solution.py:37
  450.5 14.4 %collective-permute-start.25 = (bf16[144,1024]{1,0:T(8,128)(2,1)}, bf16[144,1024]{1,0:T(8,128)(2,1)}, u32[]{:S(2)}, u32[]{:S(2)}) collective-permute-start(bf16[144,1024]{1,0:T(8,128)(2,1)} %fusion.37), channel_id=1, source_target_pairs={{0,32},{64,0},{128,64},{192,128},{224,192},{160,224},{96,160},{32,... | collective-permute-start | bytes 884744 | tf_op jit(solution)/shard_map/ppermute | solution.py:37
  460.3 10.8 %collective-permute-start.19 = (bf16[144,1024]{1,0:T(8,128)(2,1)}, bf16[144,1024]{1,0:T(8,128)(2,1)}, u32[]{:S(2)}, u32[]{:S(2)}) collective-permute-start(bf16[144,1024]{1,0:T(8,128)(2,1)} %fusion.43), channel_id=1, source_target_pairs={{0,32},{64,0},{128,64},{192,128},{224,192},{160,224},{96,160},{32,... | collective-permute-start | bytes 884744 | tf_op jit(solution)/shard_map/ppermute | solution.py:37
  466.6 10.9 %collective-permute-start.26 = (bf16[144,1024]{1,0:T(8,128)(2,1)}, bf16[144,1024]{1,0:T(8,128)(2,1)}, u32[]{:S(2)}, u32[]{:S(2)}) collective-permute-start(bf16[144,1024]{1,0:T(8,128)(2,1)} %fusion.36), channel_id=1, source_target_pairs={{0,32},{64,0},{128,64},{192,128},{224,192},{160,224},{96,160},{32,... | collective-permute-start | bytes 884744 | tf_op jit(solution)/shard_map/ppermute | solution.py:37
  470.5 14.5 %collective-permute-start = (bf16[144,1024]{1,0:T(8,128)(2,1)S(1)}, bf16[144,1024]{1,0:T(8,128)(2,1)}, u32[]{:S(2)}, u32[]{:S(2)}) collective-permute-start(bf16[144,1024]{1,0:T(8,128)(2,1)S(1)} %get-tuple-element.15), channel_id=1, source_target_pairs={{0,64},{64,128},{128,192},{192,224},{224,160},{160,96},{96,32},{32... | collective-permute-start | bytes 884744 | tf_op jit(solution)/shard_map/ppermute | solution.py:37
  473.0 12.0 %collective-permute-start.20 = (bf16[144,1024]{1,0:T(8,128)(2,1)}, bf16[144,1024]{1,0:T(8,128)(2,1)}, u32[]{:S(2)}, u32[]{:S(2)}) collective-permute-start(bf16[144,1024]{1,0:T(8,128)(2,1)} %fusion.42), channel_id=1, source_target_pairs={{0,32},{64,0},{128,64},{192,128},{224,192},{160,224},{96,160},{32,... | collective-permute-start | bytes 884744 | tf_op jit(solution)/shard_map/ppermute | solution.py:37
  475.2 12.2 %collective-permute-start.7 = (bf16[144,1024]{1,0:T(8,128)(2,1)}, bf16[144,1024]{1,0:T(8,128)(2,1)}, u32[]{:S(2)}, u32[]{:S(2)}) collective-permute-start(bf16[144,1024]{1,0:T(8,128)(2,1)} %get-tuple-element.19), channel_id=1, source_target_pairs={{0,64},{64,128},{128,192},{192,224},{224,160},{160,96},{96,32},{32... | collective-permute-start | bytes 884744 | tf_op jit(solution)/shard_map/ppermute | solution.py:37
  479.2 10.9 %collective-permute-start.27 = (bf16[144,1024]{1,0:T(8,128)(2,1)}, bf16[144,1024]{1,0:T(8,128)(2,1)}, u32[]{:S(2)}, u32[]{:S(2)}) collective-permute-start(bf16[144,1024]{1,0:T(8,128)(2,1)} %fusion.35), channel_id=1, source_target_pairs={{0,32},{64,0},{128,64},{192,128},{224,192},{160,224},{96,160},{32,... | collective-permute-start | bytes 884744 | tf_op jit(solution)/shard_map/ppermute | solution.py:37
  487.3 7.0 %collective-permute-start.1 = (bf16[144,1024]{1,0:T(8,128)(2,1)}, bf16[144,1024]{1,0:T(8,128)(2,1)}, u32[]{:S(2)}, u32[]{:S(2)}) collective-permute-start(bf16[144,1024]{1,0:T(8,128)(2,1)} %get-tuple-element.13), channel_id=1, source_target_pairs={{0,64},{64,128},{128,192},{192,224},{224,160},{160,96},{96,32},{32... | collective-permute-start | bytes 884744 | tf_op jit(solution)/shard_map/ppermute | solution.py:37
  492.2 10.1 %collective-permute-start.8 = (bf16[144,1024]{1,0:T(8,128)(2,1)}, bf16[144,1024]{1,0:T(8,128)(2,1)}, u32[]{:S(2)}, u32[]{:S(2)}) collective-permute-start(bf16[144,1024]{1,0:T(8,128)(2,1)} %get-tuple-element.17), channel_id=1, source_target_pairs={{0,64},{64,128},{128,192},{192,224},{224,160},{160,96},{96,32},{32... | collective-permute-start | bytes 884744 | tf_op jit(solution)/shard_map/ppermute | solution.py:37
  496.2 12.5 %collective-permute-start.2 = (bf16[144,1024]{1,0:T(8,128)(2,1)}, bf16[144,1024]{1,0:T(8,128)(2,1)}, u32[]{:S(2)}, u32[]{:S(2)}) collective-permute-start(bf16[144,1024]{1,0:T(8,128)(2,1)} %fusion.60), channel_id=1, source_target_pairs={{0,64},{64,128},{128,192},{192,224},{224,160},{160,96},{96,32},{32... | collective-permute-start | bytes 884744 | tf_op jit(solution)/shard_map/ppermute | solution.py:37
  504.1 10.9 %collective-permute-start.9 = (bf16[144,1024]{1,0:T(8,128)(2,1)}, bf16[144,1024]{1,0:T(8,128)(2,1)}, u32[]{:S(2)}, u32[]{:S(2)}) collective-permute-start(bf16[144,1024]{1,0:T(8,128)(2,1)} %fusion.53), channel_id=1, source_target_pairs={{0,64},{64,128},{128,192},{192,224},{224,160},{160,96},{96,32},{32... | collective-permute-start | bytes 884744 | tf_op jit(solution)/shard_map/ppermute | solution.py:37
  510.4 10.8 %collective-permute-start.3 = (bf16[144,1024]{1,0:T(8,128)(2,1)}, bf16[144,1024]{1,0:T(8,128)(2,1)}, u32[]{:S(2)}, u32[]{:S(2)}) collective-permute-start(bf16[144,1024]{1,0:T(8,128)(2,1)} %fusion.59), channel_id=1, source_target_pairs={{0,64},{64,128},{128,192},{192,224},{224,160},{160,96},{96,32},{32... | collective-permute-start | bytes 884744 | tf_op jit(solution)/shard_map/ppermute | solution.py:37
  516.7 10.9 %collective-permute-start.10 = (bf16[144,1024]{1,0:T(8,128)(2,1)}, bf16[144,1024]{1,0:T(8,128)(2,1)}, u32[]{:S(2)}, u32[]{:S(2)}) collective-permute-start(bf16[144,1024]{1,0:T(8,128)(2,1)} %fusion.52), channel_id=1, source_target_pairs={{0,64},{64,128},{128,192},{192,224},{224,160},{160,96},{96,32},{32... | collective-permute-start | bytes 884744 | tf_op jit(solution)/shard_map/ppermute | solution.py:37
  523.1 10.8 %collective-permute-start.4 = (bf16[144,1024]{1,0:T(8,128)(2,1)}, bf16[144,1024]{1,0:T(8,128)(2,1)}, u32[]{:S(2)}, u32[]{:S(2)}) collective-permute-start(bf16[144,1024]{1,0:T(8,128)(2,1)} %fusion.58), channel_id=1, source_target_pairs={{0,64},{64,128},{128,192},{192,224},{224,160},{160,96},{96,32},{32... | collective-permute-start | bytes 884744 | tf_op jit(solution)/shard_map/ppermute | solution.py:37
  529.3 10.9 %collective-permute-start.11 = (bf16[144,1024]{1,0:T(8,128)(2,1)}, bf16[144,1024]{1,0:T(8,128)(2,1)}, u32[]{:S(2)}, u32[]{:S(2)}) collective-permute-start(bf16[144,1024]{1,0:T(8,128)(2,1)} %fusion.51), channel_id=1, source_target_pairs={{0,64},{64,128},{128,192},{192,224},{224,160},{160,96},{96,32},{32... | collective-permute-start | bytes 884744 | tf_op jit(solution)/shard_map/ppermute | solution.py:37
  535.7 10.8 %collective-permute-start.5 = (bf16[144,1024]{1,0:T(8,128)(2,1)}, bf16[144,1024]{1,0:T(8,128)(2,1)}, u32[]{:S(2)}, u32[]{:S(2)}) collective-permute-start(bf16[144,1024]{1,0:T(8,128)(2,1)} %fusion.57), channel_id=1, source_target_pairs={{0,64},{64,128},{128,192},{192,224},{224,160},{160,96},{96,32},{32... | collective-permute-start | bytes 884744 | tf_op jit(solution)/shard_map/ppermute | solution.py:37
  542.0 10.9 %collective-permute-start.12 = (bf16[144,1024]{1,0:T(8,128)(2,1)}, bf16[144,1024]{1,0:T(8,128)(2,1)}, u32[]{:S(2)}, u32[]{:S(2)}) collective-permute-start(bf16[144,1024]{1,0:T(8,128)(2,1)} %fusion.50), channel_id=1, source_target_pairs={{0,64},{64,128},{128,192},{192,224},{224,160},{160,96},{96,32},{32... | collective-permute-start | bytes 884744 | tf_op jit(solution)/shard_map/ppermute | solution.py:37
  548.4 10.8 %collective-permute-start.6 = (bf16[144,1024]{1,0:T(8,128)(2,1)}, bf16[144,1024]{1,0:T(8,128)(2,1)}, u32[]{:S(2)}, u32[]{:S(2)}) collective-permute-start(bf16[144,1024]{1,0:T(8,128)(2,1)} %fusion.56), channel_id=1, source_target_pairs={{0,64},{64,128},{128,192},{192,224},{224,160},{160,96},{96,32},{32... | collective-permute-start | bytes 884744 | tf_op jit(solution)/shard_map/ppermute | solution.py:37
  554.6 10.9 %collective-permute-start.13 = (bf16[144,1024]{1,0:T(8,128)(2,1)}, bf16[144,1024]{1,0:T(8,128)(2,1)}, u32[]{:S(2)}, u32[]{:S(2)}) collective-permute-start(bf16[144,1024]{1,0:T(8,128)(2,1)} %fusion.49), channel_id=1, source_target_pairs={{0,64},{64,128},{128,192},{192,224},{224,160},{160,96},{96,32},{32... | collective-permute-start | bytes 884744 | tf_op jit(solution)/shard_map/ppermute | solution.py:37
  (40 other events, 401.8 us)

commit v4 on v3

--- a/solution.py
+++ b/solution.py
@@ -10,35 +10,36 @@
     )
 
 
-def dp_ring(n_dp):
-    half = n_dp // 2
-    return [2 * i for i in range(half)] + [2 * (half - 1 - i) + 1 for i in range(half)]
-
-
-def ring_reduce_scatter(packed, n_dp):
-    ring = dp_ring(n_dp)
-    pos_of = [ring.index(d) for d in range(n_dp)]
-    ring_arr = jnp.array(ring, dtype=jnp.int32)
-    pos = jnp.array(pos_of, dtype=jnp.int32)[lax.axis_index("dp")]
-    k = packed.shape[1] // 2
-    halves = (packed[:, :k], packed[:, k:])
+def dp_reduce_scatter(packed, n_dp):
+    n_y = n_dp // 2
+    _, n_r, lanes = packed.shape
+    me = lax.axis_index("dp")
+    y_pos = me // 2
+    x_lo = me % 2
+    by_y = packed.reshape(n_y, 2, n_r, lanes)
+    half = n_r // 2
+    halves = (by_y[:, :, :half], by_y[:, :, half:])
     steps = (1, -1)
     perms = [
-        [(ring[i], ring[(i + st) % n_dp]) for i in range(n_dp)] for st in steps
+        [(y * 2 + b, ((y + st) % n_y) * 2 + b) for y in range(n_y) for b in range(2)]
+        for st in steps
     ]
 
     def own(h, c):
-        return lax.dynamic_index_in_dim(halves[h], ring_arr[c % n_dp], axis=0, keepdims=False)
+        return lax.dynamic_index_in_dim(halves[h], c % n_y, axis=0, keepdims=False)
 
-    send = [own(h, pos - steps[h]) for h in range(2)]
-    acc = [None, None]
-    for s in range(n_dp - 1):
+    send = [own(h, y_pos - steps[h]) for h in range(2)]
+    for s in range(n_y - 1):
         for h in range(2):
             recv = lax.ppermute(send[h], "dp", perms[h])
-            chunk = pos - steps[h] * (s + 2)
-            acc[h] = recv.astype(jnp.float32) + own(h, chunk).astype(jnp.float32)
-            send[h] = acc[h].astype(jnp.bfloat16)
-    return jnp.concatenate([send[0], send[1]], axis=0)
+            chunk = y_pos - steps[h] * (s + 2)
+            acc = recv.astype(jnp.float32) + own(h, chunk).astype(jnp.float32)
+            send[h] = acc.astype(jnp.bfloat16)
+    both = jnp.concatenate(send, axis=1)
+    keep = lax.dynamic_index_in_dim(both, x_lo, axis=0, keepdims=False)
+    give = lax.dynamic_index_in_dim(both, 1 - x_lo, axis=0, keepdims=False)
+    got = lax.ppermute(give, "dp", [(d, d ^ 1) for d in range(n_dp)])
+    return (keep.astype(jnp.float32) + got.astype(jnp.float32)).astype(jnp.bfloat16)
 
 
 def expert_work(xr, scaled, w_gate, w_up, w_down):
@@ -122,7 +123,7 @@
             ],
             axis=1,
         )
-        reduced.append(ring_reduce_scatter(packed, n_dp).reshape(3, dsl * hid))
+        reduced.append(dp_reduce_scatter(packed, n_dp).reshape(3, dsl * hid))
     stack_g = jnp.stack([r[0].reshape(dsl, hid) for r in reduced], axis=0)
     stack_u = jnp.stack([r[1].reshape(dsl, hid) for r in reduced], axis=0)
     stack_d = jnp.stack([r[2].reshape(hid, dsl) for r in reduced], axis=0)

time: 587 us -> 524 us (0.89)
  between operations: 41.8 us -> 1.75 us
  starting transfers between devices: 60.6 us -> 38.6 us
  other arithmetic: 73.8 us -> 52.7 us
  waiting for transfers between devices: 294 us -> 312 us
  local copies, waits for them, and re-layouts: 48.2 us -> 54.6 us
    convert_element_type x25 -> x12, other arithmetic: 45.9 us -> 23.2 us  [the longest x10 21.6 us: dp_reduce_scatter(): send[h] = acc.astype(jnp.bfloat16)]
    ppermute x28 -> x14, starting transfers between devices: 31.3 us -> 9.25 us  [the longest x12 8.66 us: dp_reduce_scatter(): recv = lax.ppermute(send[h], 'dp', perms[h])]
    concatenate x0 -> x6, local copies, waits for them, and re-layouts: none -> 20.8 us  [per_device(): jnp.concatenate([grad_g.reshape(n_dp, dsl * hid // lanes, lanes), grad_u....]
    reshape x6 -> x0, local copies, waits for them, and re-layouts: 17.3 us -> none  [the longest x2 7.63 us: per_device(): grad_g.reshape(n_dp, dsl * hid // lanes, lanes)]
    all_to_all x2, waiting for transfers between devices: 202 us -> 219 us  [per_device(): lax.all_to_all(send, 'expert', split_axis=0, concat_axis=0, tiled=True)]
    ppermute x28 -> x14, waiting for transfers between devices: 92.3 us -> 92.6 us  [the longest x12 81.3 us: dp_reduce_scatter(): recv = lax.ppermute(send[h], 'dp', perms[h])]
  transfers between devices with their start and end apart: 31 -> 17, of which waited for: 26 -> 12; matrix products, arithmetic and copies ran while one was open for 18% -> 16% of each run, Pallas kernels for 0% -> 0%
where the time goes in v4:
time: 524 us; the launch traced here: 514 us
  waiting for transfers between devices  312 us (60%)
  local copies, waits for them, and re-layouts  54.6 us (10%)
  matrix products  54.5 us (10%)
  other arithmetic  52.7 us (10%)
  starting transfers between devices  38.6 us (7%)
    all_to_all x2, waiting for transfers between devices, per_device(): lax.all_to_all(send, 'expert', split_axis=0, concat_axis=0, tiled=True)  219 us
    ppermute x12, waiting for transfers between devices, dp_reduce_scatter(): recv = lax.ppermute(send[h], 'dp', perms[h])  81.3 us
    dot_general x22, matrix products, contract(): lax.dot_general(left, right, ((left_dims, right_dims), ((), ())), preferr...  54.5 us
    convert_element_type x10, other arithmetic, dp_reduce_scatter(): send[h] = acc.astype(jnp.bfloat16)  21.6 us
    all_to_all x2, starting transfers between devices, per_device(): lax.all_to_all(send, 'expert', split_axis=0, concat_axis=0, tiled=True)  21 us
    concatenate x6, local copies, waits for them, and re-layouts, per_device(): jnp.concatenate([grad_g.reshape(n_dp, dsl * hid // lanes, lanes), grad_u....  20.8 us
    slice x2, local copies, waits for them, and re-layouts, per_device(): scaled = recv[:, slots:]  12.7 us
    ppermute x2, waiting for transfers between devices, dp_reduce_scatter(): got = lax.ppermute(give, 'dp', [(d, d ^ 1) for d in range(n_dp)])  11.4 us
  transfers between devices with their start and end apart: 17, of which 12 were waited for; matrix products, arithmetic and copies ran while one was open for 16% of the time, Pallas kernels for 0%

profile of v4, /device:TPU:1, one launch (start us, length us, event | category | flops | bytes accessed | tf_op | source)
XLA Modules:
  0.0 513.8 jit_solution(6568757644352625598)
XLA Ops:
  3.9 4.2 fusion
  8.3 9.3 %select_reduce_fusion = f32[1152]{0:T(1024)S(1)} fusion(f32[128,8]{0,1:T(8,128)} %param.10, s32[128,8]{0,1:T(8,128)S(1)} %add_add_fusion), kind=kLoop, calls=%fused_computation.7 | loop fusion | flops 3537792 | bytes 12800 | tf_op jit(solution)/shard_map/reduce_sum | solution.py:87
  19.9 5.0 copy.55
  24.8 13.0 %all-to-all-start = ((bf16[32,36,2048]{2,1,0:T(8,128)(2,1)}), bf16[32,36,2048]{2,1,0:T(8,128)(2,1)}, u32[]{:S(2)}, u32[]{:S(2)}) async-start(bf16[32,36,2048]{2,1,0:T(8,128)(2,1)} %copy.55), calls=%async_computation | async-start | bytes 10485760 | tf_op jit(solution)/shard_map/all_to_all | solution.py:99
  39.9 4.9 copy.62
  44.7 111.5 %all-to-all-done = bf16[32,36,2048]{2,1,0:T(8,128)(2,1)} async-done(((bf16[32,36,2048]{2,1,0:T(8,128)(2,1)}), bf16[32,36,2048]{2,1,0:T(8,128)(2,1)}, u32[]{:S(2)}, u32[]{:S(2)}) %all-to-all-start) | async-done | bytes 4718624 | tf_op jit(solution)/shard_map/all_to_all | solution.py:99
  156.2 8.0 %all-to-all-start.1 = ((bf16[32,36,2048]{2,1,0:T(8,128)(2,1)}), bf16[32,36,2048]{2,1,0:T(8,128)(2,1)}, u32[]{:S(2)}, u32[]{:S(2)}) async-start(bf16[32,36,2048]{2,1,0:T(8,128)(2,1)} %copy.62), calls=%async_computation.1 | async-start | bytes 10485760 | tf_op jit(solution)/shard_map/all_to_all | solution.py:99
  164.3 6.4 %fusion.110 = (bf16[32,18,2048]{2,1,0:T(8,128)(2,1)}, bf16[32,18,2048]{2,1,0:T(8,128)(2,1)S(1)}) fusion(bf16[32,36,2048]{2,1,0:T(8,128)(2,1)} %all-to-all-done), kind=kLoop, calls=%fused_computation.202 | loop fusion | bytes 9437184 | tf_op jit(solution)/shard_map/slice | solution.py:101
  175.2 107.5 %all-to-all-done.1 = bf16[32,36,2048]{2,1,0:T(8,128)(2,1)} async-done(((bf16[32,36,2048]{2,1,0:T(8,128)(2,1)}), bf16[32,36,2048]{2,1,0:T(8,128)(2,1)}, u32[]{:S(2)}, u32[]{:S(2)}) %all-to-all-start.1) | async-done | bytes 4718624 | tf_op jit(solution)/shard_map/all_to_all | solution.py:99
  282.7 6.3 %fusion.111 = (bf16[32,18,2048]{2,1,0:T(8,128)(2,1)}, bf16[32,18,2048]{2,1,0:T(8,128)(2,1)S(1)}) fusion(bf16[32,36,2048]{2,1,0:T(8,128)(2,1)} %all-to-all-done.1), kind=kLoop, calls=%fused_computation.203 | loop fusion | bytes 9437184 | tf_op jit(solution)/shard_map/slice | solution.py:101
  297.5 3.8 bitcast_convert_fusion.5
  301.3 4.5 fusion.16
  310.0 3.7 concatenate.46
  313.8 5.8 %add_convert_fusion.1 = bf16[32,18,2048]{2,1,0:T(8,128)(2,1)S(1)} fusion(f32[32,18,2048]{2,1,0:T(8,128)} %fusion.16, bf16[2,2048,384]{2,1,0:T(8,128)(2,1)} %param.12, bf16[32,18,384]{2,0,1:T(8,128)(2,1)} %copy-done.34), kind=kOutput, calls=%fused_computation.1 | convolution fusion | flops 908328960 | bytes 10665984 | tf_op jit(solution)/shard_map/dot_general | solution.py:8
  326.0 4.0 pad_maximum_fusion
  330.0 8.4 %all-to-all-start.2 = ((bf16[32,36,2048]{2,1,0:T(8,128)(2,1)}), bf16[32,36,2048]{2,1,0:T(8,128)(2,1)}, u32[]{:S(2)}, u32[]{:S(2)}) async-start(bf16[32,36,2048]{2,1,0:T(8,128)(2,1)} %pad_maximum_fusion), calls=%async_computation.2 | async-start | bytes 10485760 | tf_op jit(solution)/shard_map/all_to_all | solution.py:108
  338.4 4.7 bitcast_convert_fusion.3
  345.2 3.7 concatenate.49
  354.0 3.6 bitcast_convert_fusion.1
  364.5 3.5 concatenate.53
  368.0 4.3 concatenate.52
  375.7 3.7 concatenate.55
  384.6 11.8 %collective-permute-done.10 = bf16[2,144,1024]{2,1,0:T(8,128)(2,1)} collective-permute-done((bf16[2,144,1024]{2,1,0:T(8,128)(2,1)}, bf16[2,144,1024]{2,1,0:T(8,128)(2,1)}, u32[]{:S(2)}, u32[]{:S(2)}) %collective-permute-start.10) | collective-permute-done | bytes 589856 | tf_op jit(solution)/shard_map/ppermute | solution.py:34
  400.2 8.8 %collective-permute-done.4 = bf16[2,144,1024]{2,1,0:T(8,128)(2,1)} collective-permute-done((bf16[2,144,1024]{2,1,0:T(8,128)(2,1)}, bf16[2,144,1024]{2,1,0:T(8,128)(2,1)}, u32[]{:S(2)}, u32[]{:S(2)}) %collective-permute-start.4) | collective-permute-done | bytes 589856 | tf_op jit(solution)/shard_map/ppermute | solution.py:34
  413.0 8.7 %collective-permute-done.11 = bf16[2,144,1024]{2,1,0:T(8,128)(2,1)} collective-permute-done((bf16[2,144,1024]{2,1,0:T(8,128)(2,1)}, bf16[2,144,1024]{2,1,0:T(8,128)(2,1)}, u32[]{:S(2)}, u32[]{:S(2)}) %collective-permute-start.11) | collective-permute-done | bytes 589856 | tf_op jit(solution)/shard_map/ppermute | solution.py:34
  425.5 8.8 %collective-permute-done.5 = bf16[2,144,1024]{2,1,0:T(8,128)(2,1)} collective-permute-done((bf16[2,144,1024]{2,1,0:T(8,128)(2,1)}, bf16[2,144,1024]{2,1,0:T(8,128)(2,1)}, u32[]{:S(2)}, u32[]{:S(2)}) %collective-permute-start.5) | collective-permute-done | bytes 589856 | tf_op jit(solution)/shard_map/ppermute | solution.py:34
  437.4 9.6 %collective-permute-done.12 = bf16[2,144,1024]{2,1,0:T(8,128)(2,1)} collective-permute-done((bf16[2,144,1024]{2,1,0:T(8,128)(2,1)}, bf16[2,144,1024]{2,1,0:T(8,128)(2,1)}, u32[]{:S(2)}, u32[]{:S(2)}) %collective-permute-start.12) | collective-permute-done | bytes 589856 | tf_op jit(solution)/shard_map/ppermute | solution.py:34
  453.9 11.3 %collective-permute-done.8 = bf16[2,144,1024]{2,1,0:T(8,128)(2,1)} collective-permute-done((bf16[2,144,1024]{2,1,0:T(8,128)(2,1)}, bf16[2,144,1024]{2,1,0:T(8,128)(2,1)}, u32[]{:S(2)}, u32[]{:S(2)}) %collective-permute-start.8) | collective-permute-done | bytes 589856 | tf_op jit(solution)/shard_map/ppermute | solution.py:34
  467.3 10.5 %collective-permute-done.2 = bf16[2,144,1024]{2,1,0:T(8,128)(2,1)} collective-permute-done((bf16[2,144,1024]{2,1,0:T(8,128)(2,1)}, bf16[2,144,1024]{2,1,0:T(8,128)(2,1)}, u32[]{:S(2)}, u32[]{:S(2)}) %collective-permute-start.2) | collective-permute-done | bytes 589856 | tf_op jit(solution)/shard_map/ppermute | solution.py:34
  480.5 10.0 %collective-permute-done.9 = bf16[2,144,1024]{2,1,0:T(8,128)(2,1)} collective-permute-done((bf16[2,144,1024]{2,1,0:T(8,128)(2,1)}, bf16[2,144,1024]{2,1,0:T(8,128)(2,1)}, u32[]{:S(2)}, u32[]{:S(2)}) %collective-permute-start.9) | collective-permute-done | bytes 589856 | tf_op jit(solution)/shard_map/ppermute | solution.py:34
  494.6 11.4 %collective-permute-done.13 = bf16[288,1024]{1,0:T(8,128)(2,1)S(1)} collective-permute-done((bf16[288,1024]{1,0:T(8,128)(2,1)}, bf16[288,1024]{1,0:T(8,128)(2,1)S(1)}, u32[]{:S(2)}, u32[]{:S(2)}) %collective-permute-start.13) | collective-permute-done | bytes 589856 | tf_op jit(solution)/shard_map/ppermute | solution.py:41
  509.2 4.2 fusion.1
  (167 shorter events, 87.0 us)
Async XLA Ops:
  0.6 17.3 %copy-start = (bf16[128,2048]{1,0:T(8,128)(2,1)S(1)}, bf16[128,2048]{1,0:T(8,128)(2,1)}, u32[]{:S(2)}) copy-start(bf16[128,2048]{1,0:T(8,128)(2,1)} %param.7) | copy-start | bytes 1572868
  0.6 18.0 %copy-start.27 = (bf16[128,2048]{1,0:T(8,128)(2,1)S(1)}, bf16[128,2048]{1,0:T(8,128)(2,1)}, u32[]{:S(2)}) copy-start(bf16[128,2048]{1,0:T(8,128)(2,1)} %param.8) | copy-start | bytes 1572868
  24.8 131.4 %all-to-all-start = ((bf16[32,36,2048]{2,1,0:T(8,128)(2,1)}), bf16[32,36,2048]{2,1,0:T(8,128)(2,1)}, u32[]{:S(2)}, u32[]{:S(2)}) async-start(bf16[32,36,2048]{2,1,0:T(8,128)(2,1)} %copy.55), calls=%async_computation | async-start | bytes 10485760 | tf_op jit(solution)/shard_map/all_to_all | solution.py:99
  156.2 126.5 %all-to-all-start.1 = ((bf16[32,36,2048]{2,1,0:T(8,128)(2,1)}), bf16[32,36,2048]{2,1,0:T(8,128)(2,1)}, u32[]{:S(2)}, u32[]{:S(2)}) async-start(bf16[32,36,2048]{2,1,0:T(8,128)(2,1)} %copy.62), calls=%async_computation.1 | async-start | bytes 10485760 | tf_op jit(solution)/shard_map/all_to_all | solution.py:99
  173.7 121.2 %copy-start.41 = (f32[32,18,384]{2,0,1:T(8,128)}, f32[32,18,384]{2,0,1:T(8,128)S(1)}, u32[]{:S(2)}) copy-start(f32[32,18,384]{2,0,1:T(8,128)S(1)} %fusion.18) | copy-start | bytes 2654212
  175.2 119.7 %copy-start.42 = (f32[32,18,384]{2,0,1:T(8,128)}, f32[32,18,384]{2,0,1:T(8,128)S(1)}, u32[]{:S(2)}) copy-start(f32[32,18,384]{2,0,1:T(8,128)S(1)} %fusion.21) | copy-start | bytes 2654212
  313.7 35.2 %copy-start.2 = (bf16[4,2,96,1024]{3,2,1,0:T(8,128)(2,1)}, bf16[4,2,96,1024]{3,2,1,0:T(8,128)(2,1)S(1)}, u32[]{:S(2)}) copy-start(bf16[4,2,96,1024]{3,2,1,0:T(8,128)(2,1)S(1)} %concatenate.46) | copy-start | bytes 4718596
  330.0 179.1 %all-to-all-start.2 = ((bf16[32,36,2048]{2,1,0:T(8,128)(2,1)}), bf16[32,36,2048]{2,1,0:T(8,128)(2,1)}, u32[]{:S(2)}, u32[]{:S(2)}) async-start(bf16[32,36,2048]{2,1,0:T(8,128)(2,1)} %pad_maximum_fusion), calls=%async_computation.2 | async-start | bytes 10485760 | tf_op jit(solution)/shard_map/all_to_all | solution.py:108
  351.2 30.9 %collective-permute-start.3 = (bf16[2,144,1024]{2,1,0:T(8,128)(2,1)}, bf16[2,144,1024]{2,1,0:T(8,128)(2,1)}, u32[]{:S(2)}, u32[]{:S(2)}) collective-permute-start(bf16[2,144,1024]{2,1,0:T(8,128)(2,1)} %get-tuple-element.14), channel_id=1, source_target_pairs={{0,192},{32,224},{64,0},{96,32},{128,64},{160,96},{192,128},{224,1... | collective-permute-start | bytes 1769480 | tf_op jit(solution)/shard_map/ppermute | solution.py:34
  381.6 14.8 %collective-permute-start.10 = (bf16[2,144,1024]{2,1,0:T(8,128)(2,1)}, bf16[2,144,1024]{2,1,0:T(8,128)(2,1)}, u32[]{:S(2)}, u32[]{:S(2)}) collective-permute-start(bf16[2,144,1024]{2,1,0:T(8,128)(2,1)} %get-tuple-element.18), channel_id=1, source_target_pairs={{0,192},{32,224},{64,0},{96,32},{128,64},{160,96},{192,128},{224,1... | collective-permute-start | bytes 1769480 | tf_op jit(solution)/shard_map/ppermute | solution.py:34
  382.1 14.3 %copy-start.6 = (bf16[4,2,96,1024]{3,2,1,0:T(8,128)(2,1)S(1)}, bf16[4,2,96,1024]{3,2,1,0:T(8,128)(2,1)}, u32[]{:S(2)}) copy-start(bf16[4,2,96,1024]{3,2,1,0:T(8,128)(2,1)} %concatenate.55) | copy-start | bytes 4718596
  384.4 24.6 %collective-permute-start.4 = (bf16[2,144,1024]{2,1,0:T(8,128)(2,1)}, bf16[2,144,1024]{2,1,0:T(8,128)(2,1)}, u32[]{:S(2)}, u32[]{:S(2)}) collective-permute-start(bf16[2,144,1024]{2,1,0:T(8,128)(2,1)} %fusion.44), channel_id=1, source_target_pairs={{0,192},{32,224},{64,0},{96,32},{128,64},{160,96},{192,128},{224,1... | collective-permute-start | bytes 1769480 | tf_op jit(solution)/shard_map/ppermute | solution.py:34
  398.6 23.2 %collective-permute-start.11 = (bf16[2,144,1024]{2,1,0:T(8,128)(2,1)}, bf16[2,144,1024]{2,1,0:T(8,128)(2,1)}, u32[]{:S(2)}, u32[]{:S(2)}) collective-permute-start(bf16[2,144,1024]{2,1,0:T(8,128)(2,1)} %fusion.37), channel_id=1, source_target_pairs={{0,192},{32,224},{64,0},{96,32},{128,64},{160,96},{192,128},{224,1... | collective-permute-start | bytes 1769480 | tf_op jit(solution)/shard_map/ppermute | solution.py:34
  400.2 21.5 %copy-start.7 = (bf16[4,2,96,1024]{3,2,1,0:T(8,128)(2,1)S(1)}, bf16[4,2,96,1024]{3,2,1,0:T(8,128)(2,1)}, u32[]{:S(2)}) copy-start(bf16[4,2,96,1024]{3,2,1,0:T(8,128)(2,1)} %concatenate.55) | copy-start | bytes 4718596
  400.2 25.3 %collective-permute-start = (bf16[2,144,1024]{2,1,0:T(8,128)(2,1)}, bf16[2,144,1024]{2,1,0:T(8,128)(2,1)}, u32[]{:S(2)}, u32[]{:S(2)}) collective-permute-start(bf16[2,144,1024]{2,1,0:T(8,128)(2,1)} %get-tuple-element.15), channel_id=1, source_target_pairs={{0,64},{32,96},{64,128},{96,160},{128,192},{160,224},{192,0},{224,... | collective-permute-start | bytes 1769480 | tf_op jit(solution)/shard_map/ppermute | solution.py:34
  411.3 23.1 %collective-permute-start.5 = (bf16[2,144,1024]{2,1,0:T(8,128)(2,1)}, bf16[2,144,1024]{2,1,0:T(8,128)(2,1)}, u32[]{:S(2)}, u32[]{:S(2)}) collective-permute-start(bf16[2,144,1024]{2,1,0:T(8,128)(2,1)} %fusion.43), channel_id=1, source_target_pairs={{0,192},{32,224},{64,0},{96,32},{128,64},{160,96},{192,128},{224,1... | collective-permute-start | bytes 1769480 | tf_op jit(solution)/shard_map/ppermute | solution.py:34
  413.0 24.4 %collective-permute-start.7 = (bf16[2,144,1024]{2,1,0:T(8,128)(2,1)}, bf16[2,144,1024]{2,1,0:T(8,128)(2,1)}, u32[]{:S(2)}, u32[]{:S(2)}) collective-permute-start(bf16[2,144,1024]{2,1,0:T(8,128)(2,1)} %get-tuple-element.19), channel_id=1, source_target_pairs={{0,64},{32,96},{64,128},{96,160},{128,192},{160,224},{192,0},{224,... | collective-permute-start | bytes 1769480 | tf_op jit(solution)/shard_map/ppermute | solution.py:34
  423.8 23.2 %collective-permute-start.12 = (bf16[2,144,1024]{2,1,0:T(8,128)(2,1)}, bf16[2,144,1024]{2,1,0:T(8,128)(2,1)}, u32[]{:S(2)}, u32[]{:S(2)}) collective-permute-start(bf16[2,144,1024]{2,1,0:T(8,128)(2,1)} %fusion.36), channel_id=1, source_target_pairs={{0,192},{32,224},{64,0},{96,32},{128,64},{160,96},{192,128},{224,1... | collective-permute-start | bytes 1769480 | tf_op jit(solution)/shard_map/ppermute | solution.py:34
  425.5 21.5 %copy-start.3 = (bf16[4,2,96,1024]{3,2,1,0:T(8,128)(2,1)S(1)}, bf16[4,2,96,1024]{3,2,1,0:T(8,128)(2,1)}, u32[]{:S(2)}) copy-start(bf16[4,2,96,1024]{3,2,1,0:T(8,128)(2,1)} %concatenate.52) | copy-start | bytes 4718596
  425.5 21.5 %copy-start.8 = (bf16[4,2,96,1024]{3,2,1,0:T(8,128)(2,1)S(1)}, bf16[4,2,96,1024]{3,2,1,0:T(8,128)(2,1)}, u32[]{:S(2)}) copy-start(bf16[4,2,96,1024]{3,2,1,0:T(8,128)(2,1)} %concatenate.55) | copy-start | bytes 4718596
  437.4 14.3 %collective-permute-start.1 = (bf16[2,144,1024]{2,1,0:T(8,128)(2,1)}, bf16[2,144,1024]{2,1,0:T(8,128)(2,1)}, u32[]{:S(2)}, u32[]{:S(2)}) collective-permute-start(bf16[2,144,1024]{2,1,0:T(8,128)(2,1)} %get-tuple-element.13), channel_id=1, source_target_pairs={{0,64},{32,96},{64,128},{96,160},{128,192},{160,224},{192,0},{224,... | collective-permute-start | bytes 1769480 | tf_op jit(solution)/shard_map/ppermute | solution.py:34
  449.8 15.4 %collective-permute-start.8 = (bf16[2,144,1024]{2,1,0:T(8,128)(2,1)}, bf16[2,144,1024]{2,1,0:T(8,128)(2,1)}, u32[]{:S(2)}, u32[]{:S(2)}) collective-permute-start(bf16[2,144,1024]{2,1,0:T(8,128)(2,1)} %get-tuple-element.17), channel_id=1, source_target_pairs={{0,64},{32,96},{64,128},{96,160},{128,192},{160,224},{192,0},{224,... | collective-permute-start | bytes 1769480 | tf_op jit(solution)/shard_map/ppermute | solution.py:34
  450.0 15.1 %copy-start.4 = (bf16[4,2,96,1024]{3,2,1,0:T(8,128)(2,1)S(1)}, bf16[4,2,96,1024]{3,2,1,0:T(8,128)(2,1)}, u32[]{:S(2)}) copy-start(bf16[4,2,96,1024]{3,2,1,0:T(8,128)(2,1)} %concatenate.52) | copy-start | bytes 4718596
  453.9 23.9 %collective-permute-start.2 = (bf16[2,144,1024]{2,1,0:T(8,128)(2,1)}, bf16[2,144,1024]{2,1,0:T(8,128)(2,1)}, u32[]{:S(2)}, u32[]{:S(2)}) collective-permute-start(bf16[2,144,1024]{2,1,0:T(8,128)(2,1)} %fusion.46), channel_id=1, source_target_pairs={{0,64},{32,96},{64,128},{96,160},{128,192},{160,224},{192,0},{224,... | collective-permute-start | bytes 1769480 | tf_op jit(solution)/shard_map/ppermute | solution.py:34
  467.3 23.1 %collective-permute-start.9 = (bf16[2,144,1024]{2,1,0:T(8,128)(2,1)}, bf16[2,144,1024]{2,1,0:T(8,128)(2,1)}, u32[]{:S(2)}, u32[]{:S(2)}) collective-permute-start(bf16[2,144,1024]{2,1,0:T(8,128)(2,1)} %fusion.39), channel_id=1, source_target_pairs={{0,64},{32,96},{64,128},{96,160},{128,192},{160,224},{192,0},{224,... | collective-permute-start | bytes 1769480 | tf_op jit(solution)/shard_map/ppermute | solution.py:34
  467.3 11.9 %copy-start.11 = (bf16[2,144,1024]{2,1,0:T(8,128)(2,1)S(1)}, bf16[2,144,1024]{2,1,0:T(8,128)(2,1)}, u32[]{:S(2)}) copy-start(bf16[2,144,1024]{2,1,0:T(8,128)(2,1)} %get-tuple-element.12) | copy-start | bytes 1769476
  467.3 23.1 %copy-start.5 = (bf16[4,2,96,1024]{3,2,1,0:T(8,128)(2,1)S(1)}, bf16[4,2,96,1024]{3,2,1,0:T(8,128)(2,1)}, u32[]{:S(2)}) copy-start(bf16[4,2,96,1024]{3,2,1,0:T(8,128)(2,1)} %concatenate.52) | copy-start | bytes 4718596
  479.2 12.5 %copy-start.9 = (bf16[2,144,1024]{2,1,0:T(8,128)(2,1)}, bf16[2,144,1024]{2,1,0:T(8,128)(2,1)S(1)}, u32[]{:S(2)}) copy-start(bf16[2,144,1024]{2,1,0:T(8,128)(2,1)S(1)} %fusion.45) | copy-start | bytes 1769476
  480.2 12.8 %copy-start.29 = (pred[1152,128]{1,0:T(8,128)(4,1)S(1)}, pred[1152,128]{1,0:T(8,128)(4,1)}, u32[]{:S(2)}) copy-start(pred[1152,128]{1,0:T(8,128)(4,1)} %copy-done.28) | copy-start | bytes 442372
  480.2 12.9 %collective-permute-start.6 = (bf16[288,1024]{1,0:T(8,128)(2,1)}, bf16[288,1024]{1,0:T(8,128)(2,1)}, u32[]{:S(2)}, u32[]{:S(2)}) collective-permute-start(bf16[288,1024]{1,0:T(8,128)(2,1)} %fusion.53), channel_id=1, source_target_pairs={{0,32},{32,0},{64,96},{96,64},{128,160},{160,128},{192,224},{224,1... | collective-permute-start | bytes 1769480 | tf_op jit(solution)/shard_map/ppermute | solution.py:41
  492.7 13.3 %copy-start.13 = (bf16[2,144,1024]{2,1,0:T(8,128)(2,1)S(1)}, bf16[2,144,1024]{2,1,0:T(8,128)(2,1)}, u32[]{:S(2)}) copy-start(bf16[2,144,1024]{2,1,0:T(8,128)(2,1)} %get-tuple-element.16) | copy-start | bytes 1769476
  492.7 13.3 %collective-permute-start.13 = (bf16[288,1024]{1,0:T(8,128)(2,1)}, bf16[288,1024]{1,0:T(8,128)(2,1)S(1)}, u32[]{:S(2)}, u32[]{:S(2)}) collective-permute-start(bf16[288,1024]{1,0:T(8,128)(2,1)} %fusion.49), channel_id=1, source_target_pairs={{0,32},{32,0},{64,96},{96,64},{128,160},{160,128},{192,224},{224,1... | collective-permute-start | bytes 1769480 | tf_op jit(solution)/shard_map/ppermute | solution.py:41
  (28 other events, 132.8 us)

commit v5 on v4

--- a/solution.py
+++ b/solution.py
@@ -71,37 +71,40 @@
 
     columns = jnp.arange(experts, dtype=jnp.int32)
     onehot = expert_ids[:, :, None] == columns[None, None, :]
-    per_tok = jnp.sum(onehot.astype(jnp.float32), axis=1).astype(jnp.bfloat16)
+    member = jnp.any(onehot, axis=1)
     t_ids = jnp.arange(tok_dev, dtype=jnp.int32)
     lower = (t_ids[None, :] < t_ids[:, None]).astype(jnp.bfloat16)
-    before = contract(lower, per_tok, (1,), (0,))
-    rank_prev = jnp.sum(jnp.where(onehot, before[:, None, :], 0.0), axis=2).astype(jnp.int32)
-    k_ids = jnp.arange(top_k, dtype=jnp.int32)
-    same = (expert_ids[:, :, None] == expert_ids[:, None, :]) & (k_ids[None, None, :] < k_ids[None, :, None])
-    rank = rank_prev + jnp.sum(same.astype(jnp.int32), axis=2)
-    dest = expert_ids * slots + rank
+    before = contract(member.astype(jnp.bfloat16), lower, (0,), (1,)).astype(jnp.int32)
+    p_tok = jnp.sum(jnp.where(onehot, route_probs[:, :, None], 0.0), axis=1).T
 
-    s_ids = jnp.arange(n_slot, dtype=jnp.int32)
-    hit = s_ids[:, None, None] == dest[None, :, :]
-    sel = jnp.any(hit, axis=2).astype(jnp.bfloat16)
-    p_slot = jnp.sum(jnp.where(hit, route_probs[None, :, :], 0.0), axis=(1, 2))
-    sel = sel.reshape(n_owner, exp_dev, slots, tok_dev)
+    r_ids = jnp.arange(slots, dtype=jnp.int32)
+    hit = member.T[:, None, :] & (before[:, None, :] == r_ids[None, :, None])
+    p_slot = jnp.sum(jnp.where(hit, p_tok[:, None, :], 0.0), axis=2)
+    sel = hit.astype(jnp.bfloat16).reshape(n_owner, exp_dev, slots, tok_dev)
     p_slot = p_slot.reshape(n_owner, exp_dev, slots)
+    both_in = jnp.concatenate([tokens, out_grad], axis=0)
+    zeros = jnp.zeros_like(sel[:, 0])
+    ones = jnp.ones((n_owner, slots), jnp.float32)
 
     contribs = []
     grads = []
+    after = None
     for local in range(exp_dev):
         sel_l = sel[:, local]
-        send_x = contract(sel_l, tokens, (2,), (0,)).astype(jnp.bfloat16)
-        dy_rows = contract(sel_l, out_grad, (2,), (0,))
-        send_dy = (p_slot[:, local][:, :, None] * dy_rows).astype(jnp.bfloat16)
-        send = jnp.concatenate([send_x, send_dy], axis=1)
+        pick = jnp.concatenate(
+            [jnp.concatenate([sel_l, zeros], axis=2), jnp.concatenate([zeros, sel_l], axis=2)], axis=1
+        )
+        scale = jnp.concatenate([ones, p_slot[:, local]], axis=1)
+        send = (scale[:, :, None] * contract(pick, both_in, (2,), (0,))).astype(jnp.bfloat16)
         recv = lax.all_to_all(send, "expert", split_axis=0, concat_axis=0, tiled=True)
+        if after is not None:
+            recv, _ = lax.optimization_barrier((recv, after))
         xr = recv[:, :slots]
         scaled = recv[:, slots:]
         contrib, grad_g, grad_u, grad_d = expert_work(
             xr, scaled, gate_weight[local], up_weight[local], down_weight[local]
         )
+        after = contrib
         contribs.append(contrib)
         grads.append((grad_g, grad_u, grad_d))
 

time: 524 us -> 493 us (0.941)
  local copies, waits for them, and re-layouts: 54.6 us -> 32.4 us
  other arithmetic: 52.7 us -> 34.7 us
  matrix products: 54.5 us -> 70.8 us
    dot_general x22 -> x20, matrix products: 54.5 us -> 70.8 us  [contract(): lax.dot_general(left, right, ((left_dims, right_dims), ((), ())), preferr...]
    slice x4 -> x1, local copies, waits for them, and re-layouts: 12.8 us -> 0.03 us  [per_device(): scale = jnp.concatenate([ones, p_slot[:, local]], axis=1)]
    reduce_sum x4 -> x2, other arithmetic: 11.7 us -> 1.05 us  [the longest x1 0.74 us: per_device(): p_tok = jnp.sum(jnp.where(onehot, route_probs[:, :, None], 0.0), axis=1).T]
  transfers between devices with their start and end apart: 17 -> 17, of which waited for: 12 -> 12; matrix products, arithmetic and copies ran while one was open for 16% -> 20% of each run, Pallas kernels for 0% -> 0%
where the time goes in v5:
time: 493 us; the launch traced here: 487 us
  waiting for transfers between devices  309 us (63%)
  matrix products  70.8 us (14%)
  starting transfers between devices  38.9 us (8%)
  other arithmetic  34.7 us (7%)
  local copies, waits for them, and re-layouts  32.4 us (7%)
    all_to_all x2, waiting for transfers between devices, per_device(): lax.all_to_all(send, 'expert', split_axis=0, concat_axis=0, tiled=True)  216 us
    ppermute x12, waiting for transfers between devices, dp_reduce_scatter(): recv = lax.ppermute(send[h], 'dp', perms[h])  81.6 us
    dot_general x20, matrix products, contract(): lax.dot_general(left, right, ((left_dims, right_dims), ((), ())), preferr...  70.8 us
    convert_element_type x10, other arithmetic, dp_reduce_scatter(): send[h] = acc.astype(jnp.bfloat16)  21.6 us
    all_to_all x2, starting transfers between devices, per_device(): lax.all_to_all(send, 'expert', split_axis=0, concat_axis=0, tiled=True)  20.8 us
    concatenate x6, local copies, waits for them, and re-layouts, per_device(): jnp.concatenate([grad_g.reshape(n_dp, dsl * hid // lanes, lanes), grad_u....  18.8 us
    ppermute x2, waiting for transfers between devices, dp_reduce_scatter(): got = lax.ppermute(give, 'dp', [(d, d ^ 1) for d in range(n_dp)])  10.4 us
  transfers between devices with their start and end apart: 17, of which 12 were waited for; matrix products, arithmetic and copies ran while one was open for 20% of the time, Pallas kernels for 0%

profile of v5, /device:TPU:1, one launch (start us, length us, event | category | flops | bytes accessed | tf_op | source)
XLA Modules:
  0.0 487.1 jit_solution(14634623774535503268)
XLA Ops:
  3.1 4.0 multiply_convert_fusion.1
  7.1 12.6 %all-to-all-start = ((bf16[32,36,2048]{2,1,0:T(8,128)(2,1)}), bf16[32,36,2048]{2,1,0:T(8,128)(2,1)}, u32[]{:S(2)}, u32[]{:S(2)}) async-start(bf16[32,36,2048]{2,1,0:T(8,128)(2,1)} %multiply_convert_fusion.1), calls=%async_computation | async-start | bytes 10485760 | tf_op jit(solution)/shard_map/all_to_all | solution.py:99
  19.8 3.9 multiply_convert_fusion
  23.7 114.5 %all-to-all-done = bf16[32,36,2048]{2,1,0:T(8,128)(2,1)} async-done(((bf16[32,36,2048]{2,1,0:T(8,128)(2,1)}), bf16[32,36,2048]{2,1,0:T(8,128)(2,1)}, u32[]{:S(2)}, u32[]{:S(2)}) %all-to-all-start) | async-done | bytes 4718624 | tf_op jit(solution)/shard_map/all_to_all | solution.py:99
  138.2 8.2 %all-to-all-start.1 = ((bf16[32,36,2048]{2,1,0:T(8,128)(2,1)}), bf16[32,36,2048]{2,1,0:T(8,128)(2,1)}, u32[]{:S(2)}, u32[]{:S(2)}) async-start(bf16[32,36,2048]{2,1,0:T(8,128)(2,1)} %multiply_convert_fusion), calls=%async_computation.1 | async-start | bytes 10485760 | tf_op jit(solution)/shard_map/all_to_all | solution.py:99
  146.5 3.9 fusion.11
  150.4 4.2 fusion.9
  154.6 4.4 multiply_convert_fusion.6
  162.8 101.9 %all-to-all-done.1 = bf16[32,36,2048]{2,1,0:T(8,128)(2,1)} async-done(((bf16[32,36,2048]{2,1,0:T(8,128)(2,1)}), bf16[32,36,2048]{2,1,0:T(8,128)(2,1)}, u32[]{:S(2)}, u32[]{:S(2)}) %all-to-all-start.1) | async-done | bytes 4718624 | tf_op jit(solution)/shard_map/all_to_all | solution.py:99
  264.8 4.3 fusion.15
  269.1 4.2 fusion.17
  273.3 4.5 multiply_convert_fusion.4
  277.9 5.4 %bitcast_convert_fusion.2 = bf16[2048,384]{1,0:T(8,128)(2,1)} fusion(bf16[32,18,384]{2,1,0:T(8,128)(2,1)S(1)} %get-tuple-element.7, bf16[32,36,2048]{2,1,0:T(8,128)(2,1)} %all-to-all-done.1), kind=kOutput, calls=%fused_computation.7 | convolution fusion | flops 906756096 | bytes 5160960 | tf_op jit(solution)/shard_map/dot_general | solution.py:8
  286.6 5.0 %copy.69 = bf16[32,36,2048]{2,1,0:T(8,128)(2,1)} copy(bf16[32,36,2048]{2,0,1:T(8,128)(2,1)S(1)} %pad_maximum_fusion) | data formatting | bytes 9437184 | tf_op jit(solution)/shard_map/concatenate | solution.py:112
  291.7 8.7 %all-to-all-start.2 = ((bf16[32,36,2048]{2,1,0:T(8,128)(2,1)}), bf16[32,36,2048]{2,1,0:T(8,128)(2,1)}, u32[]{:S(2)}, u32[]{:S(2)}) async-start(bf16[32,36,2048]{2,1,0:T(8,128)(2,1)} %copy.69), calls=%async_computation.2 | async-start | bytes 10485760 | tf_op jit(solution)/shard_map/all_to_all | solution.py:111
  300.4 3.9 bitcast_convert_fusion.4
  304.4 4.7 bitcast_convert_fusion.3
  309.1 5.0 %bitcast_convert_fusion.5 = bf16[2048,384]{1,0:T(8,128)(2,1)} fusion(bf16[32,18,384]{2,1,0:T(8,128)(2,1)S(1)} %copy-done.22, bf16[32,36,2048]{2,1,0:T(8,128)(2,1)} %all-to-all-done), kind=kOutput, calls=%fused_computation.10 | convolution fusion | flops 906756096 | bytes 5160960 | tf_op jit(solution)/shard_map/dot_general | solution.py:8
  323.1 3.7 concatenate.77
  332.1 3.5 bitcast_convert_fusion
  335.6 4.9 %bitcast_convert_fusion.1 = bf16[2048,384]{1,0:T(8,128)(2,1)} fusion(bf16[32,18,384]{2,1,0:T(8,128)(2,1)S(1)} %copy-done.24, bf16[32,36,2048]{2,1,0:T(8,128)(2,1)} %all-to-all-done.1), kind=kOutput, calls=%fused_computation.6 | convolution fusion | flops 906756096 | bytes 5160960 | tf_op jit(solution)/shard_map/dot_general | solution.py:8
  343.6 4.3 concatenate.80
  356.4 11.9 %collective-permute-done.10 = bf16[2,144,1024]{2,1,0:T(8,128)(2,1)} collective-permute-done((bf16[2,144,1024]{2,1,0:T(8,128)(2,1)}, bf16[2,144,1024]{2,1,0:T(8,128)(2,1)}, u32[]{:S(2)}, u32[]{:S(2)}) %collective-permute-start.10) | collective-permute-done | bytes 589856 | tf_op jit(solution)/shard_map/ppermute | solution.py:34
  372.1 8.8 %collective-permute-done.4 = bf16[2,144,1024]{2,1,0:T(8,128)(2,1)} collective-permute-done((bf16[2,144,1024]{2,1,0:T(8,128)(2,1)}, bf16[2,144,1024]{2,1,0:T(8,128)(2,1)}, u32[]{:S(2)}, u32[]{:S(2)}) %collective-permute-start.4) | collective-permute-done | bytes 589856 | tf_op jit(solution)/shard_map/ppermute | solution.py:34
  385.0 8.5 %collective-permute-done.11 = bf16[2,144,1024]{2,1,0:T(8,128)(2,1)} collective-permute-done((bf16[2,144,1024]{2,1,0:T(8,128)(2,1)}, bf16[2,144,1024]{2,1,0:T(8,128)(2,1)}, u32[]{:S(2)}, u32[]{:S(2)}) %collective-permute-start.11) | collective-permute-done | bytes 589856 | tf_op jit(solution)/shard_map/ppermute | solution.py:34
  397.4 8.8 %collective-permute-done.5 = bf16[2,144,1024]{2,1,0:T(8,128)(2,1)} collective-permute-done((bf16[2,144,1024]{2,1,0:T(8,128)(2,1)}, bf16[2,144,1024]{2,1,0:T(8,128)(2,1)}, u32[]{:S(2)}, u32[]{:S(2)}) %collective-permute-start.5) | collective-permute-done | bytes 589856 | tf_op jit(solution)/shard_map/ppermute | solution.py:34
  409.3 9.6 %collective-permute-done.12 = bf16[2,144,1024]{2,1,0:T(8,128)(2,1)} collective-permute-done((bf16[2,144,1024]{2,1,0:T(8,128)(2,1)}, bf16[2,144,1024]{2,1,0:T(8,128)(2,1)}, u32[]{:S(2)}, u32[]{:S(2)}) %collective-permute-start.12) | collective-permute-done | bytes 589856 | tf_op jit(solution)/shard_map/ppermute | solution.py:34
  425.8 11.5 %collective-permute-done.8 = bf16[2,144,1024]{2,1,0:T(8,128)(2,1)} collective-permute-done((bf16[2,144,1024]{2,1,0:T(8,128)(2,1)}, bf16[2,144,1024]{2,1,0:T(8,128)(2,1)}, u32[]{:S(2)}, u32[]{:S(2)}) %collective-permute-start.8) | collective-permute-done | bytes 589856 | tf_op jit(solution)/shard_map/ppermute | solution.py:34
  439.4 10.5 %collective-permute-done.2 = bf16[2,144,1024]{2,1,0:T(8,128)(2,1)} collective-permute-done((bf16[2,144,1024]{2,1,0:T(8,128)(2,1)}, bf16[2,144,1024]{2,1,0:T(8,128)(2,1)}, u32[]{:S(2)}, u32[]{:S(2)}) %collective-permute-start.2) | collective-permute-done | bytes 589856 | tf_op jit(solution)/shard_map/ppermute | solution.py:34
  452.5 10.0 %collective-permute-done.9 = bf16[2,144,1024]{2,1,0:T(8,128)(2,1)} collective-permute-done((bf16[2,144,1024]{2,1,0:T(8,128)(2,1)}, bf16[2,144,1024]{2,1,0:T(8,128)(2,1)}, u32[]{:S(2)}, u32[]{:S(2)}) %collective-permute-start.9) | collective-permute-done | bytes 589856 | tf_op jit(solution)/shard_map/ppermute | solution.py:34
  467.9 10.4 %collective-permute-done.13 = bf16[288,1024]{1,0:T(8,128)(2,1)} collective-permute-done((bf16[288,1024]{1,0:T(8,128)(2,1)}, bf16[288,1024]{1,0:T(8,128)(2,1)}, u32[]{:S(2)}, u32[]{:S(2)}) %collective-permute-start.13) | collective-permute-done | bytes 589856 | tf_op jit(solution)/shard_map/ppermute | solution.py:41
  482.6 4.3 fusion.6
  (159 shorter events, 71.2 us)
Async XLA Ops:
  7.1 131.2 %all-to-all-start = ((bf16[32,36,2048]{2,1,0:T(8,128)(2,1)}), bf16[32,36,2048]{2,1,0:T(8,128)(2,1)}, u32[]{:S(2)}, u32[]{:S(2)}) async-start(bf16[32,36,2048]{2,1,0:T(8,128)(2,1)} %multiply_convert_fusion.1), calls=%async_computation | async-start | bytes 10485760 | tf_op jit(solution)/shard_map/all_to_all | solution.py:99
  23.7 122.8 %copy-start.15 = (bf16[2,2048,384]{2,1,0:T(8,128)(2,1)S(1)}, bf16[2,2048,384]{2,1,0:T(8,128)(2,1)}, u32[]{:S(2)}) copy-start(bf16[2,2048,384]{2,1,0:T(8,128)(2,1)} %param.12) | copy-start | bytes 9437188
  138.2 126.6 %all-to-all-start.1 = ((bf16[32,36,2048]{2,1,0:T(8,128)(2,1)}), bf16[32,36,2048]{2,1,0:T(8,128)(2,1)}, u32[]{:S(2)}, u32[]{:S(2)}) async-start(bf16[32,36,2048]{2,1,0:T(8,128)(2,1)} %multiply_convert_fusion), calls=%async_computation.1 | async-start | bytes 10485760 | tf_op jit(solution)/shard_map/all_to_all | solution.py:99
  277.9 6.9 %copy-start.23 = (bf16[32,18,384]{2,1,0:T(8,128)(2,1)}, bf16[32,18,384]{2,1,0:T(8,128)(2,1)S(1)}, u32[]{:S(2)}) copy-start(bf16[32,18,384]{2,1,0:T(8,128)(2,1)S(1)} %get-tuple-element.6) | copy-start | bytes 1327108
  291.7 8.8 %copy-start.26 = (bf16[32,18,384]{2,1,0:T(8,128)(2,1)S(1)}, bf16[32,18,384]{2,1,0:T(8,128)(2,1)}, u32[]{:S(2)}) copy-start(bf16[32,18,384]{2,1,0:T(8,128)(2,1)} %copy-done.25) | copy-start | bytes 1327108
  291.7 190.9 %all-to-all-start.2 = ((bf16[32,36,2048]{2,1,0:T(8,128)(2,1)}), bf16[32,36,2048]{2,1,0:T(8,128)(2,1)}, u32[]{:S(2)}, u32[]{:S(2)}) async-start(bf16[32,36,2048]{2,1,0:T(8,128)(2,1)} %copy.69), calls=%async_computation.2 | async-start | bytes 10485760 | tf_op jit(solution)/shard_map/all_to_all | solution.py:111
  319.2 7.7 %copy-start = (bf16[4,2,96,1024]{3,2,1,0:T(8,128)(2,1)}, bf16[4,2,96,1024]{3,2,1,0:T(8,128)(2,1)S(1)}, u32[]{:S(2)}) copy-start(bf16[4,2,96,1024]{3,2,1,0:T(8,128)(2,1)S(1)} %concatenate.74) | copy-start | bytes 4718596
  329.2 6.4 %copy-start.24 = (bf16[32,18,384]{2,1,0:T(8,128)(2,1)S(1)}, bf16[32,18,384]{2,1,0:T(8,128)(2,1)}, u32[]{:S(2)}) copy-start(bf16[32,18,384]{2,1,0:T(8,128)(2,1)} %copy-done.23) | copy-start | bytes 1327108
  329.2 24.8 %collective-permute-start.3 = (bf16[2,144,1024]{2,1,0:T(8,128)(2,1)}, bf16[2,144,1024]{2,1,0:T(8,128)(2,1)}, u32[]{:S(2)}, u32[]{:S(2)}) collective-permute-start(bf16[2,144,1024]{2,1,0:T(8,128)(2,1)} %get-tuple-element.12), channel_id=1, source_target_pairs={{0,192},{32,224},{64,0},{96,32},{128,64},{160,96},{192,128},{224,1... | collective-permute-start | bytes 1769480 | tf_op jit(solution)/shard_map/ppermute | solution.py:34
  353.5 14.8 %collective-permute-start.10 = (bf16[2,144,1024]{2,1,0:T(8,128)(2,1)}, bf16[2,144,1024]{2,1,0:T(8,128)(2,1)}, u32[]{:S(2)}, u32[]{:S(2)}) collective-permute-start(bf16[2,144,1024]{2,1,0:T(8,128)(2,1)} %get-tuple-element.16), channel_id=1, source_target_pairs={{0,192},{32,224},{64,0},{96,32},{128,64},{160,96},{192,128},{224,1... | collective-permute-start | bytes 1769480 | tf_op jit(solution)/shard_map/ppermute | solution.py:34
  354.0 14.3 %copy-start.4 = (bf16[4,2,96,1024]{3,2,1,0:T(8,128)(2,1)S(1)}, bf16[4,2,96,1024]{3,2,1,0:T(8,128)(2,1)}, u32[]{:S(2)}) copy-start(bf16[4,2,96,1024]{3,2,1,0:T(8,128)(2,1)} %concatenate.83) | copy-start | bytes 4718596
  356.3 24.7 %collective-permute-start.4 = (bf16[2,144,1024]{2,1,0:T(8,128)(2,1)}, bf16[2,144,1024]{2,1,0:T(8,128)(2,1)}, u32[]{:S(2)}, u32[]{:S(2)}) collective-permute-start(bf16[2,144,1024]{2,1,0:T(8,128)(2,1)} %fusion.55), channel_id=1, source_target_pairs={{0,192},{32,224},{64,0},{96,32},{128,64},{160,96},{192,128},{224,1... | collective-permute-start | bytes 1769480 | tf_op jit(solution)/shard_map/ppermute | solution.py:34
  370.4 23.2 %collective-permute-start.11 = (bf16[2,144,1024]{2,1,0:T(8,128)(2,1)}, bf16[2,144,1024]{2,1,0:T(8,128)(2,1)}, u32[]{:S(2)}, u32[]{:S(2)}) collective-permute-start(bf16[2,144,1024]{2,1,0:T(8,128)(2,1)} %fusion.48), channel_id=1, source_target_pairs={{0,192},{32,224},{64,0},{96,32},{128,64},{160,96},{192,128},{224,1... | collective-permute-start | bytes 1769480 | tf_op jit(solution)/shard_map/ppermute | solution.py:34
  372.1 21.5 %copy-start.5 = (bf16[4,2,96,1024]{3,2,1,0:T(8,128)(2,1)S(1)}, bf16[4,2,96,1024]{3,2,1,0:T(8,128)(2,1)}, u32[]{:S(2)}) copy-start(bf16[4,2,96,1024]{3,2,1,0:T(8,128)(2,1)} %concatenate.83) | copy-start | bytes 4718596
  372.1 25.3 %collective-permute-start = (bf16[2,144,1024]{2,1,0:T(8,128)(2,1)}, bf16[2,144,1024]{2,1,0:T(8,128)(2,1)}, u32[]{:S(2)}, u32[]{:S(2)}) collective-permute-start(bf16[2,144,1024]{2,1,0:T(8,128)(2,1)} %get-tuple-element.13), channel_id=1, source_target_pairs={{0,64},{32,96},{64,128},{96,160},{128,192},{160,224},{192,0},{224,... | collective-permute-start | bytes 1769480 | tf_op jit(solution)/shard_map/ppermute | solution.py:34
  383.2 23.1 %collective-permute-start.5 = (bf16[2,144,1024]{2,1,0:T(8,128)(2,1)}, bf16[2,144,1024]{2,1,0:T(8,128)(2,1)}, u32[]{:S(2)}, u32[]{:S(2)}) collective-permute-start(bf16[2,144,1024]{2,1,0:T(8,128)(2,1)} %fusion.54), channel_id=1, source_target_pairs={{0,192},{32,224},{64,0},{96,32},{128,64},{160,96},{192,128},{224,1... | collective-permute-start | bytes 1769480 | tf_op jit(solution)/shard_map/ppermute | solution.py:34
  384.8 24.4 %collective-permute-start.7 = (bf16[2,144,1024]{2,1,0:T(8,128)(2,1)}, bf16[2,144,1024]{2,1,0:T(8,128)(2,1)}, u32[]{:S(2)}, u32[]{:S(2)}) collective-permute-start(bf16[2,144,1024]{2,1,0:T(8,128)(2,1)} %get-tuple-element.17), channel_id=1, source_target_pairs={{0,64},{32,96},{64,128},{96,160},{128,192},{160,224},{192,0},{224,... | collective-permute-start | bytes 1769480 | tf_op jit(solution)/shard_map/ppermute | solution.py:34
  395.7 23.2 %collective-permute-start.12 = (bf16[2,144,1024]{2,1,0:T(8,128)(2,1)}, bf16[2,144,1024]{2,1,0:T(8,128)(2,1)}, u32[]{:S(2)}, u32[]{:S(2)}) collective-permute-start(bf16[2,144,1024]{2,1,0:T(8,128)(2,1)} %fusion.47), channel_id=1, source_target_pairs={{0,192},{32,224},{64,0},{96,32},{128,64},{160,96},{192,128},{224,1... | collective-permute-start | bytes 1769480 | tf_op jit(solution)/shard_map/ppermute | solution.py:34
  397.4 21.5 %copy-start.1 = (bf16[4,2,96,1024]{3,2,1,0:T(8,128)(2,1)S(1)}, bf16[4,2,96,1024]{3,2,1,0:T(8,128)(2,1)}, u32[]{:S(2)}) copy-start(bf16[4,2,96,1024]{3,2,1,0:T(8,128)(2,1)} %concatenate.80) | copy-start | bytes 4718596
  397.4 21.5 %copy-start.6 = (bf16[4,2,96,1024]{3,2,1,0:T(8,128)(2,1)S(1)}, bf16[4,2,96,1024]{3,2,1,0:T(8,128)(2,1)}, u32[]{:S(2)}) copy-start(bf16[4,2,96,1024]{3,2,1,0:T(8,128)(2,1)} %concatenate.83) | copy-start | bytes 4718596
  409.2 14.3 %collective-permute-start.1 = (bf16[2,144,1024]{2,1,0:T(8,128)(2,1)}, bf16[2,144,1024]{2,1,0:T(8,128)(2,1)}, u32[]{:S(2)}, u32[]{:S(2)}) collective-permute-start(bf16[2,144,1024]{2,1,0:T(8,128)(2,1)} %get-tuple-element.11), channel_id=1, source_target_pairs={{0,64},{32,96},{64,128},{96,160},{128,192},{160,224},{192,0},{224,... | collective-permute-start | bytes 1769480 | tf_op jit(solution)/shard_map/ppermute | solution.py:34
  421.7 15.6 %collective-permute-start.8 = (bf16[2,144,1024]{2,1,0:T(8,128)(2,1)}, bf16[2,144,1024]{2,1,0:T(8,128)(2,1)}, u32[]{:S(2)}, u32[]{:S(2)}) collective-permute-start(bf16[2,144,1024]{2,1,0:T(8,128)(2,1)} %get-tuple-element.15), channel_id=1, source_target_pairs={{0,64},{32,96},{64,128},{96,160},{128,192},{160,224},{192,0},{224,... | collective-permute-start | bytes 1769480 | tf_op jit(solution)/shard_map/ppermute | solution.py:34
  421.7 15.6 %copy-start.2 = (bf16[4,2,96,1024]{3,2,1,0:T(8,128)(2,1)S(1)}, bf16[4,2,96,1024]{3,2,1,0:T(8,128)(2,1)}, u32[]{:S(2)}) copy-start(bf16[4,2,96,1024]{3,2,1,0:T(8,128)(2,1)} %concatenate.80) | copy-start | bytes 4718596
  425.8 24.1 %collective-permute-start.2 = (bf16[2,144,1024]{2,1,0:T(8,128)(2,1)}, bf16[2,144,1024]{2,1,0:T(8,128)(2,1)}, u32[]{:S(2)}, u32[]{:S(2)}) collective-permute-start(bf16[2,144,1024]{2,1,0:T(8,128)(2,1)} %fusion.57), channel_id=1, source_target_pairs={{0,64},{32,96},{64,128},{96,160},{128,192},{160,224},{192,0},{224,... | collective-permute-start | bytes 1769480 | tf_op jit(solution)/shard_map/ppermute | solution.py:34
  439.4 23.1 %collective-permute-start.9 = (bf16[2,144,1024]{2,1,0:T(8,128)(2,1)}, bf16[2,144,1024]{2,1,0:T(8,128)(2,1)}, u32[]{:S(2)}, u32[]{:S(2)}) collective-permute-start(bf16[2,144,1024]{2,1,0:T(8,128)(2,1)} %fusion.50), channel_id=1, source_target_pairs={{0,64},{32,96},{64,128},{96,160},{128,192},{160,224},{192,0},{224,... | collective-permute-start | bytes 1769480 | tf_op jit(solution)/shard_map/ppermute | solution.py:34
  439.4 11.9 %copy-start.9 = (bf16[2,144,1024]{2,1,0:T(8,128)(2,1)S(1)}, bf16[2,144,1024]{2,1,0:T(8,128)(2,1)}, u32[]{:S(2)}) copy-start(bf16[2,144,1024]{2,1,0:T(8,128)(2,1)} %get-tuple-element.10) | copy-start | bytes 1769476
  451.3 12.5 %copy-start.7 = (bf16[2,144,1024]{2,1,0:T(8,128)(2,1)}, bf16[2,144,1024]{2,1,0:T(8,128)(2,1)S(1)}, u32[]{:S(2)}) copy-start(bf16[2,144,1024]{2,1,0:T(8,128)(2,1)S(1)} %fusion.56) | copy-start | bytes 1769476
  451.3 11.2 %copy-start.3 = (bf16[4,2,96,1024]{3,2,1,0:T(8,128)(2,1)S(1)}, bf16[4,2,96,1024]{3,2,1,0:T(8,128)(2,1)}, u32[]{:S(2)}) copy-start(bf16[4,2,96,1024]{3,2,1,0:T(8,128)(2,1)} %concatenate.80) | copy-start | bytes 4718596
  452.2 11.7 %copy-start.11 = (bf16[2,144,1024]{2,1,0:T(8,128)(2,1)S(1)}, bf16[2,144,1024]{2,1,0:T(8,128)(2,1)}, u32[]{:S(2)}) copy-start(bf16[2,144,1024]{2,1,0:T(8,128)(2,1)} %get-tuple-element.14) | copy-start | bytes 1769476
  452.2 14.1 %collective-permute-start.6 = (bf16[288,1024]{1,0:T(8,128)(2,1)}, bf16[288,1024]{1,0:T(8,128)(2,1)}, u32[]{:S(2)}, u32[]{:S(2)}) collective-permute-start(bf16[288,1024]{1,0:T(8,128)(2,1)} %fusion.81), channel_id=1, source_target_pairs={{0,32},{32,0},{64,96},{96,64},{128,160},{160,128},{192,224},{224,1... | collective-permute-start | bytes 1769480 | tf_op jit(solution)/shard_map/ppermute | solution.py:41
  464.7 13.6 %collective-permute-start.13 = (bf16[288,1024]{1,0:T(8,128)(2,1)}, bf16[288,1024]{1,0:T(8,128)(2,1)}, u32[]{:S(2)}, u32[]{:S(2)}) collective-permute-start(bf16[288,1024]{1,0:T(8,128)(2,1)} %fusion.77), channel_id=1, source_target_pairs={{0,32},{32,0},{64,96},{96,64},{128,160},{160,128},{192,224},{224,1... | collective-permute-start | bytes 1769480 | tf_op jit(solution)/shard_map/ppermute | solution.py:41
  466.3 12.0 %copy-start.12 = (bf16[2,144,1024]{2,1,0:T(8,128)(2,1)S(1)}, bf16[2,144,1024]{2,1,0:T(8,128)(2,1)}, u32[]{:S(2)}) copy-start(bf16[2,144,1024]{2,1,0:T(8,128)(2,1)} %get-tuple-element.14) | copy-start | bytes 1769476
  (26 other events, 91.0 us)

commit v6 on v5

--- a/solution.py
+++ b/solution.py
@@ -40,6 +40,19 @@
     give = lax.dynamic_index_in_dim(both, 1 - x_lo, axis=0, keepdims=False)
     got = lax.ppermute(give, "dp", [(d, d ^ 1) for d in range(n_dp)])
     return (keep.astype(jnp.float32) + got.astype(jnp.float32)).astype(jnp.bfloat16)
+
+
+def pack_grads(grad_g, grad_u, grad_d, n_dp, lanes=1024):
+    width, hid = grad_g.shape
+    dsl = width // n_dp
+    return jnp.concatenate(
+        [
+            grad_g.reshape(n_dp, dsl * hid // lanes, lanes),
+            grad_u.reshape(n_dp, dsl * hid // lanes, lanes),
+            grad_d.reshape(hid, n_dp, dsl).transpose(1, 0, 2).reshape(n_dp, hid * dsl // lanes, lanes),
+        ],
+        axis=1,
+    )
 
 
 def expert_work(xr, scaled, w_gate, w_up, w_down):
@@ -104,9 +117,10 @@
         contrib, grad_g, grad_u, grad_d = expert_work(
             xr, scaled, gate_weight[local], up_weight[local], down_weight[local]
         )
-        after = contrib
+        reduced = dp_reduce_scatter(pack_grads(grad_g, grad_u, grad_d, n_dp), n_dp)
+        after = (contrib, reduced)
         contribs.append(contrib)
-        grads.append((grad_g, grad_u, grad_d))
+        grads.append(reduced.reshape(3, -1))
 
     back = lax.all_to_all(
         jnp.concatenate(contribs, axis=1), "expert", split_axis=0, concat_axis=0, tiled=True
@@ -115,21 +129,9 @@
     in_grad = contract(sel_all, back, (0, 1), (0, 1)).astype(jnp.bfloat16)
 
     dsl = width // n_dp
-    reduced = []
-    for grad_g, grad_u, grad_d in grads:
-        lanes = 1024
-        packed = jnp.concatenate(
-            [
-                grad_g.reshape(n_dp, dsl * hid // lanes, lanes),
-                grad_u.reshape(n_dp, dsl * hid // lanes, lanes),
-                grad_d.reshape(hid, n_dp, dsl).transpose(1, 0, 2).reshape(n_dp, hid * dsl // lanes, lanes),
-            ],
-            axis=1,
-        )
-        reduced.append(dp_reduce_scatter(packed, n_dp).reshape(3, dsl * hid))
-    stack_g = jnp.stack([r[0].reshape(dsl, hid) for r in reduced], axis=0)
-    stack_u = jnp.stack([r[1].reshape(dsl, hid) for r in reduced], axis=0)
-    stack_d = jnp.stack([r[2].reshape(hid, dsl) for r in reduced], axis=0)
+    stack_g = jnp.stack([r[0].reshape(dsl, hid) for r in grads], axis=0)
+    stack_u = jnp.stack([r[1].reshape(dsl, hid) for r in grads], axis=0)
+    stack_d = jnp.stack([r[2].reshape(hid, dsl) for r in grads], axis=0)
     return (in_grad, stack_g, stack_u, stack_d)
 
 

time: 493 us -> 447 us (0.907)
  waiting for transfers between devices: 309 us -> 271 us
  other arithmetic: 34.7 us -> 23.1 us
  starting transfers between devices: 38.9 us -> 49.9 us
  local copies, waits for them, and re-layouts: 32.4 us -> 26.5 us
    all_to_all x2, waiting for transfers between devices: 216 us -> 114 us  [per_device(): lax.all_to_all(send, 'expert', split_axis=0, concat_axis=0, tiled=True)]
    ppermute x12, waiting for transfers between devices: 81.6 us -> 131 us  [dp_reduce_scatter(): recv = lax.ppermute(send[h], 'dp', perms[h])]
    ppermute x2, waiting for transfers between devices: 10.4 us -> 25.5 us  [dp_reduce_scatter(): got = lax.ppermute(give, 'dp', [(d, d ^ 1) for d in range(n_dp)])]
    convert_element_type x10, other arithmetic: 21.6 us -> 12.3 us  [dp_reduce_scatter(): send[h] = acc.astype(jnp.bfloat16)]
    ppermute x12, starting transfers between devices: 8.74 us -> 14.7 us  [dp_reduce_scatter(): recv = lax.ppermute(send[h], 'dp', perms[h])]
  transfers between devices with their start and end apart: 17 -> 17, of which waited for: 12 -> 13; matrix products, arithmetic and copies ran while one was open for 20% -> 19% of each run, Pallas kernels for 0% -> 0%
where the time goes in v6:
time: 447 us; the launch traced here: 441 us
  waiting for transfers between devices  271 us (61%)
  matrix products  69.2 us (15%)
  starting transfers between devices  49.9 us (11%)
  local copies, waits for them, and re-layouts  26.5 us (6%)
  other arithmetic  23.1 us (5%)
    ppermute x12, waiting for transfers between devices, dp_reduce_scatter(): recv = lax.ppermute(send[h], 'dp', perms[h])  131 us
    all_to_all x2, waiting for transfers between devices, per_device(): lax.all_to_all(send, 'expert', split_axis=0, concat_axis=0, tiled=True)  114 us
    dot_general x20, matrix products, contract(): lax.dot_general(left, right, ((left_dims, right_dims), ((), ())), preferr...  69.2 us
    ppermute x2, waiting for transfers between devices, dp_reduce_scatter(): got = lax.ppermute(give, 'dp', [(d, d ^ 1) for d in range(n_dp)])  25.5 us
    all_to_all x2, starting transfers between devices, per_device(): lax.all_to_all(send, 'expert', split_axis=0, concat_axis=0, tiled=True)  21.1 us
    concatenate x6, local copies, waits for them, and re-layouts, pack_grads(): jnp.concatenate([grad_g.reshape(n_dp, dsl * hid // lanes, lanes), grad_u....  15.2 us
    ppermute x12, starting transfers between devices, dp_reduce_scatter(): recv = lax.ppermute(send[h], 'dp', perms[h])  14.7 us
    all_to_all x1, starting transfers between devices, per_device(): lax.all_to_all(jnp.concatenate(contribs, axis=1), 'expert', split_axis=0,...  13.2 us
  transfers between devices with their start and end apart: 17, of which 13 were waited for; matrix products, arithmetic and copies ran while one was open for 19% of the time, Pallas kernels for 0%

profile of v6, /device:TPU:1, one launch (start us, length us, event | category | flops | bytes accessed | tf_op | source)
XLA Modules:
  0.0 441.2 jit_solution(4250528698519354333)
XLA Ops:
  3.1 3.9 multiply_convert_fusion.1
  7.0 12.6 %all-to-all-start = ((bf16[32,36,2048]{2,1,0:T(8,128)(2,1)}), bf16[32,36,2048]{2,1,0:T(8,128)(2,1)}, u32[]{:S(2)}, u32[]{:S(2)}) async-start(bf16[32,36,2048]{2,1,0:T(8,128)(2,1)} %multiply_convert_fusion.1), calls=%async_computation | async-start | bytes 10485760 | tf_op jit(solution)/shard_map/all_to_all | solution.py:112
  19.8 4.0 multiply_convert_fusion
  23.7 114.4 %all-to-all-done = bf16[32,36,2048]{2,1,0:T(8,128)(2,1)} async-done(((bf16[32,36,2048]{2,1,0:T(8,128)(2,1)}), bf16[32,36,2048]{2,1,0:T(8,128)(2,1)}, u32[]{:S(2)}, u32[]{:S(2)}) %all-to-all-start) | async-done | bytes 4718624 | tf_op jit(solution)/shard_map/all_to_all | solution.py:112
  138.2 8.4 %all-to-all-start.1 = ((bf16[32,36,2048]{2,1,0:T(8,128)(2,1)}), bf16[32,36,2048]{2,1,0:T(8,128)(2,1)}, u32[]{:S(2)}, u32[]{:S(2)}) async-start(bf16[32,36,2048]{2,1,0:T(8,128)(2,1)} %multiply_convert_fusion), calls=%async_computation.1 | async-start | bytes 10485760 | tf_op jit(solution)/shard_map/all_to_all | solution.py:112
  146.6 3.9 fusion.9
  150.5 4.2 fusion.11
  154.7 3.9 bitcast_convert_fusion.3
  161.7 5.6 %multiply_convert_fusion.6 = (bf16[32,18,384]{2,1,0:T(8,128)(2,1)S(1)}, bf16[32,18,384]{2,1,0:T(8,128)(2,1)}) fusion(f32[32,18,384]{2,1,0:T(8,128)S(1)} %copy-done.28, f32[32,18,384]{2,1,0:T(8,128)} %copy-done.29, bf16[2,384,2048]{2,1,0:T(8,128)(2,1)} %param.13, bf16[32,36,2048]{2,1,0:T(8,128)(2,1)} %all-to-all-done), kind=kOutput, calls=%fused_computation.132 | convolution fusion | flops 908845056 | bytes 7667712 | tf_op jit(solution)/shard_map/dot_general | solution.py:8
  168.2 3.7 bitcast_convert_fusion.4
  173.8 5.0 %bitcast_convert_fusion.5 = bf16[2048,384]{1,0:T(8,128)(2,1)} fusion(bf16[32,18,384]{2,1,0:T(8,128)(2,1)} %get-tuple-element.9, bf16[32,36,2048]{2,1,0:T(8,128)(2,1)} %all-to-all-done), kind=kOutput, calls=%fused_computation.10 | convolution fusion | flops 906756096 | bytes 5308416 | tf_op jit(solution)/shard_map/dot_general | solution.py:8
  178.8 3.7 concatenate.73
  187.3 12.9 %collective-permute-done.3 = bf16[2,144,1024]{2,1,0:T(8,128)(2,1)} collective-permute-done((bf16[2,144,1024]{2,1,0:T(8,128)(2,1)}, bf16[2,144,1024]{2,1,0:T(8,128)(2,1)}, u32[]{:S(2)}, u32[]{:S(2)}) %collective-permute-start.3) | collective-permute-done | bytes 589856 | tf_op jit(solution)/shard_map/ppermute | solution.py:34
  205.8 12.0 %collective-permute-done.4 = bf16[2,144,1024]{2,1,0:T(8,128)(2,1)} collective-permute-done((bf16[2,144,1024]{2,1,0:T(8,128)(2,1)}, bf16[2,144,1024]{2,1,0:T(8,128)(2,1)}, u32[]{:S(2)}, u32[]{:S(2)}) %collective-permute-start.4) | collective-permute-done | bytes 589856 | tf_op jit(solution)/shard_map/ppermute | solution.py:34
  223.5 11.2 %collective-permute-done.5 = bf16[2,144,1024]{2,1,0:T(8,128)(2,1)} collective-permute-done((bf16[2,144,1024]{2,1,0:T(8,128)(2,1)}, bf16[2,144,1024]{2,1,0:T(8,128)(2,1)}, u32[]{:S(2)}, u32[]{:S(2)}) %collective-permute-start.5) | collective-permute-done | bytes 589856 | tf_op jit(solution)/shard_map/ppermute | solution.py:34
  237.6 14.7 %collective-permute-done.1 = bf16[2,144,1024]{2,1,0:T(8,128)(2,1)} collective-permute-done((bf16[2,144,1024]{2,1,0:T(8,128)(2,1)}, bf16[2,144,1024]{2,1,0:T(8,128)(2,1)}, u32[]{:S(2)}, u32[]{:S(2)}) %collective-permute-start.1) | collective-permute-done | bytes 589856 | tf_op jit(solution)/shard_map/ppermute | solution.py:34
  254.4 13.1 %collective-permute-done.2 = bf16[2,144,1024]{2,1,0:T(8,128)(2,1)} collective-permute-done((bf16[2,144,1024]{2,1,0:T(8,128)(2,1)}, bf16[2,144,1024]{2,1,0:T(8,128)(2,1)}, u32[]{:S(2)}, u32[]{:S(2)}) %collective-permute-start.2) | collective-permute-done | bytes 589856 | tf_op jit(solution)/shard_map/ppermute | solution.py:34
  273.1 7.0 %collective-permute-done.6 = bf16[288,1024]{1,0:T(8,128)(2,1)S(1)} collective-permute-done((bf16[288,1024]{1,0:T(8,128)(2,1)S(1)}, bf16[288,1024]{1,0:T(8,128)(2,1)S(1)}, u32[]{:S(2)}, u32[]{:S(2)}) %collective-permute-start.6) | collective-permute-done | bytes 589856 | tf_op jit(solution)/shard_map/ppermute | solution.py:41
  281.2 4.3 fusion.15
  285.5 3.9 fusion.17
  289.4 4.5 %multiply_convert_fusion.3 = (bf16[32,18,384]{2,1,0:T(8,128)(2,1)S(1)}, bf16[32,18,384]{2,1,0:T(8,128)(2,1)S(1)}) fusion(f32[32,18,384]{2,1,0:T(8,128)S(1)} %fusion.15, f32[32,18,384]{2,1,0:T(8,128)S(1)} %fusion.17, bf16[2,384,2048]{2,1,0:T(8,128)(2,1)S(1)} %copy-done.22, bf16[32,36,2048]{2,1,0:T(8,128)(2,1)} %all-to-all-done.1), kind=kOutput, calls=%fused_computation.128 | convolution fusion | flops 908845056 | bytes 7962624 | tf_op jit(solution)/shard_map/dot_general | solution.py:8
  297.2 5.1 %copy.70 = bf16[32,36,2048]{2,1,0:T(8,128)(2,1)} copy(bf16[32,36,2048]{2,0,1:T(8,128)(2,1)S(1)} %pad_maximum_fusion) | data formatting | bytes 9437184 | tf_op jit(solution)/shard_map/concatenate | solution.py:126
  302.3 13.2 %all-to-all-start.2 = ((bf16[32,36,2048]{2,1,0:T(8,128)(2,1)}), bf16[32,36,2048]{2,1,0:T(8,128)(2,1)}, u32[]{:S(2)}, u32[]{:S(2)}) async-start(bf16[32,36,2048]{2,1,0:T(8,128)(2,1)} %copy.70), calls=%async_computation.2 | async-start | bytes 10485760 | tf_op jit(solution)/shard_map/all_to_all | solution.py:125
  322.1 3.9 bitcast_convert_fusion.1
  327.9 5.0 %bitcast_convert_fusion.2 = bf16[2048,384]{1,0:T(8,128)(2,1)} fusion(bf16[32,18,384]{2,1,0:T(8,128)(2,1)} %copy-done.16, bf16[32,36,2048]{2,1,0:T(8,128)(2,1)} %all-to-all-done.1), kind=kOutput, calls=%fused_computation.7 | convolution fusion | flops 906756096 | bytes 5308416 | tf_op jit(solution)/shard_map/dot_general | solution.py:8
  337.5 14.7 %collective-permute-done.10 = bf16[2,144,1024]{2,1,0:T(8,128)(2,1)S(1)} collective-permute-done((bf16[2,144,1024]{2,1,0:T(8,128)(2,1)S(1)}, bf16[2,144,1024]{2,1,0:T(8,128)(2,1)S(1)}, u32[]{:S(2)}, u32[]{:S(2)}) %collective-permute-start.10) | collective-permute-done | bytes 589856 | tf_op jit(solution)/shard_map/ppermute | solution.py:34
  354.0 12.4 %collective-permute-done.11 = bf16[2,144,1024]{2,1,0:T(8,128)(2,1)S(1)} collective-permute-done((bf16[2,144,1024]{2,1,0:T(8,128)(2,1)S(1)}, bf16[2,144,1024]{2,1,0:T(8,128)(2,1)S(1)}, u32[]{:S(2)}, u32[]{:S(2)}) %collective-permute-start.11) | collective-permute-done | bytes 589856 | tf_op jit(solution)/shard_map/ppermute | solution.py:34
  370.0 11.2 %collective-permute-done.12 = bf16[2,144,1024]{2,1,0:T(8,128)(2,1)S(1)} collective-permute-done((bf16[2,144,1024]{2,1,0:T(8,128)(2,1)S(1)}, bf16[2,144,1024]{2,1,0:T(8,128)(2,1)S(1)}, u32[]{:S(2)}, u32[]{:S(2)}) %collective-permute-start.12) | collective-permute-done | bytes 589856 | tf_op jit(solution)/shard_map/ppermute | solution.py:34
  381.7 15.0 %collective-permute-done.8 = bf16[2,144,1024]{2,1,0:T(8,128)(2,1)S(1)} collective-permute-done((bf16[2,144,1024]{2,1,0:T(8,128)(2,1)S(1)}, bf16[2,144,1024]{2,1,0:T(8,128)(2,1)S(1)}, u32[]{:S(2)}, u32[]{:S(2)}) %collective-permute-start.8) | collective-permute-done | bytes 589856 | tf_op jit(solution)/shard_map/ppermute | solution.py:34
  397.1 13.4 %collective-permute-done.9 = bf16[2,144,1024]{2,1,0:T(8,128)(2,1)S(1)} collective-permute-done((bf16[2,144,1024]{2,1,0:T(8,128)(2,1)S(1)}, bf16[2,144,1024]{2,1,0:T(8,128)(2,1)S(1)}, u32[]{:S(2)}, u32[]{:S(2)}) %collective-permute-start.9) | collective-permute-done | bytes 589856 | tf_op jit(solution)/shard_map/ppermute | solution.py:34
  414.3 18.5 %collective-permute-done.13 = bf16[288,1024]{1,0:T(8,128)(2,1)} collective-permute-done((bf16[288,1024]{1,0:T(8,128)(2,1)}, bf16[288,1024]{1,0:T(8,128)(2,1)}, u32[]{:S(2)}, u32[]{:S(2)}) %collective-permute-start.13) | collective-permute-done | bytes 589856 | tf_op jit(solution)/shard_map/ppermute | solution.py:41
  436.5 4.3 fusion.6
  (137 shorter events, 65.7 us)
Async XLA Ops:
  1.5 5.5 %copy-start.20 = (pred[128,64]{0,1:T(8,128)(4,1)}, pred[128,64]{0,1:T(8,128)(4,1)S(1)}, u32[]{:S(2)}) copy-start(pred[128,64]{0,1:T(8,128)(4,1)S(1)} %fusion.125) | copy-start | bytes 24580
  1.6 5.4 %copy-start.13 = (s32[64,128]{1,0:T(8,128)}, s32[64,128]{1,0:T(8,128)S(1)}, u32[]{:S(2)}) copy-start(s32[64,128]{1,0:T(8,128)S(1)} %convolution_convert_fusion) | copy-start | bytes 98308
  7.0 131.2 %all-to-all-start = ((bf16[32,36,2048]{2,1,0:T(8,128)(2,1)}), bf16[32,36,2048]{2,1,0:T(8,128)(2,1)}, u32[]{:S(2)}, u32[]{:S(2)}) async-start(bf16[32,36,2048]{2,1,0:T(8,128)(2,1)} %multiply_convert_fusion.1), calls=%async_computation | async-start | bytes 10485760 | tf_op jit(solution)/shard_map/all_to_all | solution.py:112
  23.7 122.9 %copy-start.6 = (bf16[2,2048,384]{2,1,0:T(8,128)(2,1)S(1)}, bf16[2,2048,384]{2,1,0:T(8,128)(2,1)}, u32[]{:S(2)}) copy-start(bf16[2,2048,384]{2,1,0:T(8,128)(2,1)} %param.11) | copy-start | bytes 9437188
  138.2 143.0 %all-to-all-start.1 = ((bf16[32,36,2048]{2,1,0:T(8,128)(2,1)}), bf16[32,36,2048]{2,1,0:T(8,128)(2,1)}, u32[]{:S(2)}, u32[]{:S(2)}) async-start(bf16[32,36,2048]{2,1,0:T(8,128)(2,1)} %multiply_convert_fusion), calls=%async_computation.1 | async-start | bytes 10485760 | tf_op jit(solution)/shard_map/all_to_all | solution.py:112
  146.6 3.9 copy-start.9
  150.5 4.2 copy-start.27
  154.7 3.9 copy-start.29
  184.6 15.6 %collective-permute-start.3 = (bf16[2,144,1024]{2,1,0:T(8,128)(2,1)}, bf16[2,144,1024]{2,1,0:T(8,128)(2,1)}, u32[]{:S(2)}, u32[]{:S(2)}) collective-permute-start(bf16[2,144,1024]{2,1,0:T(8,128)(2,1)} %get-tuple-element.16), channel_id=1, source_target_pairs={{0,192},{32,224},{64,0},{96,32},{128,64},{160,96},{192,128},{224,1... | collective-permute-start | bytes 1769480 | tf_op jit(solution)/shard_map/ppermute | solution.py:34
  202.4 15.4 %collective-permute-start.4 = (bf16[2,144,1024]{2,1,0:T(8,128)(2,1)}, bf16[2,144,1024]{2,1,0:T(8,128)(2,1)}, u32[]{:S(2)}, u32[]{:S(2)}) collective-permute-start(bf16[2,144,1024]{2,1,0:T(8,128)(2,1)} %fusion.55), channel_id=1, source_target_pairs={{0,192},{32,224},{64,0},{96,32},{128,64},{160,96},{192,128},{224,1... | collective-permute-start | bytes 1769480 | tf_op jit(solution)/shard_map/ppermute | solution.py:34
  205.8 17.7 %collective-permute-start = (bf16[2,144,1024]{2,1,0:T(8,128)(2,1)}, bf16[2,144,1024]{2,1,0:T(8,128)(2,1)}, u32[]{:S(2)}, u32[]{:S(2)}) collective-permute-start(bf16[2,144,1024]{2,1,0:T(8,128)(2,1)} %get-tuple-element.17), channel_id=1, source_target_pairs={{0,64},{32,96},{64,128},{96,160},{128,192},{160,224},{192,0},{224,... | collective-permute-start | bytes 1769480 | tf_op jit(solution)/shard_map/ppermute | solution.py:34
  220.1 14.6 %collective-permute-start.5 = (bf16[2,144,1024]{2,1,0:T(8,128)(2,1)}, bf16[2,144,1024]{2,1,0:T(8,128)(2,1)}, u32[]{:S(2)}, u32[]{:S(2)}) collective-permute-start(bf16[2,144,1024]{2,1,0:T(8,128)(2,1)} %fusion.54), channel_id=1, source_target_pairs={{0,192},{32,224},{64,0},{96,32},{128,64},{160,96},{192,128},{224,1... | collective-permute-start | bytes 1769480 | tf_op jit(solution)/shard_map/ppermute | solution.py:34
  237.6 14.7 %collective-permute-start.1 = (bf16[2,144,1024]{2,1,0:T(8,128)(2,1)}, bf16[2,144,1024]{2,1,0:T(8,128)(2,1)}, u32[]{:S(2)}, u32[]{:S(2)}) collective-permute-start(bf16[2,144,1024]{2,1,0:T(8,128)(2,1)} %get-tuple-element.15), channel_id=1, source_target_pairs={{0,64},{32,96},{64,128},{96,160},{128,192},{160,224},{192,0},{224,... | collective-permute-start | bytes 1769480 | tf_op jit(solution)/shard_map/ppermute | solution.py:34
  254.4 13.1 %collective-permute-start.2 = (bf16[2,144,1024]{2,1,0:T(8,128)(2,1)}, bf16[2,144,1024]{2,1,0:T(8,128)(2,1)}, u32[]{:S(2)}, u32[]{:S(2)}) collective-permute-start(bf16[2,144,1024]{2,1,0:T(8,128)(2,1)} %fusion.57), channel_id=1, source_target_pairs={{0,64},{32,96},{64,128},{96,160},{128,192},{160,224},{192,0},{224,... | collective-permute-start | bytes 1769480 | tf_op jit(solution)/shard_map/ppermute | solution.py:34
  254.4 14.6 %copy-start.3 = (bf16[2,144,1024]{2,1,0:T(8,128)(2,1)S(1)}, bf16[2,144,1024]{2,1,0:T(8,128)(2,1)}, u32[]{:S(2)}) copy-start(bf16[2,144,1024]{2,1,0:T(8,128)(2,1)} %get-tuple-element.14) | copy-start | bytes 1769476
  269.1 11.0 %collective-permute-start.6 = (bf16[288,1024]{1,0:T(8,128)(2,1)S(1)}, bf16[288,1024]{1,0:T(8,128)(2,1)S(1)}, u32[]{:S(2)}, u32[]{:S(2)}) collective-permute-start(bf16[288,1024]{1,0:T(8,128)(2,1)S(1)} %fusion.81), channel_id=1, source_target_pairs={{0,32},{32,0},{64,96},{96,64},{128,160},{160,128},{192,224},{224,1... | collective-permute-start | bytes 1769480 | tf_op jit(solution)/shard_map/ppermute | solution.py:41
  281.2 4.3 copy-start.11
  289.4 4.5 %copy-start.25 = (f32[32,18,384]{2,1,0:T(8,128)}, f32[32,18,384]{2,1,0:T(8,128)S(1)}, u32[]{:S(2)}) copy-start(f32[32,18,384]{2,1,0:T(8,128)S(1)} %fusion.17) | copy-start | bytes 2654212
  289.4 4.5 %copy-start.8 = (bf16[2,2048,384]{2,1,0:T(8,128)(2,1)S(1)}, bf16[2,2048,384]{2,1,0:T(8,128)(2,1)}, u32[]{:S(2)}) copy-start(bf16[2,2048,384]{2,1,0:T(8,128)(2,1)} %param.11) | copy-start | bytes 9437188
  302.3 13.2 %copy-start.26 = (f32[32,18,384]{2,1,0:T(8,128)S(1)}, f32[32,18,384]{2,1,0:T(8,128)}, u32[]{:S(2)}) copy-start(f32[32,18,384]{2,1,0:T(8,128)} %copy-done.25) | copy-start | bytes 2654212
  302.3 134.2 %all-to-all-start.2 = ((bf16[32,36,2048]{2,1,0:T(8,128)(2,1)}), bf16[32,36,2048]{2,1,0:T(8,128)(2,1)}, u32[]{:S(2)}, u32[]{:S(2)}) async-start(bf16[32,36,2048]{2,1,0:T(8,128)(2,1)} %copy.70), calls=%async_computation.2 | async-start | bytes 10485760 | tf_op jit(solution)/shard_map/all_to_all | solution.py:125
  336.2 16.0 %copy-start = (bf16[4,2,96,1024]{3,2,1,0:T(8,128)(2,1)S(1)}, bf16[4,2,96,1024]{3,2,1,0:T(8,128)(2,1)}, u32[]{:S(2)}) copy-start(bf16[4,2,96,1024]{3,2,1,0:T(8,128)(2,1)} %concatenate.83) | copy-start | bytes 4718596
  337.4 14.8 %collective-permute-start.10 = (bf16[2,144,1024]{2,1,0:T(8,128)(2,1)S(1)}, bf16[2,144,1024]{2,1,0:T(8,128)(2,1)S(1)}, u32[]{:S(2)}, u32[]{:S(2)}) collective-permute-start(bf16[2,144,1024]{2,1,0:T(8,128)(2,1)S(1)} %get-tuple-element.12), channel_id=1, source_target_pairs={{0,192},{32,224},{64,0},{96,32},{128,64},{160,96},{192,128},{224,1... | collective-permute-start | bytes 1769480 | tf_op jit(solution)/shard_map/ppermute | solution.py:34
  352.4 14.0 %collective-permute-start.11 = (bf16[2,144,1024]{2,1,0:T(8,128)(2,1)S(1)}, bf16[2,144,1024]{2,1,0:T(8,128)(2,1)S(1)}, u32[]{:S(2)}, u32[]{:S(2)}) collective-permute-start(bf16[2,144,1024]{2,1,0:T(8,128)(2,1)S(1)} %fusion.48), channel_id=1, source_target_pairs={{0,192},{32,224},{64,0},{96,32},{128,64},{160,96},{192,128},{224,1... | collective-permute-start | bytes 1769480 | tf_op jit(solution)/shard_map/ppermute | solution.py:34
  354.0 16.0 %collective-permute-start.7 = (bf16[2,144,1024]{2,1,0:T(8,128)(2,1)S(1)}, bf16[2,144,1024]{2,1,0:T(8,128)(2,1)S(1)}, u32[]{:S(2)}, u32[]{:S(2)}) collective-permute-start(bf16[2,144,1024]{2,1,0:T(8,128)(2,1)S(1)} %get-tuple-element.13), channel_id=1, source_target_pairs={{0,64},{32,96},{64,128},{96,160},{128,192},{160,224},{192,0},{224,... | collective-permute-start | bytes 1769480 | tf_op jit(solution)/shard_map/ppermute | solution.py:34
  366.7 14.5 %collective-permute-start.12 = (bf16[2,144,1024]{2,1,0:T(8,128)(2,1)S(1)}, bf16[2,144,1024]{2,1,0:T(8,128)(2,1)S(1)}, u32[]{:S(2)}, u32[]{:S(2)}) collective-permute-start(bf16[2,144,1024]{2,1,0:T(8,128)(2,1)S(1)} %fusion.47), channel_id=1, source_target_pairs={{0,192},{32,224},{64,0},{96,32},{128,64},{160,96},{192,128},{224,1... | collective-permute-start | bytes 1769480 | tf_op jit(solution)/shard_map/ppermute | solution.py:34
  381.6 29.2 %copy-start.4 = (bf16[2,144,1024]{2,1,0:T(8,128)(2,1)}, bf16[2,144,1024]{2,1,0:T(8,128)(2,1)S(1)}, u32[]{:S(2)}) copy-start(bf16[2,144,1024]{2,1,0:T(8,128)(2,1)S(1)} %get-tuple-element.10) | copy-start | bytes 1769476
  381.7 15.1 %collective-permute-start.8 = (bf16[2,144,1024]{2,1,0:T(8,128)(2,1)S(1)}, bf16[2,144,1024]{2,1,0:T(8,128)(2,1)S(1)}, u32[]{:S(2)}, u32[]{:S(2)}) collective-permute-start(bf16[2,144,1024]{2,1,0:T(8,128)(2,1)S(1)} %get-tuple-element.11), channel_id=1, source_target_pairs={{0,64},{32,96},{64,128},{96,160},{128,192},{160,224},{192,0},{224,... | collective-permute-start | bytes 1769480 | tf_op jit(solution)/shard_map/ppermute | solution.py:34
  397.0 13.5 %collective-permute-start.9 = (bf16[2,144,1024]{2,1,0:T(8,128)(2,1)S(1)}, bf16[2,144,1024]{2,1,0:T(8,128)(2,1)S(1)}, u32[]{:S(2)}, u32[]{:S(2)}) collective-permute-start(bf16[2,144,1024]{2,1,0:T(8,128)(2,1)S(1)} %fusion.50), channel_id=1, source_target_pairs={{0,64},{32,96},{64,128},{96,160},{128,192},{160,224},{192,0},{224,... | collective-permute-start | bytes 1769480 | tf_op jit(solution)/shard_map/ppermute | solution.py:34
  412.5 20.3 %collective-permute-start.13 = (bf16[288,1024]{1,0:T(8,128)(2,1)}, bf16[288,1024]{1,0:T(8,128)(2,1)}, u32[]{:S(2)}, u32[]{:S(2)}) collective-permute-start(bf16[288,1024]{1,0:T(8,128)(2,1)} %fusion.77), channel_id=1, source_target_pairs={{0,32},{32,0},{64,96},{96,64},{128,160},{160,128},{192,224},{224,1... | collective-permute-start | bytes 1769480 | tf_op jit(solution)/shard_map/ppermute | solution.py:41
  413.1 19.6 %copy-start.2 = (bf16[2,144,1024]{2,1,0:T(8,128)(2,1)S(1)}, bf16[2,144,1024]{2,1,0:T(8,128)(2,1)}, u32[]{:S(2)}) copy-start(bf16[2,144,1024]{2,1,0:T(8,128)(2,1)} %copy-done.1) | copy-start | bytes 1769476
  413.1 19.6 %copy-start.5 = (bf16[2,144,1024]{2,1,0:T(8,128)(2,1)S(1)}, bf16[2,144,1024]{2,1,0:T(8,128)(2,1)}, u32[]{:S(2)}) copy-start(bf16[2,144,1024]{2,1,0:T(8,128)(2,1)} %copy-done.4) | copy-start | bytes 1769476
  (15 other events, 29.6 us)

commit v7 on v6

--- a/solution.py
+++ b/solution.py
@@ -55,17 +55,18 @@
     )
 
 
-def expert_work(xr, scaled, w_gate, w_up, w_down):
-    gate = contract(xr, w_gate, (2,), (0,))
-    up = contract(xr, w_up, (2,), (0,))
+def expert_work(xr, scaled, w_gate_up, w_down):
+    hid = w_down.shape[0]
+    gate_up = contract(xr, w_gate_up, (2,), (0,))
+    gate = gate_up[..., :hid]
+    up = gate_up[..., hid:]
     sig = jax.nn.sigmoid(gate)
     act = (gate * sig * up).astype(jnp.bfloat16)
     dh = contract(scaled, w_down, (2,), (1,))
     dgate = (dh * up * sig * (1.0 + gate * (1.0 - sig))).astype(jnp.bfloat16)
     dup = (dh * gate * sig).astype(jnp.bfloat16)
-    contrib = (contract(dgate, w_gate, (2,), (1,)) + contract(dup, w_up, (2,), (1,))).astype(
-        jnp.bfloat16
-    )
+    dboth = jnp.concatenate([dgate, dup], axis=2)
+    contrib = contract(dboth, w_gate_up, (2,), (1,)).astype(jnp.bfloat16)
     grad_g = contract(xr, dgate, (0, 1), (0, 1)).astype(jnp.bfloat16)
     grad_u = contract(xr, dup, (0, 1), (0, 1)).astype(jnp.bfloat16)
     grad_d = contract(act, scaled, (0, 1), (0, 1)).astype(jnp.bfloat16)
@@ -99,6 +100,7 @@
     zeros = jnp.zeros_like(sel[:, 0])
     ones = jnp.ones((n_owner, slots), jnp.float32)
 
+    w_gate_up = jnp.concatenate([gate_weight, up_weight], axis=2)
     contribs = []
     grads = []
     after = None
@@ -115,7 +117,7 @@
         xr = recv[:, :slots]
         scaled = recv[:, slots:]
         contrib, grad_g, grad_u, grad_d = expert_work(
-            xr, scaled, gate_weight[local], up_weight[local], down_weight[local]
+            xr, scaled, w_gate_up[local], down_weight[local]
         )
         reduced = dp_reduce_scatter(pack_grads(grad_g, grad_u, grad_d, n_dp), n_dp)
         after = (contrib, reduced)

time: 447 us -> 448 us (level)
  local copies, waits for them, and re-layouts: 26.5 us -> 33.7 us
  waiting for transfers between devices: 271 us -> 264 us
    all_to_all x2, waiting for transfers between devices: 114 us -> 109 us  [per_device(): lax.all_to_all(send, 'expert', split_axis=0, concat_axis=0, tiled=True)]
    dot_general x20 -> x16, matrix products: 69.2 us -> 68 us  [contract(): lax.dot_general(left, right, ((left_dims, right_dims), ((), ())), preferr...]
  transfers between devices with their start and end apart: 17 -> 17, of which waited for: 13 -> 13; matrix products, arithmetic and copies ran while one was open for 19% -> 20% of each run, Pallas kernels for 0% -> 0%
where the time goes in v7:
time: 448 us; the launch traced here: 442 us
  waiting for transfers between devices  264 us (59%)
  matrix products  68 us (15%)
  starting transfers between devices  51.2 us (11%)
  local copies, waits for them, and re-layouts  33.7 us (8%)
  other arithmetic  23.1 us (5%)
    ppermute x12, waiting for transfers between devices, dp_reduce_scatter(): recv = lax.ppermute(send[h], 'dp', perms[h])  132 us
    all_to_all x2, waiting for transfers between devices, per_device(): lax.all_to_all(send, 'expert', split_axis=0, concat_axis=0, tiled=True)  109 us
    dot_general x16, matrix products, contract(): lax.dot_general(left, right, ((left_dims, right_dims), ((), ())), preferr...  68 us
    ppermute x2, waiting for transfers between devices, dp_reduce_scatter(): got = lax.ppermute(give, 'dp', [(d, d ^ 1) for d in range(n_dp)])  23.6 us
    all_to_all x2, starting transfers between devices, per_device(): lax.all_to_all(send, 'expert', split_axis=0, concat_axis=0, tiled=True)  21.6 us
    concatenate x6, local copies, waits for them, and re-layouts, pack_grads(): jnp.concatenate([grad_g.reshape(n_dp, dsl * hid // lanes, lanes), grad_u....  16.5 us
    ppermute x12, starting transfers between devices, dp_reduce_scatter(): recv = lax.ppermute(send[h], 'dp', perms[h])  14.6 us
    all_to_all x1, starting transfers between devices, per_device(): lax.all_to_all(jnp.concatenate(contribs, axis=1), 'expert', split_axis=0,...  13.9 us
  transfers between devices with their start and end apart: 17, of which 13 were waited for; matrix products, arithmetic and copies ran while one was open for 20% of the time, Pallas kernels for 0%

profile of v7, /device:TPU:1, one launch (start us, length us, event | category | flops | bytes accessed | tf_op | source)
XLA Modules:
  0.0 442.1 jit_solution(7170131609103692980)
XLA Ops:
  3.1 3.9 multiply_convert_fusion.1
  7.0 12.9 %all-to-all-start = ((bf16[32,36,2048]{2,1,0:T(8,128)(2,1)}), bf16[32,36,2048]{2,1,0:T(8,128)(2,1)}, u32[]{:S(2)}, u32[]{:S(2)}) async-start(bf16[32,36,2048]{2,1,0:T(8,128)(2,1)} %multiply_convert_fusion.1), calls=%async_computation | async-start | bytes 10485760 | tf_op jit(solution)/shard_map/all_to_all | solution.py:114
  25.2 3.8 multiply_convert_fusion
  29.1 109.3 %all-to-all-done = bf16[32,36,2048]{2,1,0:T(8,128)(2,1)} async-done(((bf16[32,36,2048]{2,1,0:T(8,128)(2,1)}), bf16[32,36,2048]{2,1,0:T(8,128)(2,1)}, u32[]{:S(2)}, u32[]{:S(2)}) %all-to-all-start) | async-done | bytes 4718624 | tf_op jit(solution)/shard_map/all_to_all | solution.py:114
  138.4 8.7 %all-to-all-start.1 = ((bf16[32,36,2048]{2,1,0:T(8,128)(2,1)}), bf16[32,36,2048]{2,1,0:T(8,128)(2,1)}, u32[]{:S(2)}, u32[]{:S(2)}) async-start(bf16[32,36,2048]{2,1,0:T(8,128)(2,1)} %multiply_convert_fusion), calls=%async_computation.1 | async-start | bytes 10485760 | tf_op jit(solution)/shard_map/all_to_all | solution.py:114
  147.2 5.6 %fusion = f32[32,18,768]{2,1,0:T(8,128)S(1)} fusion(bf16[2,2048,768]{2,1,0:T(8,128)(2,1)} %copy-done.9, bf16[32,36,2048]{2,1,0:T(8,128)(2,1)} %all-to-all-done), kind=kOutput, calls=%fused_computation.13 | convolution fusion | flops 1811939328 | bytes 8060928 | tf_op jit(solution)/shard_map/dot_general | solution.py:8
  152.8 5.7 %multiply_convert_fusion.7 = (bf16[32,18,384]{2,1,0:T(8,128)(2,1)}, bf16[32,18,384]{2,1,0:T(8,128)(2,1)S(1)}) fusion(f32[32,18,768]{2,1,0:T(8,128)S(1)} %fusion, bf16[2,384,2048]{2,1,0:T(8,128)(2,1)S(1)} %copy-done.20, bf16[32,36,2048]{2,1,0:T(8,128)(2,1)} %all-to-all-done), kind=kOutput, calls=%fused_computation.115 | convolution fusion | flops 908845056 | bytes 7962624 | tf_op jit(solution)/shard_map/dot_general | solution.py:8
  159.3 3.7 bitcast_convert_fusion.4
  164.9 5.1 %bitcast_convert_fusion.5 = bf16[2048,384]{1,0:T(8,128)(2,1)} fusion(bf16[32,18,384]{2,1,0:T(8,128)(2,1)} %get-tuple-element.8, bf16[32,36,2048]{2,1,0:T(8,128)(2,1)} %all-to-all-done), kind=kOutput, calls=%fused_computation.10 | convolution fusion | flops 906756096 | bytes 5308416 | tf_op jit(solution)/shard_map/dot_general | solution.py:8
  173.5 4.2 bitcast_convert_fusion.3
  179.7 3.7 concatenate.87
  188.2 12.9 %collective-permute-done.3 = bf16[2,144,1024]{2,1,0:T(8,128)(2,1)} collective-permute-done((bf16[2,144,1024]{2,1,0:T(8,128)(2,1)}, bf16[2,144,1024]{2,1,0:T(8,128)(2,1)}, u32[]{:S(2)}, u32[]{:S(2)}) %collective-permute-start.3) | collective-permute-done | bytes 589856 | tf_op jit(solution)/shard_map/ppermute | solution.py:34
  206.8 12.0 %collective-permute-done.4 = bf16[2,144,1024]{2,1,0:T(8,128)(2,1)} collective-permute-done((bf16[2,144,1024]{2,1,0:T(8,128)(2,1)}, bf16[2,144,1024]{2,1,0:T(8,128)(2,1)}, u32[]{:S(2)}, u32[]{:S(2)}) %collective-permute-start.4) | collective-permute-done | bytes 589856 | tf_op jit(solution)/shard_map/ppermute | solution.py:34
  224.4 11.2 %collective-permute-done.5 = bf16[2,144,1024]{2,1,0:T(8,128)(2,1)} collective-permute-done((bf16[2,144,1024]{2,1,0:T(8,128)(2,1)}, bf16[2,144,1024]{2,1,0:T(8,128)(2,1)}, u32[]{:S(2)}, u32[]{:S(2)}) %collective-permute-start.5) | collective-permute-done | bytes 589856 | tf_op jit(solution)/shard_map/ppermute | solution.py:34
  238.4 14.7 %collective-permute-done.1 = bf16[2,144,1024]{2,1,0:T(8,128)(2,1)} collective-permute-done((bf16[2,144,1024]{2,1,0:T(8,128)(2,1)}, bf16[2,144,1024]{2,1,0:T(8,128)(2,1)}, u32[]{:S(2)}, u32[]{:S(2)}) %collective-permute-start.1) | collective-permute-done | bytes 589856 | tf_op jit(solution)/shard_map/ppermute | solution.py:34
  255.3 13.1 %collective-permute-done.2 = bf16[2,144,1024]{2,1,0:T(8,128)(2,1)} collective-permute-done((bf16[2,144,1024]{2,1,0:T(8,128)(2,1)}, bf16[2,144,1024]{2,1,0:T(8,128)(2,1)}, u32[]{:S(2)}, u32[]{:S(2)}) %collective-permute-start.2) | collective-permute-done | bytes 589856 | tf_op jit(solution)/shard_map/ppermute | solution.py:34
  271.1 3.9 convolution_convert_fusion.1
  275.0 5.9 %collective-permute-done.6 = bf16[288,1024]{1,0:T(8,128)(2,1)S(1)} collective-permute-done((bf16[288,1024]{1,0:T(8,128)(2,1)S(1)}, bf16[288,1024]{1,0:T(8,128)(2,1)S(1)}, u32[]{:S(2)}, u32[]{:S(2)}) %collective-permute-start.6) | collective-permute-done | bytes 589856 | tf_op jit(solution)/shard_map/ppermute | solution.py:41
  281.9 5.6 %fusion.1 = f32[32,18,768]{2,1,0:T(8,128)S(1)} fusion(bf16[2,2048,768]{2,1,0:T(8,128)(2,1)} %copy-done.9, bf16[32,36,2048]{2,1,0:T(8,128)(2,1)} %all-to-all-done.1), kind=kOutput, calls=%fused_computation.14 | convolution fusion | flops 1811939328 | bytes 8060928 | tf_op jit(solution)/shard_map/dot_general | solution.py:8
  287.5 5.0 %multiply_convert_fusion.4 = (bf16[32,18,384]{2,1,0:T(8,128)(2,1)S(1)}, bf16[32,18,384]{2,1,0:T(8,128)(2,1)S(1)}) fusion(f32[32,18,768]{2,1,0:T(8,128)S(1)} %fusion.1, bf16[2,384,2048]{2,1,0:T(8,128)(2,1)S(1)} %copy-done.21, bf16[32,36,2048]{2,1,0:T(8,128)(2,1)} %all-to-all-done.1), kind=kOutput, calls=%fused_computation.111 | convolution fusion | flops 908845056 | bytes 7962624 | tf_op jit(solution)/shard_map/dot_general | solution.py:8
  292.7 4.2 convolution_convert_fusion
  297.3 4.9 %copy.74 = bf16[32,36,2048]{2,1,0:T(8,128)(2,1)} copy(bf16[32,36,2048]{2,0,1:T(8,128)(2,1)S(1)} %pad_maximum_fusion) | data formatting | bytes 9437184 | tf_op jit(solution)/shard_map/concatenate | solution.py:128
  302.2 13.9 %all-to-all-start.2 = ((bf16[32,36,2048]{2,1,0:T(8,128)(2,1)}), bf16[32,36,2048]{2,1,0:T(8,128)(2,1)}, u32[]{:S(2)}, u32[]{:S(2)}) async-start(bf16[32,36,2048]{2,1,0:T(8,128)(2,1)} %copy.74), calls=%async_computation.2 | async-start | bytes 10485760 | tf_op jit(solution)/shard_map/all_to_all | solution.py:127
  321.7 4.2 bitcast_convert_fusion
  329.0 5.0 %bitcast_convert_fusion.1 = bf16[2048,384]{1,0:T(8,128)(2,1)} fusion(bf16[32,18,384]{2,1,0:T(8,128)(2,1)} %copy-done.13, bf16[32,36,2048]{2,1,0:T(8,128)(2,1)} %all-to-all-done.1), kind=kOutput, calls=%fused_computation.6 | convolution fusion | flops 906756096 | bytes 5308416 | tf_op jit(solution)/shard_map/dot_general | solution.py:8
  338.6 14.9 %collective-permute-done.10 = bf16[2,144,1024]{2,1,0:T(8,128)(2,1)S(1)} collective-permute-done((bf16[2,144,1024]{2,1,0:T(8,128)(2,1)S(1)}, bf16[2,144,1024]{2,1,0:T(8,128)(2,1)S(1)}, u32[]{:S(2)}, u32[]{:S(2)}) %collective-permute-start.10) | collective-permute-done | bytes 589856 | tf_op jit(solution)/shard_map/ppermute | solution.py:34
  355.3 12.6 %collective-permute-done.11 = bf16[2,144,1024]{2,1,0:T(8,128)(2,1)S(1)} collective-permute-done((bf16[2,144,1024]{2,1,0:T(8,128)(2,1)S(1)}, bf16[2,144,1024]{2,1,0:T(8,128)(2,1)S(1)}, u32[]{:S(2)}, u32[]{:S(2)}) %collective-permute-start.11) | collective-permute-done | bytes 589856 | tf_op jit(solution)/shard_map/ppermute | solution.py:34
  371.4 11.3 %collective-permute-done.12 = bf16[2,144,1024]{2,1,0:T(8,128)(2,1)S(1)} collective-permute-done((bf16[2,144,1024]{2,1,0:T(8,128)(2,1)S(1)}, bf16[2,144,1024]{2,1,0:T(8,128)(2,1)S(1)}, u32[]{:S(2)}, u32[]{:S(2)}) %collective-permute-start.12) | collective-permute-done | bytes 589856 | tf_op jit(solution)/shard_map/ppermute | solution.py:34
  383.3 15.2 %collective-permute-done.8 = bf16[2,144,1024]{2,1,0:T(8,128)(2,1)S(1)} collective-permute-done((bf16[2,144,1024]{2,1,0:T(8,128)(2,1)S(1)}, bf16[2,144,1024]{2,1,0:T(8,128)(2,1)S(1)}, u32[]{:S(2)}, u32[]{:S(2)}) %collective-permute-start.8) | collective-permute-done | bytes 589856 | tf_op jit(solution)/shard_map/ppermute | solution.py:34
  398.9 13.6 %collective-permute-done.9 = bf16[2,144,1024]{2,1,0:T(8,128)(2,1)S(1)} collective-permute-done((bf16[2,144,1024]{2,1,0:T(8,128)(2,1)S(1)}, bf16[2,144,1024]{2,1,0:T(8,128)(2,1)S(1)}, u32[]{:S(2)}, u32[]{:S(2)}) %collective-permute-start.9) | collective-permute-done | bytes 589856 | tf_op jit(solution)/shard_map/ppermute | solution.py:34
  416.2 17.7 %collective-permute-done.13 = bf16[288,1024]{1,0:T(8,128)(2,1)} collective-permute-done((bf16[288,1024]{1,0:T(8,128)(2,1)}, bf16[288,1024]{1,0:T(8,128)(2,1)}, u32[]{:S(2)}, u32[]{:S(2)}) %collective-permute-start.13) | collective-permute-done | bytes 589856 | tf_op jit(solution)/shard_map/ppermute | solution.py:41
  437.7 4.3 fusion.8
  (133 shorter events, 67.8 us)
Async XLA Ops:
  7.0 13.0 %copy-start.6 = (bf16[2,2048,384]{2,1,0:T(8,128)(2,1)S(1)}, bf16[2,2048,384]{2,1,0:T(8,128)(2,1)}, u32[]{:S(2)}) copy-start(bf16[2,2048,384]{2,1,0:T(8,128)(2,1)} %param.11) | copy-start | bytes 9437188
  7.0 131.4 %all-to-all-start = ((bf16[32,36,2048]{2,1,0:T(8,128)(2,1)}), bf16[32,36,2048]{2,1,0:T(8,128)(2,1)}, u32[]{:S(2)}, u32[]{:S(2)}) async-start(bf16[32,36,2048]{2,1,0:T(8,128)(2,1)} %multiply_convert_fusion.1), calls=%async_computation | async-start | bytes 10485760 | tf_op jit(solution)/shard_map/all_to_all | solution.py:114
  21.9 3.3 copy-start.23
  21.9 3.3 copy-start.25
  138.4 143.5 %all-to-all-start.1 = ((bf16[32,36,2048]{2,1,0:T(8,128)(2,1)}), bf16[32,36,2048]{2,1,0:T(8,128)(2,1)}, u32[]{:S(2)}, u32[]{:S(2)}) async-start(bf16[32,36,2048]{2,1,0:T(8,128)(2,1)} %multiply_convert_fusion), calls=%async_computation.1 | async-start | bytes 10485760 | tf_op jit(solution)/shard_map/all_to_all | solution.py:114
  147.2 5.6 %copy-start.20 = (bf16[2,384,2048]{2,1,0:T(8,128)(2,1)S(1)}, bf16[2,384,2048]{2,1,0:T(8,128)(2,1)}, u32[]{:S(2)}) copy-start(bf16[2,384,2048]{2,1,0:T(8,128)(2,1)} %param.13) | copy-start | bytes 9437188
  152.8 5.7 %copy-start.27 = (f32[32,18,768]{2,1,0:T(8,128)}, f32[32,18,768]{2,1,0:T(8,128)S(1)}, u32[]{:S(2)}) copy-start(f32[32,18,768]{2,1,0:T(8,128)S(1)} %fusion) | copy-start | bytes 5308420
  185.5 15.6 %collective-permute-start.3 = (bf16[2,144,1024]{2,1,0:T(8,128)(2,1)}, bf16[2,144,1024]{2,1,0:T(8,128)(2,1)}, u32[]{:S(2)}, u32[]{:S(2)}) collective-permute-start(bf16[2,144,1024]{2,1,0:T(8,128)(2,1)} %get-tuple-element.16), channel_id=1, source_target_pairs={{0,192},{32,224},{64,0},{96,32},{128,64},{160,96},{192,128},{224,1... | collective-permute-start | bytes 1769480 | tf_op jit(solution)/shard_map/ppermute | solution.py:34
  203.3 15.4 %collective-permute-start.4 = (bf16[2,144,1024]{2,1,0:T(8,128)(2,1)}, bf16[2,144,1024]{2,1,0:T(8,128)(2,1)}, u32[]{:S(2)}, u32[]{:S(2)}) collective-permute-start(bf16[2,144,1024]{2,1,0:T(8,128)(2,1)} %fusion.33), channel_id=1, source_target_pairs={{0,192},{32,224},{64,0},{96,32},{128,64},{160,96},{192,128},{224,1... | collective-permute-start | bytes 1769480 | tf_op jit(solution)/shard_map/ppermute | solution.py:34
  206.8 17.7 %collective-permute-start = (bf16[2,144,1024]{2,1,0:T(8,128)(2,1)}, bf16[2,144,1024]{2,1,0:T(8,128)(2,1)}, u32[]{:S(2)}, u32[]{:S(2)}) collective-permute-start(bf16[2,144,1024]{2,1,0:T(8,128)(2,1)} %get-tuple-element.17), channel_id=1, source_target_pairs={{0,64},{32,96},{64,128},{96,160},{128,192},{160,224},{192,0},{224,... | collective-permute-start | bytes 1769480 | tf_op jit(solution)/shard_map/ppermute | solution.py:34
  221.0 14.6 %collective-permute-start.5 = (bf16[2,144,1024]{2,1,0:T(8,128)(2,1)}, bf16[2,144,1024]{2,1,0:T(8,128)(2,1)}, u32[]{:S(2)}, u32[]{:S(2)}) collective-permute-start(bf16[2,144,1024]{2,1,0:T(8,128)(2,1)} %fusion.32), channel_id=1, source_target_pairs={{0,192},{32,224},{64,0},{96,32},{128,64},{160,96},{192,128},{224,1... | collective-permute-start | bytes 1769480 | tf_op jit(solution)/shard_map/ppermute | solution.py:34
  238.4 14.7 %collective-permute-start.1 = (bf16[2,144,1024]{2,1,0:T(8,128)(2,1)}, bf16[2,144,1024]{2,1,0:T(8,128)(2,1)}, u32[]{:S(2)}, u32[]{:S(2)}) collective-permute-start(bf16[2,144,1024]{2,1,0:T(8,128)(2,1)} %get-tuple-element.15), channel_id=1, source_target_pairs={{0,64},{32,96},{64,128},{96,160},{128,192},{160,224},{192,0},{224,... | collective-permute-start | bytes 1769480 | tf_op jit(solution)/shard_map/ppermute | solution.py:34
  255.3 13.1 %collective-permute-start.2 = (bf16[2,144,1024]{2,1,0:T(8,128)(2,1)}, bf16[2,144,1024]{2,1,0:T(8,128)(2,1)}, u32[]{:S(2)}, u32[]{:S(2)}) collective-permute-start(bf16[2,144,1024]{2,1,0:T(8,128)(2,1)} %fusion.35), channel_id=1, source_target_pairs={{0,64},{32,96},{64,128},{96,160},{128,192},{160,224},{192,0},{224,... | collective-permute-start | bytes 1769480 | tf_op jit(solution)/shard_map/ppermute | solution.py:34
  255.3 14.4 %copy-start.3 = (bf16[2,144,1024]{2,1,0:T(8,128)(2,1)S(1)}, bf16[2,144,1024]{2,1,0:T(8,128)(2,1)}, u32[]{:S(2)}) copy-start(bf16[2,144,1024]{2,1,0:T(8,128)(2,1)} %get-tuple-element.14) | copy-start | bytes 1769476
  269.8 11.1 %collective-permute-start.6 = (bf16[288,1024]{1,0:T(8,128)(2,1)S(1)}, bf16[288,1024]{1,0:T(8,128)(2,1)S(1)}, u32[]{:S(2)}, u32[]{:S(2)}) collective-permute-start(bf16[288,1024]{1,0:T(8,128)(2,1)S(1)} %fusion.61), channel_id=1, source_target_pairs={{0,32},{32,0},{64,96},{96,64},{128,160},{160,128},{192,224},{224,1... | collective-permute-start | bytes 1769480 | tf_op jit(solution)/shard_map/ppermute | solution.py:41
  281.9 5.6 %copy-start.21 = (bf16[2,384,2048]{2,1,0:T(8,128)(2,1)S(1)}, bf16[2,384,2048]{2,1,0:T(8,128)(2,1)}, u32[]{:S(2)}) copy-start(bf16[2,384,2048]{2,1,0:T(8,128)(2,1)} %param.13) | copy-start | bytes 9437188
  287.5 5.0 %copy-start.26 = (f32[32,18,768]{2,1,0:T(8,128)}, f32[32,18,768]{2,1,0:T(8,128)S(1)}, u32[]{:S(2)}) copy-start(f32[32,18,768]{2,1,0:T(8,128)S(1)} %fusion.1) | copy-start | bytes 5308420
  292.5 4.4 copy-start.13
  292.5 4.4 copy-start.14
  302.2 13.9 %copy-start.15 = (bf16[32,18,384]{2,1,0:T(8,128)(2,1)S(1)}, bf16[32,18,384]{2,1,0:T(8,128)(2,1)}, u32[]{:S(2)}) copy-start(bf16[32,18,384]{2,1,0:T(8,128)(2,1)} %copy-done.14) | copy-start | bytes 1327108
  302.2 135.4 %all-to-all-start.2 = ((bf16[32,36,2048]{2,1,0:T(8,128)(2,1)}), bf16[32,36,2048]{2,1,0:T(8,128)(2,1)}, u32[]{:S(2)}, u32[]{:S(2)}) async-start(bf16[32,36,2048]{2,1,0:T(8,128)(2,1)} %copy.74), calls=%async_computation.2 | async-start | bytes 10485760 | tf_op jit(solution)/shard_map/all_to_all | solution.py:127
  337.3 16.2 %copy-start = (bf16[4,2,96,1024]{3,2,1,0:T(8,128)(2,1)S(1)}, bf16[4,2,96,1024]{3,2,1,0:T(8,128)(2,1)}, u32[]{:S(2)}) copy-start(bf16[4,2,96,1024]{3,2,1,0:T(8,128)(2,1)} %concatenate.95) | copy-start | bytes 4718596
  338.6 14.9 %collective-permute-start.10 = (bf16[2,144,1024]{2,1,0:T(8,128)(2,1)S(1)}, bf16[2,144,1024]{2,1,0:T(8,128)(2,1)S(1)}, u32[]{:S(2)}, u32[]{:S(2)}) collective-permute-start(bf16[2,144,1024]{2,1,0:T(8,128)(2,1)S(1)} %get-tuple-element.12), channel_id=1, source_target_pairs={{0,192},{32,224},{64,0},{96,32},{128,64},{160,96},{192,128},{224,1... | collective-permute-start | bytes 1769480 | tf_op jit(solution)/shard_map/ppermute | solution.py:34
  353.7 14.2 %collective-permute-start.11 = (bf16[2,144,1024]{2,1,0:T(8,128)(2,1)S(1)}, bf16[2,144,1024]{2,1,0:T(8,128)(2,1)S(1)}, u32[]{:S(2)}, u32[]{:S(2)}) collective-permute-start(bf16[2,144,1024]{2,1,0:T(8,128)(2,1)S(1)} %fusion.26), channel_id=1, source_target_pairs={{0,192},{32,224},{64,0},{96,32},{128,64},{160,96},{192,128},{224,1... | collective-permute-start | bytes 1769480 | tf_op jit(solution)/shard_map/ppermute | solution.py:34
  355.3 16.1 %collective-permute-start.7 = (bf16[2,144,1024]{2,1,0:T(8,128)(2,1)S(1)}, bf16[2,144,1024]{2,1,0:T(8,128)(2,1)S(1)}, u32[]{:S(2)}, u32[]{:S(2)}) collective-permute-start(bf16[2,144,1024]{2,1,0:T(8,128)(2,1)S(1)} %get-tuple-element.13), channel_id=1, source_target_pairs={{0,64},{32,96},{64,128},{96,160},{128,192},{160,224},{192,0},{224,... | collective-permute-start | bytes 1769480 | tf_op jit(solution)/shard_map/ppermute | solution.py:34
  368.2 14.6 %collective-permute-start.12 = (bf16[2,144,1024]{2,1,0:T(8,128)(2,1)S(1)}, bf16[2,144,1024]{2,1,0:T(8,128)(2,1)S(1)}, u32[]{:S(2)}, u32[]{:S(2)}) collective-permute-start(bf16[2,144,1024]{2,1,0:T(8,128)(2,1)S(1)} %fusion.25), channel_id=1, source_target_pairs={{0,192},{32,224},{64,0},{96,32},{128,64},{160,96},{192,128},{224,1... | collective-permute-start | bytes 1769480 | tf_op jit(solution)/shard_map/ppermute | solution.py:34
  383.2 29.5 %copy-start.4 = (bf16[2,144,1024]{2,1,0:T(8,128)(2,1)}, bf16[2,144,1024]{2,1,0:T(8,128)(2,1)S(1)}, u32[]{:S(2)}) copy-start(bf16[2,144,1024]{2,1,0:T(8,128)(2,1)S(1)} %get-tuple-element.10) | copy-start | bytes 1769476
  383.2 15.3 %collective-permute-start.8 = (bf16[2,144,1024]{2,1,0:T(8,128)(2,1)S(1)}, bf16[2,144,1024]{2,1,0:T(8,128)(2,1)S(1)}, u32[]{:S(2)}, u32[]{:S(2)}) collective-permute-start(bf16[2,144,1024]{2,1,0:T(8,128)(2,1)S(1)} %get-tuple-element.11), channel_id=1, source_target_pairs={{0,64},{32,96},{64,128},{96,160},{128,192},{160,224},{192,0},{224,... | collective-permute-start | bytes 1769480 | tf_op jit(solution)/shard_map/ppermute | solution.py:34
  398.8 13.7 %collective-permute-start.9 = (bf16[2,144,1024]{2,1,0:T(8,128)(2,1)S(1)}, bf16[2,144,1024]{2,1,0:T(8,128)(2,1)S(1)}, u32[]{:S(2)}, u32[]{:S(2)}) collective-permute-start(bf16[2,144,1024]{2,1,0:T(8,128)(2,1)S(1)} %fusion.28), channel_id=1, source_target_pairs={{0,64},{32,96},{64,128},{96,160},{128,192},{160,224},{192,0},{224,... | collective-permute-start | bytes 1769480 | tf_op jit(solution)/shard_map/ppermute | solution.py:34
  414.4 19.5 %collective-permute-start.13 = (bf16[288,1024]{1,0:T(8,128)(2,1)}, bf16[288,1024]{1,0:T(8,128)(2,1)}, u32[]{:S(2)}, u32[]{:S(2)}) collective-permute-start(bf16[288,1024]{1,0:T(8,128)(2,1)} %fusion.57), channel_id=1, source_target_pairs={{0,32},{32,0},{64,96},{96,64},{128,160},{160,128},{192,224},{224,1... | collective-permute-start | bytes 1769480 | tf_op jit(solution)/shard_map/ppermute | solution.py:41
  415.1 18.8 %copy-start.2 = (bf16[2,144,1024]{2,1,0:T(8,128)(2,1)S(1)}, bf16[2,144,1024]{2,1,0:T(8,128)(2,1)}, u32[]{:S(2)}) copy-start(bf16[2,144,1024]{2,1,0:T(8,128)(2,1)} %copy-done.1) | copy-start | bytes 1769476
  415.1 18.8 %copy-start.5 = (bf16[2,144,1024]{2,1,0:T(8,128)(2,1)S(1)}, bf16[2,144,1024]{2,1,0:T(8,128)(2,1)}, u32[]{:S(2)}) copy-start(bf16[2,144,1024]{2,1,0:T(8,128)(2,1)} %copy-done.4) | copy-start | bytes 1769476
  (13 other events, 20.3 us)

commit v8 on v6

--- a/solution.py
+++ b/solution.py
@@ -17,25 +17,17 @@
     y_pos = me // 2
     x_lo = me % 2
     by_y = packed.reshape(n_y, 2, n_r, lanes)
-    half = n_r // 2
-    halves = (by_y[:, :, :half], by_y[:, :, half:])
-    steps = (1, -1)
-    perms = [
-        [(y * 2 + b, ((y + st) % n_y) * 2 + b) for y in range(n_y) for b in range(2)]
-        for st in steps
-    ]
+    perm = [(y * 2 + b, ((y + 1) % n_y) * 2 + b) for y in range(n_y) for b in range(2)]
 
-    def own(h, c):
-        return lax.dynamic_index_in_dim(halves[h], c % n_y, axis=0, keepdims=False)
+    def own(c):
+        return lax.dynamic_index_in_dim(by_y, c % n_y, axis=0, keepdims=False)
 
-    send = [own(h, y_pos - steps[h]) for h in range(2)]
+    send = own(y_pos - 1)
     for s in range(n_y - 1):
-        for h in range(2):
-            recv = lax.ppermute(send[h], "dp", perms[h])
-            chunk = y_pos - steps[h] * (s + 2)
-            acc = recv.astype(jnp.float32) + own(h, chunk).astype(jnp.float32)
-            send[h] = acc.astype(jnp.bfloat16)
-    both = jnp.concatenate(send, axis=1)
+        recv = lax.ppermute(send, "dp", perm)
+        acc = recv.astype(jnp.float32) + own(y_pos - (s + 2)).astype(jnp.float32)
+        send = acc.astype(jnp.bfloat16)
+    both = send
     keep = lax.dynamic_index_in_dim(both, x_lo, axis=0, keepdims=False)
     give = lax.dynamic_index_in_dim(both, 1 - x_lo, axis=0, keepdims=False)
     got = lax.ppermute(give, "dp", [(d, d ^ 1) for d in range(n_dp)])

time: 447 us -> 469 us (1.049)
  waiting for transfers between devices: 271 us -> 305 us
  starting transfers between devices: 49.9 us -> 36.8 us
  other arithmetic: 23.1 us -> 13.1 us
  local copies, waits for them, and re-layouts: 26.5 us -> 34.5 us
    ppermute x12 -> x6, waiting for transfers between devices: 131 us -> 167 us  [dp_reduce_scatter(): recv = lax.ppermute(send, 'dp', perm)]
    ppermute x12 -> x6, starting transfers between devices: 14.7 us -> 1.79 us  [dp_reduce_scatter(): recv = lax.ppermute(send, 'dp', perm)]
    convert_element_type x10 -> x6, other arithmetic: 12.3 us -> 6.6 us  [dp_reduce_scatter(): send = acc.astype(jnp.bfloat16)]
    concatenate x6 -> x8, local copies, waits for them, and re-layouts: 15.2 us -> 18.2 us  [pack_grads(): jnp.concatenate([grad_g.reshape(n_dp, dsl * hid // lanes, lanes), grad_u....]
  transfers between devices with their start and end apart: 17 -> 11, of which waited for: 13 -> 9; matrix products, arithmetic and copies ran while one was open for 19% -> 15% of each run, Pallas kernels for 0% -> 0%
where the time goes in v8:
time: 469 us; the launch traced here: 462 us
  waiting for transfers between devices  305 us (65%)
  matrix products  70.6 us (15%)
  starting transfers between devices  36.8 us (8%)
  local copies, waits for them, and re-layouts  34.5 us (7%)
  other arithmetic  13.1 us (3%)
    ppermute x6, waiting for transfers between devices, dp_reduce_scatter(): recv = lax.ppermute(send, 'dp', perm)  167 us
    all_to_all x2, waiting for transfers between devices, per_device(): lax.all_to_all(send, 'expert', split_axis=0, concat_axis=0, tiled=True)  114 us
    dot_general x20, matrix products, contract(): lax.dot_general(left, right, ((left_dims, right_dims), ((), ())), preferr...  70.6 us
    ppermute x2, waiting for transfers between devices, dp_reduce_scatter(): got = lax.ppermute(give, 'dp', [(d, d ^ 1) for d in range(n_dp)])  24.4 us
    all_to_all x2, starting transfers between devices, per_device(): lax.all_to_all(send, 'expert', split_axis=0, concat_axis=0, tiled=True)  21.1 us
    concatenate x8, local copies, waits for them, and re-layouts, pack_grads(): jnp.concatenate([grad_g.reshape(n_dp, dsl * hid // lanes, lanes), grad_u....  18.2 us
    all_to_all x1, starting transfers between devices, per_device(): lax.all_to_all(jnp.concatenate(contribs, axis=1), 'expert', split_axis=0,...  12.5 us
  transfers between devices with their start and end apart: 11, of which 9 were waited for; matrix products, arithmetic and copies ran while one was open for 15% of the time, Pallas kernels for 0%

profile of v8, /device:TPU:1, one launch (start us, length us, event | category | flops | bytes accessed | tf_op | source)
XLA Modules:
  0.0 462.1 jit_solution(11727644320824322710)
XLA Ops:
  3.1 3.9 multiply_convert_fusion.1
  7.0 12.6 %all-to-all-start = ((bf16[32,36,2048]{2,1,0:T(8,128)(2,1)}), bf16[32,36,2048]{2,1,0:T(8,128)(2,1)}, u32[]{:S(2)}, u32[]{:S(2)}) async-start(bf16[32,36,2048]{2,1,0:T(8,128)(2,1)} %multiply_convert_fusion.1), calls=%async_computation | async-start | bytes 10485760 | tf_op jit(solution)/shard_map/all_to_all | solution.py:104
  19.7 3.9 multiply_convert_fusion
  23.7 114.5 %all-to-all-done = bf16[32,36,2048]{2,1,0:T(8,128)(2,1)} async-done(((bf16[32,36,2048]{2,1,0:T(8,128)(2,1)}), bf16[32,36,2048]{2,1,0:T(8,128)(2,1)}, u32[]{:S(2)}, u32[]{:S(2)}) %all-to-all-start) | async-done | bytes 4718624 | tf_op jit(solution)/shard_map/all_to_all | solution.py:104
  138.1 8.5 %all-to-all-start.1 = ((bf16[32,36,2048]{2,1,0:T(8,128)(2,1)}), bf16[32,36,2048]{2,1,0:T(8,128)(2,1)}, u32[]{:S(2)}, u32[]{:S(2)}) async-start(bf16[32,36,2048]{2,1,0:T(8,128)(2,1)} %multiply_convert_fusion), calls=%async_computation.1 | async-start | bytes 10485760 | tf_op jit(solution)/shard_map/all_to_all | solution.py:104
  146.7 3.9 fusion.15
  150.6 3.7 fusion.17
  154.3 3.6 bitcast_convert_fusion.3
  158.0 5.1 %multiply_convert_fusion.6 = (bf16[32,18,384]{2,1,0:T(8,128)(2,1)}, bf16[32,18,384]{2,1,0:T(8,128)(2,1)}) fusion(f32[32,18,384]{2,1,0:T(8,128)S(1)} %fusion.15, f32[32,18,384]{2,1,0:T(8,128)S(1)} %fusion.17, bf16[2,384,2048]{2,1,0:T(8,128)(2,1)S(1)} %copy-done.19, bf16[32,36,2048]{2,1,0:T(8,128)(2,1)} %all-to-all-done), kind=kOutput, calls=%fused_computation.82 | convolution fusion | flops 908845056 | bytes 7962624 | tf_op jit(solution)/shard_map/dot_general | solution.py:8
  164.8 5.0 %bitcast_convert_fusion.5 = bf16[2048,384]{1,0:T(8,128)(2,1)} fusion(bf16[32,18,384]{2,1,0:T(8,128)(2,1)} %get-tuple-element.9, bf16[32,36,2048]{2,1,0:T(8,128)(2,1)} %all-to-all-done), kind=kOutput, calls=%fused_computation.10 | convolution fusion | flops 906756096 | bytes 5308416 | tf_op jit(solution)/shard_map/dot_general | solution.py:8
  169.8 3.6 concatenate.59
  173.5 5.0 %bitcast_convert_fusion.4 = bf16[2048,384]{1,0:T(8,128)(2,1)} fusion(bf16[32,18,384]{2,1,0:T(8,128)(2,1)} %get-tuple-element.8, bf16[32,36,2048]{2,1,0:T(8,128)(2,1)} %all-to-all-done), kind=kOutput, calls=%fused_computation.9 | convolution fusion | flops 906756096 | bytes 5308416 | tf_op jit(solution)/shard_map/dot_general | solution.py:8
  178.5 4.3 concatenate.60
  188.1 27.6 %collective-permute-done = bf16[2,288,1024]{2,1,0:T(8,128)(2,1)S(1)} collective-permute-done((bf16[2,288,1024]{2,1,0:T(8,128)(2,1)S(1)}, bf16[2,288,1024]{2,1,0:T(8,128)(2,1)S(1)}, u32[]{:S(2)}, u32[]{:S(2)}) %collective-permute-start) | collective-permute-done | bytes 1179680 | tf_op jit(solution)/shard_map/ppermute | solution.py:27
  217.5 28.0 %collective-permute-done.1 = bf16[2,288,1024]{2,1,0:T(8,128)(2,1)S(1)} collective-permute-done((bf16[2,288,1024]{2,1,0:T(8,128)(2,1)S(1)}, bf16[2,288,1024]{2,1,0:T(8,128)(2,1)S(1)}, u32[]{:S(2)}, u32[]{:S(2)}) %collective-permute-start.1) | collective-permute-done | bytes 1179680 | tf_op jit(solution)/shard_map/ppermute | solution.py:27
  247.4 27.1 %collective-permute-done.2 = bf16[2,288,1024]{2,1,0:T(8,128)(2,1)S(1)} collective-permute-done((bf16[2,288,1024]{2,1,0:T(8,128)(2,1)S(1)}, bf16[2,288,1024]{2,1,0:T(8,128)(2,1)S(1)}, u32[]{:S(2)}, u32[]{:S(2)}) %collective-permute-start.2) | collective-permute-done | bytes 1179680 | tf_op jit(solution)/shard_map/ppermute | solution.py:27
  280.1 9.3 %collective-permute-done.3 = bf16[288,1024]{1,0:T(8,128)(2,1)S(1)} collective-permute-done((bf16[288,1024]{1,0:T(8,128)(2,1)S(1)}, bf16[288,1024]{1,0:T(8,128)(2,1)S(1)}, u32[]{:S(2)}, u32[]{:S(2)}) %collective-permute-start.3) | collective-permute-done | bytes 589856 | tf_op jit(solution)/shard_map/ppermute | solution.py:33
  290.5 4.3 fusion.21
  294.8 3.9 fusion.23
  298.7 4.0 multiply_convert_fusion.3
  302.7 3.9 bitcast_convert_fusion
  308.6 3.9 concatenate.66
  317.4 4.9 %copy.70 = bf16[32,36,2048]{2,1,0:T(8,128)(2,1)} copy(bf16[32,36,2048]{2,0,1:T(8,128)(2,1)S(1)} %pad_maximum_fusion) | data formatting | bytes 9437184 | tf_op jit(solution)/shard_map/concatenate | solution.py:118
  322.3 12.5 %all-to-all-start.2 = ((bf16[32,36,2048]{2,1,0:T(8,128)(2,1)}), bf16[32,36,2048]{2,1,0:T(8,128)(2,1)}, u32[]{:S(2)}, u32[]{:S(2)}) async-start(bf16[32,36,2048]{2,1,0:T(8,128)(2,1)} %copy.70), calls=%async_computation.2 | async-start | bytes 10485760 | tf_op jit(solution)/shard_map/all_to_all | solution.py:117
  334.8 3.7 bitcast_convert_fusion.2
  340.4 5.0 %bitcast_convert_fusion.1 = bf16[2048,384]{1,0:T(8,128)(2,1)} fusion(bf16[32,18,384]{2,1,0:T(8,128)(2,1)} %copy-done.16, bf16[32,36,2048]{2,1,0:T(8,128)(2,1)} %all-to-all-done.1), kind=kOutput, calls=%fused_computation.6 | convolution fusion | flops 906756096 | bytes 5308416 | tf_op jit(solution)/shard_map/dot_general | solution.py:8
  345.4 3.3 concatenate.65
  350.6 28.7 %collective-permute-done.4 = bf16[2,288,1024]{2,1,0:T(8,128)(2,1)S(1)} collective-permute-done((bf16[2,288,1024]{2,1,0:T(8,128)(2,1)S(1)}, bf16[2,288,1024]{2,1,0:T(8,128)(2,1)S(1)}, u32[]{:S(2)}, u32[]{:S(2)}) %collective-permute-start.4) | collective-permute-done | bytes 1179680 | tf_op jit(solution)/shard_map/ppermute | solution.py:27
  379.9 28.0 %collective-permute-done.5 = bf16[2,288,1024]{2,1,0:T(8,128)(2,1)S(1)} collective-permute-done((bf16[2,288,1024]{2,1,0:T(8,128)(2,1)S(1)}, bf16[2,288,1024]{2,1,0:T(8,128)(2,1)S(1)}, u32[]{:S(2)}, u32[]{:S(2)}) %collective-permute-start.5) | collective-permute-done | bytes 1179680 | tf_op jit(solution)/shard_map/ppermute | solution.py:27
  408.4 27.2 %collective-permute-done.6 = bf16[2,288,1024]{2,1,0:T(8,128)(2,1)S(1)} collective-permute-done((bf16[2,288,1024]{2,1,0:T(8,128)(2,1)S(1)}, bf16[2,288,1024]{2,1,0:T(8,128)(2,1)S(1)}, u32[]{:S(2)}, u32[]{:S(2)}) %collective-permute-start.6) | collective-permute-done | bytes 1179680 | tf_op jit(solution)/shard_map/ppermute | solution.py:27
  438.8 15.1 %collective-permute-done.7 = bf16[288,1024]{1,0:T(8,128)(2,1)} collective-permute-done((bf16[288,1024]{1,0:T(8,128)(2,1)}, bf16[288,1024]{1,0:T(8,128)(2,1)}, u32[]{:S(2)}, u32[]{:S(2)}) %collective-permute-start.7) | collective-permute-done | bytes 589856 | tf_op jit(solution)/shard_map/ppermute | solution.py:33
  457.6 4.3 fusion.6
  (113 shorter events, 38.2 us)
Async XLA Ops:
  0.6 2.5 copy-start.21
  0.6 2.5 copy-start.22
  1.5 5.5 %copy-start.17 = (pred[128,64]{0,1:T(8,128)(4,1)}, pred[128,64]{0,1:T(8,128)(4,1)S(1)}, u32[]{:S(2)}) copy-start(pred[128,64]{0,1:T(8,128)(4,1)S(1)} %fusion.79) | copy-start | bytes 24580
  1.6 5.4 %copy-start.10 = (s32[64,128]{1,0:T(8,128)}, s32[64,128]{1,0:T(8,128)S(1)}, u32[]{:S(2)}) copy-start(s32[64,128]{1,0:T(8,128)S(1)} %convolution_convert_fusion) | copy-start | bytes 98308
  7.0 131.2 %all-to-all-start = ((bf16[32,36,2048]{2,1,0:T(8,128)(2,1)}), bf16[32,36,2048]{2,1,0:T(8,128)(2,1)}, u32[]{:S(2)}, u32[]{:S(2)}) async-start(bf16[32,36,2048]{2,1,0:T(8,128)(2,1)} %multiply_convert_fusion.1), calls=%async_computation | async-start | bytes 10485760 | tf_op jit(solution)/shard_map/all_to_all | solution.py:104
  23.7 123.0 %copy-start.3 = (bf16[2,2048,384]{2,1,0:T(8,128)(2,1)S(1)}, bf16[2,2048,384]{2,1,0:T(8,128)(2,1)}, u32[]{:S(2)}) copy-start(bf16[2,2048,384]{2,1,0:T(8,128)(2,1)} %param.11) | copy-start | bytes 9437188
  138.1 152.3 %all-to-all-start.1 = ((bf16[32,36,2048]{2,1,0:T(8,128)(2,1)}), bf16[32,36,2048]{2,1,0:T(8,128)(2,1)}, u32[]{:S(2)}, u32[]{:S(2)}) async-start(bf16[32,36,2048]{2,1,0:T(8,128)(2,1)} %multiply_convert_fusion), calls=%async_computation.1 | async-start | bytes 10485760 | tf_op jit(solution)/shard_map/all_to_all | solution.py:104
  146.7 3.9 copy-start.5
  154.3 3.6 copy-start.19
  184.4 2.2 copy-start
  186.7 28.9 %collective-permute-start = (bf16[2,288,1024]{2,1,0:T(8,128)(2,1)S(1)}, bf16[2,288,1024]{2,1,0:T(8,128)(2,1)S(1)}, u32[]{:S(2)}, u32[]{:S(2)}) collective-permute-start(bf16[2,288,1024]{2,1,0:T(8,128)(2,1)S(1)} %dynamic-slice_bitcast_fusion.1), channel_id=1, source_target_pairs={{0,64},{32,96},{64,128},{96,160},{128,192},{160,224},{192,0},{224,... | collective-permute-start | bytes 3538952 | tf_op jit(solution)/shard_map/ppermute | solution.py:27
  217.4 28.1 %collective-permute-start.1 = (bf16[2,288,1024]{2,1,0:T(8,128)(2,1)S(1)}, bf16[2,288,1024]{2,1,0:T(8,128)(2,1)S(1)}, u32[]{:S(2)}, u32[]{:S(2)}) collective-permute-start(bf16[2,288,1024]{2,1,0:T(8,128)(2,1)S(1)} %fusion.12), channel_id=1, source_target_pairs={{0,64},{32,96},{64,128},{96,160},{128,192},{160,224},{192,0},{224,... | collective-permute-start | bytes 3538952 | tf_op jit(solution)/shard_map/ppermute | solution.py:27
  247.2 27.3 %collective-permute-start.2 = (bf16[2,288,1024]{2,1,0:T(8,128)(2,1)S(1)}, bf16[2,288,1024]{2,1,0:T(8,128)(2,1)S(1)}, u32[]{:S(2)}, u32[]{:S(2)}) collective-permute-start(bf16[2,288,1024]{2,1,0:T(8,128)(2,1)S(1)} %fusion.11), channel_id=1, source_target_pairs={{0,64},{32,96},{64,128},{96,160},{128,192},{160,224},{192,0},{224,... | collective-permute-start | bytes 3538952 | tf_op jit(solution)/shard_map/ppermute | solution.py:27
  247.4 29.9 %copy-start.4 = (bf16[2,2048,384]{2,1,0:T(8,128)(2,1)S(1)}, bf16[2,2048,384]{2,1,0:T(8,128)(2,1)}, u32[]{:S(2)}) copy-start(bf16[2,2048,384]{2,1,0:T(8,128)(2,1)} %param.11) | copy-start | bytes 9437188
  247.4 29.9 %copy-start.12 = (bf16[32,18,384]{2,1,0:T(8,128)(2,1)S(1)}, bf16[32,18,384]{2,1,0:T(8,128)(2,1)}, u32[]{:S(2)}) copy-start(bf16[32,18,384]{2,1,0:T(8,128)(2,1)} %get-tuple-element.9) | copy-start | bytes 1327108
  276.3 2.4 copy-start.6
  276.3 2.4 copy-start.15
  276.3 13.1 %collective-permute-start.3 = (bf16[288,1024]{1,0:T(8,128)(2,1)S(1)}, bf16[288,1024]{1,0:T(8,128)(2,1)S(1)}, u32[]{:S(2)}, u32[]{:S(2)}) collective-permute-start(bf16[288,1024]{1,0:T(8,128)(2,1)S(1)} %dynamic-slice_bitcast_fusion.3), channel_id=1, source_target_pairs={{0,32},{32,0},{64,96},{96,64},{128,160},{160,128},{192,224},{224,1... | collective-permute-start | bytes 1769480 | tf_op jit(solution)/shard_map/ppermute | solution.py:33
  290.5 4.3 copy-start.7
  294.8 3.9 copy-start.20
  302.7 9.8 %copy-start.13 = (bf16[32,18,384]{2,1,0:T(8,128)(2,1)}, bf16[32,18,384]{2,1,0:T(8,128)(2,1)S(1)}, u32[]{:S(2)}) copy-start(bf16[32,18,384]{2,1,0:T(8,128)(2,1)S(1)} %get-tuple-element.7) | copy-start | bytes 1327108
  302.7 12.8 %copy-start.16 = (bf16[32,18,384]{2,1,0:T(8,128)(2,1)}, bf16[32,18,384]{2,1,0:T(8,128)(2,1)S(1)}, u32[]{:S(2)}) copy-start(bf16[32,18,384]{2,1,0:T(8,128)(2,1)S(1)} %get-tuple-element.6) | copy-start | bytes 1327108
  312.5 3.0 copy-start.8
  322.3 12.5 %copy-start.14 = (bf16[32,18,384]{2,1,0:T(8,128)(2,1)S(1)}, bf16[32,18,384]{2,1,0:T(8,128)(2,1)}, u32[]{:S(2)}) copy-start(bf16[32,18,384]{2,1,0:T(8,128)(2,1)} %copy-done.13) | copy-start | bytes 1327108
  322.3 135.3 %all-to-all-start.2 = ((bf16[32,36,2048]{2,1,0:T(8,128)(2,1)}), bf16[32,36,2048]{2,1,0:T(8,128)(2,1)}, u32[]{:S(2)}, u32[]{:S(2)}) async-start(bf16[32,36,2048]{2,1,0:T(8,128)(2,1)} %copy.70), calls=%async_computation.2 | async-start | bytes 10485760 | tf_op jit(solution)/shard_map/all_to_all | solution.py:117
  348.9 1.4 copy-start.1
  350.5 28.8 %collective-permute-start.4 = (bf16[2,288,1024]{2,1,0:T(8,128)(2,1)S(1)}, bf16[2,288,1024]{2,1,0:T(8,128)(2,1)S(1)}, u32[]{:S(2)}, u32[]{:S(2)}) collective-permute-start(bf16[2,288,1024]{2,1,0:T(8,128)(2,1)S(1)} %dynamic-slice_bitcast_fusion), channel_id=1, source_target_pairs={{0,64},{32,96},{64,128},{96,160},{128,192},{160,224},{192,0},{224,... | collective-permute-start | bytes 3538952 | tf_op jit(solution)/shard_map/ppermute | solution.py:27
  379.8 28.1 %collective-permute-start.5 = (bf16[2,288,1024]{2,1,0:T(8,128)(2,1)S(1)}, bf16[2,288,1024]{2,1,0:T(8,128)(2,1)S(1)}, u32[]{:S(2)}, u32[]{:S(2)}) collective-permute-start(bf16[2,288,1024]{2,1,0:T(8,128)(2,1)S(1)} %fusion.9), channel_id=1, source_target_pairs={{0,64},{32,96},{64,128},{96,160},{128,192},{160,224},{192,0},{224,... | collective-permute-start | bytes 3538952 | tf_op jit(solution)/shard_map/ppermute | solution.py:27
  408.3 29.2 %copy-start.18 = (pred[128,64]{0,1:T(8,128)(4,1)S(1)}, pred[128,64]{0,1:T(8,128)(4,1)}, u32[]{:S(2)}) copy-start(pred[128,64]{0,1:T(8,128)(4,1)} %copy-done.17) | copy-start | bytes 24580
  408.4 27.3 %collective-permute-start.6 = (bf16[2,288,1024]{2,1,0:T(8,128)(2,1)S(1)}, bf16[2,288,1024]{2,1,0:T(8,128)(2,1)S(1)}, u32[]{:S(2)}, u32[]{:S(2)}) collective-permute-start(bf16[2,288,1024]{2,1,0:T(8,128)(2,1)S(1)} %fusion.8), channel_id=1, source_target_pairs={{0,64},{32,96},{64,128},{96,160},{128,192},{160,224},{192,0},{224,... | collective-permute-start | bytes 3538952 | tf_op jit(solution)/shard_map/ppermute | solution.py:27
  436.1 1.6 copy-start.11
  437.0 16.8 %collective-permute-start.7 = (bf16[288,1024]{1,0:T(8,128)(2,1)}, bf16[288,1024]{1,0:T(8,128)(2,1)}, u32[]{:S(2)}, u32[]{:S(2)}) collective-permute-start(bf16[288,1024]{1,0:T(8,128)(2,1)} %dynamic-slice_bitcast_fusion.2), channel_id=1, source_target_pairs={{0,32},{32,0},{64,96},{96,64},{128,160},{160,128},{192,224},{224,1... | collective-permute-start | bytes 1769480 | tf_op jit(solution)/shard_map/ppermute | solution.py:33
  (2 other events, 2.5 us)
